TPU v7x, 32 devices: a whole 2x2x4 slice. The times are simulated.
32 devices in a mesh: seq: 8 (over y, x, core), chan: 4 (over z).
Axes of the slice: x: 2, y: 2, z: 4, core: 2. Of those that a mesh axis runs over, the one named last changes fastest.
Arguments:
- signal: bfloat16 [512, 8192], P(None, ('seq', 'chan')), may hold values from -6 to 6
- inner_gate: bfloat16 [512, 8192], P(None, ('seq', 'chan')), may hold values from -6 to 6
- outer_gate: bfloat16 [512, 8192], P(None, ('seq', 'chan')), may hold values from -6 to 6
- decay_rate: float32 [512, 16], replicated, may hold values from 3.0517578e-05 to 0.04
- residue: float32 [512, 16], replicated, may hold values from -0.1 to 0.1
- skip_gain: float32 [512], replicated, may hold values from -0.15 to 0.15
Outputs:
- layer_out: bfloat16 [512, 8192], P(None, ('seq', 'chan'))
- modal_state: float32 [512, 16], replicated
All inputs are finite; a program needn't handle non-finite values.
Results may differ from a plain program's by a relative error of at most 0.006.
Values may be sent and summed in bfloat16 or wider, within the bound.
No kernel may reach another device: no remote copies, remote signals or barrier semaphores. Data moves between devices by JAX's collectives and lax.ppermute only.
A program may use at most 64 MiB of HBM per device.

v0:
```python
import jax
import jax.numpy as jnp
from jax import lax
from jax.sharding import PartitionSpec as P


def prefix_matrix(length):
    rows = lax.iota(jnp.int32, length)
    return (rows[:, None] <= rows[None, :]).astype(jnp.bfloat16)


def prefix_sum(values, tri):
    upper = values.astype(jnp.bfloat16)
    lower = (values - upper.astype(jnp.float32)).astype(jnp.bfloat16)
    first = jnp.einsum("mcs,st->mct", upper, tri, preferred_element_type=jnp.float32)
    second = jnp.einsum("mcs,st->mct", lower, tri, preferred_element_type=jnp.float32)
    return first + second


def on_device(signal, inner_gate, outer_gate, decay_rate, residue, skip_gain):
    channels, tok_block = signal.shape
    seq_count = lax.axis_size("seq")
    chan_count = lax.axis_size("chan")
    blocks = seq_count * chan_count
    owner_idx = lax.axis_index("seq") * chan_count + lax.axis_index("chan")
    gated_in = (inner_gate.astype(jnp.float32) * signal.astype(jnp.float32)).astype(jnp.bfloat16)
    driven = lax.optimization_barrier(gated_in).astype(jnp.float32)
    rate_t = decay_rate.T
    residue_t = residue.T
    offsets = jnp.arange(tok_block, dtype=jnp.float32)
    rising = jnp.exp(rate_t[:, :, None] * offsets[None, None, :])
    falling = jnp.exp(-rate_t[:, :, None] * offsets[None, None, :])
    running = prefix_sum(rising * driven[None, :, :], prefix_matrix(tok_block))
    block_state = running[:, :, tok_block - 1] * falling[:, :, tok_block - 1]
    gathered = lax.all_gather(block_state, ("seq", "chan"), axis=0, tiled=False)
    source = jnp.arange(blocks, dtype=jnp.int32)
    lag = jnp.maximum(owner_idx - 1 - source, 0).astype(jnp.float32)
    carry_w = jnp.exp(-rate_t[None] * (tok_block * lag)[:, None, None])
    carry_w = jnp.where((source < owner_idx)[:, None, None], carry_w, 0.0)
    carry_in = jnp.sum(carry_w * gathered, axis=0)
    tail_lag = (blocks - 1 - source).astype(jnp.float32)
    tail_w = jnp.exp(-rate_t[None] * (tok_block * tail_lag)[:, None, None])
    final_state = jnp.sum(tail_w * gathered, axis=0)
    modal_state = residue * final_state.T
    local_part = jnp.sum(residue_t[:, :, None] * falling * running, axis=0)
    carry_coef = residue_t * jnp.exp(-rate_t) * carry_in
    carry_part = jnp.sum(carry_coef[:, :, None] * falling, axis=0)
    convolved = local_part + carry_part
    layer_out = (outer_gate.astype(jnp.float32) * (convolved + skip_gain[:, None] * driven)).astype(
        jnp.bfloat16
    )
    return (layer_out, modal_state)


def solution(mesh):
    placed = (
        P(None, ("seq", "chan")),
        P(None, ("seq", "chan")),
        P(None, ("seq", "chan")),
        P(),
        P(),
        P(),
    )
    return jax.shard_map(
        on_device,
        mesh=mesh,
        in_specs=placed,
        out_specs=(P(None, ("seq", "chan")), P()),
        check_vma=False,
    )
```

profile of v0, /device:TPU:0, one launch (start us, length us, event | category | flops | bytes accessed | tf_op | source)
XLA Modules:
  0.0 91.0 jit_solution(482284198931856323)
XLA Ops:
  7.2 0.0 copy-start.2
  7.2 0.0 all-gather.3.cloned.1.call-start
  7.2 1.1 %copy.10 = bf16[512,256]{0,1:T(8,128)(2,1)S(1)} copy(bf16[512,256]{1,0:T(8,128)(2,1)} %param.6) | data formatting | bytes 524288 | tf_op args[0]
  8.3 1.1 %copy.9 = bf16[512,256]{0,1:T(8,128)(2,1)S(1)} copy(bf16[512,256]{1,0:T(8,128)(2,1)} %param.7) | data formatting | bytes 524288 | tf_op args[1]
  9.4 0.1 multiply_convert_fusion.1
  9.5 0.1 copy.11
  9.6 0.8 bitcast_negate_fusion
  10.4 2.4 %fusion.1 = f32[16,512,256]{1,2,0:T(8,128)S(1)} fusion(f32[512,256]{1,0:T(8,128)S(1)} %copy.11, f32[16,512]{1,0:T(8,128)} %bitcast.15), kind=kOutput, calls=%fused_computation.6 | convolution fusion | flops 1080098816 | bytes 8945664 | tf_op jit(solution)/shard_map/mcs,st->mct/dot_general | solution.py:15
  12.8 2.5 %fusion.8 = f32[16,512,256]{1,2,0:T(8,128)S(1)} fusion(f32[16,512,256]{1,2,0:T(8,128)S(1)} %fusion.1, f32[512,256]{1,0:T(8,128)S(1)} %copy.11, f32[16,512]{1,0:T(8,128)S(1)} %bitcast.16), kind=kOutput, calls=%fused_computation.12 | convolution fusion | flops 1088487424 | bytes 17334272 | tf_op jit(solution)/shard_map/mcs,st->mct/dot_general | solution.py:16
  15.3 0.0 copy-start.3
  15.3 0.0 copy-start.1
  15.3 1.1 %multiply_exponential_fusion = f32[16,512,256]{1,2,0:T(8,128)S(1)} fusion(f32[16,512]{1,0:T(8,128)S(1)} %bitcast_negate_fusion), kind=kLoop, calls=%fused_computation.5 | loop fusion | flops 2097152 | bytes 8421376 | tf_op jit(solution)/shard_map/exp | solution.py:32
  16.4 2.1 %copy-done = f32[16,512,256]{1,2,0:T(8,128)} copy-done((f32[16,512,256]{1,2,0:T(8,128)}, f32[16,512,256]{1,2,0:T(8,128)S(1)}, u32[]{:S(2)}) %copy-start) | copy-done | bytes 8388632
  18.5 0.7 slice_multiply_fusion
  19.2 0.0 all-gather.3.cloned.1.call-update
  19.2 0.1 copy.8
  19.4 56.4 %all-gather.3.cloned.1.call-done = f32[512,512,1]{1,2,0:T(1,128)} async-done(((f32[16,512,1]{1,2,0:T(1,128)}), f32[512,512,1]{1,2,0:T(1,128)}) %all-gather.3.cloned.1.call-update) | async-done | bytes 1048592 | tf_op jit(solution)/shard_map/all_gather | solution.py:35
  75.8 1.3 %copy.13 = f32[512,512,1]{1,0,2:T(8,128)S(1)} copy(f32[512,512,1]{1,2,0:T(1,128)} %all-gather.3.cloned.1.call-done) | data formatting | bytes 2097152
  77.1 0.5 multiply_reduce_fusion.2
  77.6 4.8 %multiply_reduce_fusion = (f32[512,256]{0,1:T(8,128)S(1)}, f32[512,256]{0,1:T(8,128)S(1)}) fusion(f32[16,512]{1,0:T(8,128)S(1)} %multiply_multiply_fusion, f32[16,512]{1,0:T(8,128)S(1)} %bitcast_negate_fusion, f32[16,512,256]{1,2,0:T(8,128)} %copy-done, f32[16,512]{1,0:T(8,128)S(1)} %bitcast.14), kind=kLoop, calls=%fused_computation | loop fusion | flops 12320768 | bytes 9535488 | tf_op jit(solution)/shard_map/reduce_sum | solution.py:47
  82.4 0.0 copy-done.4
  82.5 0.2 multiply_convert_fusion
  82.6 0.8 copy.12
  83.5 0.6 bitcast_multiply_fusion
  (8 shorter events, 0.0 us)
Async XLA Ops:
  7.2 5.6 %copy-start.2 = (f32[512,16]{0,1:T(8,128)S(1)}, f32[512,16]{0,1:T(8,128)}, u32[]{:S(2)}) copy-start(f32[512,16]{0,1:T(8,128)} %param.9) | copy-start | bytes 98308
  7.2 68.7 %all-gather.3.cloned.1.call-start = ((), (), s32[]{:S(2)}) async-start(), calls=%async_computation | async-start | bytes 1081344 | tf_op jit(solution)/shard_map/all_gather | solution.py:35
  15.3 3.2 %copy-start = (f32[16,512,256]{1,2,0:T(8,128)}, f32[16,512,256]{1,2,0:T(8,128)S(1)}, u32[]{:S(2)}) copy-start(f32[16,512,256]{1,2,0:T(8,128)S(1)} %fusion.8) | copy-start | bytes 25165828
  15.3 3.9 %copy-start.3 = (bf16[512,256]{1,0:T(8,128)(2,1)S(1)}, bf16[512,256]{1,0:T(8,128)(2,1)}, u32[]{:S(2)}) copy-start(bf16[512,256]{1,0:T(8,128)(2,1)} %param.8) | copy-start | bytes 786436
  15.3 62.3 %copy-start.1 = (f32[512,16]{0,1:T(8,128)S(1)}, f32[512,16]{0,1:T(8,128)}, u32[]{:S(2)}) copy-start(f32[512,16]{0,1:T(8,128)} %param.10) | copy-start | bytes 98308
  18.5 63.9 %copy-start.4 = (f32[512]{0:T(512)S(1)}, f32[512]{0:T(512)}, u32[]{:S(2)}) copy-start(f32[512]{0:T(512)} %param.11) | copy-start | bytes 6148
Sparse Core Ops, SparseCore 0:
  19.3 56.4 all-gather.2
where the time goes:
time: 91.3 us; the launch traced here: 91 us
  waiting for transfers between devices  56.4 us (62%)
  between operations  14.2 us (16%)
  other arithmetic  8.71 us (10%)
  local copies, waits for them, and re-layouts  6.7 us (7%)
  matrix products  4.88 us (5%)
    all_gather x1, waiting for transfers between devices, on_device(): gathered = lax.all_gather(block_state, ('seq', 'chan'), axis=0, tiled=False)  56.4 us
    unnamed x15, local copies, waits for them, and re-layouts  6.57 us
    reduce_sum x1, other arithmetic, on_device(): carry_part = jnp.sum(carry_coef[:, :, None] * falling, axis=0)  4.8 us
    dot_general x1, matrix products, prefix_sum(): jnp.einsum('mcs,st->mct', lower, tri, preferred_element_type=jnp.float32)  2.51 us
    dot_general x1, matrix products, prefix_sum(): jnp.einsum('mcs,st->mct', upper, tri, preferred_element_type=jnp.float32)  2.37 us
  transfers between devices with their start and end apart: 1, of which 1 were waited for; matrix products, arithmetic and copies ran while one was open for 0% of the time, Pallas kernels for 0%

commit v1 on v0

--- a/solution.py
+++ b/solution.py
@@ -31,17 +31,24 @@
     rising = jnp.exp(rate_t[:, :, None] * offsets[None, None, :])
     falling = jnp.exp(-rate_t[:, :, None] * offsets[None, None, :])
     running = prefix_sum(rising * driven[None, :, :], prefix_matrix(tok_block))
-    block_state = running[:, :, tok_block - 1] * falling[:, :, tok_block - 1]
-    gathered = lax.all_gather(block_state, ("seq", "chan"), axis=0, tiled=False)
-    source = jnp.arange(blocks, dtype=jnp.int32)
-    lag = jnp.maximum(owner_idx - 1 - source, 0).astype(jnp.float32)
-    carry_w = jnp.exp(-rate_t[None] * (tok_block * lag)[:, None, None])
-    carry_w = jnp.where((source < owner_idx)[:, None, None], carry_w, 0.0)
-    carry_in = jnp.sum(carry_w * gathered, axis=0)
-    tail_lag = (blocks - 1 - source).astype(jnp.float32)
-    tail_w = jnp.exp(-rate_t[None] * (tok_block * tail_lag)[:, None, None])
-    final_state = jnp.sum(tail_w * gathered, axis=0)
-    modal_state = residue * final_state.T
+    to_end = jnp.exp(-rate_t[:, :, None] * (tok_block - 1.0 - offsets)[None, None, :])
+    block_state = jnp.sum(to_end * driven[None, :, :], axis=2)
+    rounds = blocks.bit_length() - 1
+    assert 1 << rounds == blocks
+    span_rate = rate_t * tok_block
+    carry_in = jnp.zeros_like(block_state)
+    group_total = block_state
+    for level in range(rounds):
+        width = 1 << level
+        pairs = [(src_i, src_i ^ width) for src_i in range(blocks)]
+        other = lax.ppermute(group_total, ("seq", "chan"), pairs)
+        upper = (owner_idx & width) != 0
+        place = (owner_idx % width).astype(jnp.float32)
+        carry_in = jnp.where(upper, carry_in + jnp.exp(-span_rate * place) * other, carry_in)
+        later = jnp.where(upper, group_total, other)
+        earlier = jnp.where(upper, other, group_total)
+        group_total = later + jnp.exp(-span_rate * width) * earlier
+    modal_state = residue * group_total.T
     local_part = jnp.sum(residue_t[:, :, None] * falling * running, axis=0)
     carry_coef = residue_t * jnp.exp(-rate_t) * carry_in
     carry_part = jnp.sum(carry_coef[:, :, None] * falling, axis=0)

time: 91.3 us -> 40.2 us (0.44)
  waiting for transfers between devices: 56.4 us -> 4.98 us
  between operations: 14.2 us -> 0.77 us
  starting transfers between devices: 0.04 us -> 9.73 us
  matrix products: 4.88 us -> 13.3 us
  local copies, waits for them, and re-layouts: 6.7 us -> 0.01 us
  other arithmetic: 8.71 us -> 10.8 us
    all_gather x1 -> x0, waiting for transfers between devices: 56.4 us -> none  [on_device(): gathered = lax.all_gather(block_state, ('seq', 'chan'), axis=0, tiled=False)]
    ppermute x0 -> x5, starting transfers between devices: none -> 9.73 us  [on_device(): other = lax.ppermute(group_total, ('seq', 'chan'), pairs)]
    unnamed x15 -> x8, local copies, waits for them, and re-layouts: 6.57 us -> 0.01 us
    dot_general x1, matrix products: 2.37 us -> 7.92 us  [prefix_sum(): jnp.einsum('mcs,st->mct', upper, tri, preferred_element_type=jnp.float32)]
    ppermute x0 -> x5, waiting for transfers between devices: none -> 4.98 us  [on_device(): other = lax.ppermute(group_total, ('seq', 'chan'), pairs)]
    dot_general x1, matrix products: 2.51 us -> 5.39 us  [prefix_sum(): jnp.einsum('mcs,st->mct', lower, tri, preferred_element_type=jnp.float32)]
    add x0 -> x4, other arithmetic: none -> 2.34 us  [on_device(): group_total = later + jnp.exp(-span_rate * width) * earlier]
    reduce_sum x1, other arithmetic: 4.8 us -> 2.5 us  [on_device(): carry_part = jnp.sum(carry_coef[:, :, None] * falling, axis=0)]
  transfers between devices with their start and end apart: 1 -> 5, of which waited for: 1 -> 3; matrix products, arithmetic and copies ran while one was open for 0% -> 34% of each run, Pallas kernels for 0% -> 0%
where the time goes in v1:
time: 40.2 us; the launch traced here: 39.6 us
  matrix products  13.3 us (33%)
  other arithmetic  10.8 us (27%)
  starting transfers between devices  9.73 us (24%)
  waiting for transfers between devices  4.98 us (12%)
  between operations  0.77 us (2%)
    ppermute x5, starting transfers between devices, on_device(): other = lax.ppermute(group_total, ('seq', 'chan'), pairs)  9.73 us
    dot_general x1, matrix products, prefix_sum(): jnp.einsum('mcs,st->mct', upper, tri, preferred_element_type=jnp.float32)  7.92 us
    dot_general x1, matrix products, prefix_sum(): jnp.einsum('mcs,st->mct', lower, tri, preferred_element_type=jnp.float32)  5.39 us
    ppermute x5, waiting for transfers between devices, on_device(): other = lax.ppermute(group_total, ('seq', 'chan'), pairs)  4.98 us
    reduce_sum x1, other arithmetic, on_device(): carry_part = jnp.sum(carry_coef[:, :, None] * falling, axis=0)  2.5 us
    reduce_sum x1, other arithmetic, on_device(): block_state = jnp.sum(to_end * driven[None, :, :], axis=2)  2.45 us
    add x4, other arithmetic, on_device(): group_total = later + jnp.exp(-span_rate * width) * earlier  2.34 us
    convert_element_type x1, other arithmetic, on_device(): (inner_gate.astype(jnp.float32) * signal.astype(jnp.float32)).astype(jnp....  1.1 us
  transfers between devices with their start and end apart: 5, of which 3 were waited for; matrix products, arithmetic and copies ran while one was open for 34% of the time, Pallas kernels for 0%

profile of v1, /device:TPU:0, one launch (start us, length us, event | category | flops | bytes accessed | tf_op | source)
XLA Modules:
  0.0 39.6 jit_solution(9919268691279622656)
XLA Ops:
  0.6 1.1 %multiply_convert_fusion.1 = bf16[512,256]{1,0:T(8,128)(2,1)S(1)} fusion(bf16[512,256]{1,0:T(8,128)(2,1)} %param.6, bf16[512,256]{1,0:T(8,128)(2,1)} %param.7), kind=kLoop, calls=%fused_computation.14 | loop fusion | flops 524288 | bytes 786432 | tf_op jit(solution)/shard_map/convert_element_type | solution.py:26
  1.8 0.8 %bitcast_negate_fusion = f32[16,512]{1,0:T(8,128)S(1)} fusion(f32[512,16]{0,1:T(8,128)} %param.9), kind=kLoop, calls=%fused_computation.29 | loop fusion | flops 8192 | bytes 65536 | tf_op jit(solution)/shard_map/neg | solution.py:32
  2.5 2.5 %multiply_reduce_fusion.1 = f32[16,512]{1,0:T(8,128)S(1)} fusion(f32[256]{0:T(256)S(1)} %iota_subtract_fusion, f32[512,256]{1,0:T(8,128)S(1)} %convert_element_type.45, f32[16,512]{1,0:T(8,128)S(1)} %bitcast_negate_fusion), kind=kLoop, calls=%fused_computation.1 | loop fusion | flops 6283264 | bytes 590848 | tf_op jit(solution)/shard_map/reduce_sum | solution.py:35
  5.0 3.1 %collective-permute-start = (f32[16,512]{1,0:T(8,128)S(1)}, f32[16,512]{1,0:T(8,128)S(1)}, u32[]{:S(2)}, u32[]{:S(2)}) collective-permute-start(f32[16,512]{1,0:T(8,128)S(1)} %multiply_reduce_fusion.1), channel_id=1, source_target_pairs={{0,1},{1,0},{2,3},{3,2},{4,5},{5,4},{6,7},{7,6},{8,9},{9,8},{10,11... | collective-permute-start | bytes 98312 | tf_op jit(solution)/shard_map/ppermute | solution.py:44
  8.1 1.9 %collective-permute-done = f32[16,512]{1,0:T(8,128)S(1)} collective-permute-done((f32[16,512]{1,0:T(8,128)S(1)}, f32[16,512]{1,0:T(8,128)S(1)}, u32[]{:S(2)}, u32[]{:S(2)}) %collective-permute-start) | collective-permute-done | bytes 32800 | tf_op jit(solution)/shard_map/ppermute | solution.py:44
  10.0 0.8 %multiply_add_fusion.3 = f32[16,512]{1,0:T(8,128)S(1)} fusion(f32[16,512]{1,0:T(8,128)S(1)} %collective-permute-done, f32[16,512]{1,0:T(8,128)S(1)} %multiply_reduce_fusion.1, pred[]{:T(512)S(6)} %ne.39, f32[512,16]{0,1:T(8,128)} %param.9), kind=kLoop, calls=%fused_computation.26 | loop fusion | flops 49152 | bytes 131073 | tf_op jit(solution)/shard_map/add | solution.py:50
  10.8 3.1 %collective-permute-start.1 = (f32[16,512]{1,0:T(8,128)S(1)}, f32[16,512]{1,0:T(8,128)S(1)}, u32[]{:S(2)}, u32[]{:S(2)}) collective-permute-start(f32[16,512]{1,0:T(8,128)S(1)} %multiply_add_fusion.3), channel_id=1, source_target_pairs={{0,2},{1,3},{2,0},{3,1},{4,6},{5,7},{6,4},{7,5},{8,10},{9,11},{10,... | collective-permute-start | bytes 98312 | tf_op jit(solution)/shard_map/ppermute | solution.py:44
  13.9 1.9 %collective-permute-done.1 = f32[16,512]{1,0:T(8,128)S(1)} collective-permute-done((f32[16,512]{1,0:T(8,128)S(1)}, f32[16,512]{1,0:T(8,128)S(1)}, u32[]{:S(2)}, u32[]{:S(2)}) %collective-permute-start.1) | collective-permute-done | bytes 32800 | tf_op jit(solution)/shard_map/ppermute | solution.py:44
  15.8 0.8 %multiply_add_fusion.2 = f32[16,512]{1,0:T(8,128)S(1)} fusion(f32[16,512]{1,0:T(8,128)S(1)} %collective-permute-done.1, f32[16,512]{1,0:T(8,128)S(1)} %multiply_add_fusion.3, pred[]{:T(512)S(6)} %ne.38, f32[512,16]{0,1:T(8,128)} %param.9), kind=kLoop, calls=%fused_computation.25 | loop fusion | flops 57344 | bytes 131073 | tf_op jit(solution)/shard_map/add | solution.py:50
  16.5 0.1 collective-permute-start.2
  16.6 1.2 %collective-permute-done.2 = f32[16,512]{1,0:T(8,128)S(1)} collective-permute-done((f32[16,512]{1,0:T(8,128)S(1)}, f32[16,512]{1,0:T(8,128)S(1)}, u32[]{:S(2)}, u32[]{:S(2)}) %collective-permute-start.2) | collective-permute-done | bytes 32800 | tf_op jit(solution)/shard_map/ppermute | solution.py:44
  17.8 0.8 %multiply_add_fusion.1 = f32[16,512]{1,0:T(8,128)S(1)} fusion(f32[16,512]{1,0:T(8,128)S(1)} %collective-permute-done.2, f32[16,512]{1,0:T(8,128)S(1)} %multiply_add_fusion.2, pred[]{:T(512)S(6)} %ne.37, f32[512,16]{0,1:T(8,128)} %param.9), kind=kLoop, calls=%fused_computation.24 | loop fusion | flops 57344 | bytes 131073 | tf_op jit(solution)/shard_map/add | solution.py:50
  18.6 1.9 %collective-permute-start.3 = (f32[16,512]{1,0:T(8,128)S(1)}, f32[16,512]{1,0:T(8,128)S(1)}, u32[]{:S(2)}, u32[]{:S(2)}) collective-permute-start(f32[16,512]{1,0:T(8,128)S(1)} %multiply_add_fusion.1), channel_id=1, source_target_pairs={{0,8},{1,9},{2,10},{3,11},{4,12},{5,13},{6,14},{7,15},{8,0},{9,1},... | collective-permute-start | bytes 98312 | tf_op jit(solution)/shard_map/ppermute | solution.py:44
  20.5 5.4 %fusion.3 = f32[16,512,256]{2,1,0:T(8,128)} fusion(f32[512,256]{1,0:T(8,128)S(1)} %convert_element_type.45, f32[16,512]{1,0:T(8,128)} %bitcast.18), kind=kOutput, calls=%fused_computation.8 | convolution fusion | flops 1086390272 | bytes 8945664 | tf_op jit(solution)/shard_map/mcs,st->mct/dot_general | solution.py:16
  25.9 0.0 collective-permute-done.3
  25.9 0.0 copy-done
  25.9 1.6 %collective-permute-start.4 = (f32[16,512]{1,0:T(8,128)S(1)}, f32[16,512]{1,0:T(8,128)S(1)}, u32[]{:S(2)}, u32[]{:S(2)}) collective-permute-start(f32[16,512]{1,0:T(8,128)S(1)} %multiply_add_fusion), channel_id=1, source_target_pairs={{0,16},{1,17},{2,18},{3,19},{4,20},{5,21},{6,22},{7,23},{8,24},{9,... | collective-permute-start | bytes 98312 | tf_op jit(solution)/shard_map/ppermute | solution.py:44
  27.5 0.0 copy-done.2
  27.5 7.9 %multiply_reduce_fusion.2 = f32[512,256]{1,0:T(8,128)S(1)} fusion(f32[16,512,256]{2,1,0:T(8,128)} %fusion.3, f32[16,512]{1,0:T(8,128)S(1)} %bitcast_negate_fusion, f32[16,512]{1,0:T(8,128)S(1)} %bitcast.20, f32[512,256]{1,0:T(8,128)S(1)} %convert_element_type.45, f32[16,512]{1,0:T(8,128)S(1)} %bitcast.19), kind=kOutput, calls=%fused_computation.2 | convolution fusion | flops 1090453504 | bytes 9535488 | tf_op jit(solution)/shard_map/mcs,st->mct/dot_general | solution.py:15
  35.5 0.0 collective-permute-done.4
  35.5 0.1 fusion.13
  35.5 2.5 %multiply_reduce_fusion = f32[512,256]{1,0:T(8,128)S(1)} fusion(f32[16,512]{1,0:T(8,128)S(1)} %fusion.13, f32[16,512]{1,0:T(8,128)S(1)} %bitcast_negate_fusion), kind=kLoop, calls=%fused_computation | loop fusion | flops 6160384 | bytes 589824 | tf_op jit(solution)/shard_map/reduce_sum | solution.py:54
  38.1 0.9 %multiply_convert_fusion = bf16[512,256]{1,0:T(8,128)(2,1)} fusion(f32[512,256]{1,0:T(8,128)S(1)} %multiply_reduce_fusion.2, f32[512,256]{1,0:T(8,128)S(1)} %multiply_reduce_fusion, bf16[512,256]{1,0:T(8,128)(2,1)S(1)} %copy-done.1, f32[512]{0:T(512)S(1)} %copy-done.3, bf16[512,256]{1,0:T(8,128)(2,1)S(1)} %multiply_convert_fusion.1), kind=kLoop, calls=%fused_computation.13 | loop fusion | flops 917504 | bytes 1837056 | tf_op jit(solution)/shard_map/convert_element_type | solution.py:56
  39.0 0.6 %bitcast_multiply_fusion = f32[512,16]{0,1:T(8,128)} fusion(f32[512,16]{0,1:T(8,128)S(1)} %copy-done.2, f32[16,512]{1,0:T(8,128)S(1)} %collective-permute-done.4, f32[16,512]{1,0:T(8,128)S(1)} %multiply_add_fusion, pred[]{:T(512)S(6)} %ne.35, f32[512,16]{0,1:T(8,128)S(1)} %copy-done), kind=kLoop, calls=%fused_computation.22 | loop fusion | flops 65536 | bytes 163841 | tf_op jit(solution)/shard_map/mul | solution.py:51
  (9 shorter events, 0.1 us)
Async XLA Ops:
  5.0 5.0 %collective-permute-start = (f32[16,512]{1,0:T(8,128)S(1)}, f32[16,512]{1,0:T(8,128)S(1)}, u32[]{:S(2)}, u32[]{:S(2)}) collective-permute-start(f32[16,512]{1,0:T(8,128)S(1)} %multiply_reduce_fusion.1), channel_id=1, source_target_pairs={{0,1},{1,0},{2,3},{3,2},{4,5},{5,4},{6,7},{7,6},{8,9},{9,8},{10,11... | collective-permute-start | bytes 98312 | tf_op jit(solution)/shard_map/ppermute | solution.py:44
  10.8 5.0 %collective-permute-start.1 = (f32[16,512]{1,0:T(8,128)S(1)}, f32[16,512]{1,0:T(8,128)S(1)}, u32[]{:S(2)}, u32[]{:S(2)}) collective-permute-start(f32[16,512]{1,0:T(8,128)S(1)} %multiply_add_fusion.3), channel_id=1, source_target_pairs={{0,2},{1,3},{2,0},{3,1},{4,6},{5,7},{6,4},{7,5},{8,10},{9,11},{10,... | collective-permute-start | bytes 98312 | tf_op jit(solution)/shard_map/ppermute | solution.py:44
  16.5 1.3 %collective-permute-start.2 = (f32[16,512]{1,0:T(8,128)S(1)}, f32[16,512]{1,0:T(8,128)S(1)}, u32[]{:S(2)}, u32[]{:S(2)}) collective-permute-start(f32[16,512]{1,0:T(8,128)S(1)} %multiply_add_fusion.2), channel_id=1, source_target_pairs={{0,4},{1,5},{2,6},{3,7},{4,0},{5,1},{6,2},{7,3},{8,12},{9,13},{10,... | collective-permute-start | bytes 98312 | tf_op jit(solution)/shard_map/ppermute | solution.py:44
  18.6 7.3 %collective-permute-start.3 = (f32[16,512]{1,0:T(8,128)S(1)}, f32[16,512]{1,0:T(8,128)S(1)}, u32[]{:S(2)}, u32[]{:S(2)}) collective-permute-start(f32[16,512]{1,0:T(8,128)S(1)} %multiply_add_fusion.1), channel_id=1, source_target_pairs={{0,8},{1,9},{2,10},{3,11},{4,12},{5,13},{6,14},{7,15},{8,0},{9,1},... | collective-permute-start | bytes 98312 | tf_op jit(solution)/shard_map/ppermute | solution.py:44
  20.5 5.4 %copy-start = (f32[512,16]{0,1:T(8,128)S(1)}, f32[512,16]{0,1:T(8,128)}, u32[]{:S(2)}) copy-start(f32[512,16]{0,1:T(8,128)} %param.9) | copy-start | bytes 98308
  20.5 7.0 %copy-start.2 = (f32[512,16]{0,1:T(8,128)S(1)}, f32[512,16]{0,1:T(8,128)}, u32[]{:S(2)}) copy-start(f32[512,16]{0,1:T(8,128)} %param.10) | copy-start | bytes 98308
  25.9 9.6 %collective-permute-start.4 = (f32[16,512]{1,0:T(8,128)S(1)}, f32[16,512]{1,0:T(8,128)S(1)}, u32[]{:S(2)}, u32[]{:S(2)}) collective-permute-start(f32[16,512]{1,0:T(8,128)S(1)} %multiply_add_fusion), channel_id=1, source_target_pairs={{0,16},{1,17},{2,18},{3,19},{4,20},{5,21},{6,22},{7,23},{8,24},{9,... | collective-permute-start | bytes 98312 | tf_op jit(solution)/shard_map/ppermute | solution.py:44
  27.5 10.5 %copy-start.1 = (bf16[512,256]{1,0:T(8,128)(2,1)S(1)}, bf16[512,256]{1,0:T(8,128)(2,1)}, u32[]{:S(2)}) copy-start(bf16[512,256]{1,0:T(8,128)(2,1)} %param.8) | copy-start | bytes 786436
  27.5 10.6 %copy-start.3 = (f32[512]{0:T(512)S(1)}, f32[512]{0:T(512)}, u32[]{:S(2)}) copy-start(f32[512]{0:T(512)} %param.11) | copy-start | bytes 6148

commit v2 on v1

--- a/solution.py
+++ b/solution.py
@@ -17,6 +17,16 @@
     return first + second
 
 
+def local_chunk(driven, rate_t, residue_t, skip_gain):
+    tok_block = driven.shape[1]
+    offsets = jnp.arange(tok_block, dtype=jnp.float32)
+    rising = jnp.exp(rate_t[:, :, None] * offsets[None, None, :])
+    falling = jnp.exp(-rate_t[:, :, None] * offsets[None, None, :])
+    running = prefix_sum(rising * driven[None, :, :], prefix_matrix(tok_block))
+    local_part = jnp.sum(residue_t[:, :, None] * falling * running, axis=0)
+    return local_part + skip_gain[:, None] * driven
+
+
 def on_device(signal, inner_gate, outer_gate, decay_rate, residue, skip_gain):
     channels, tok_block = signal.shape
     seq_count = lax.axis_size("seq")
@@ -28,34 +38,42 @@
     rate_t = decay_rate.T
     residue_t = residue.T
     offsets = jnp.arange(tok_block, dtype=jnp.float32)
-    rising = jnp.exp(rate_t[:, :, None] * offsets[None, None, :])
-    falling = jnp.exp(-rate_t[:, :, None] * offsets[None, None, :])
-    running = prefix_sum(rising * driven[None, :, :], prefix_matrix(tok_block))
     to_end = jnp.exp(-rate_t[:, :, None] * (tok_block - 1.0 - offsets)[None, None, :])
     block_state = jnp.sum(to_end * driven[None, :, :], axis=2)
     rounds = blocks.bit_length() - 1
     assert 1 << rounds == blocks
+    pieces = min(rounds, 4)
+    piece = channels // pieces
     span_rate = rate_t * tok_block
     carry_in = jnp.zeros_like(block_state)
     group_total = block_state
+    direct = []
     for level in range(rounds):
         width = 1 << level
+        if level < pieces:
+            lo = level * piece
+            group_total, chunk_in = lax.optimization_barrier((group_total, driven[lo:lo + piece]))
         pairs = [(src_i, src_i ^ width) for src_i in range(blocks)]
         other = lax.ppermute(group_total, ("seq", "chan"), pairs)
+        if level < pieces:
+            chunk_out = local_chunk(
+                chunk_in, rate_t[:, lo:lo + piece], residue_t[:, lo:lo + piece], skip_gain[lo:lo + piece]
+            )
         upper = (owner_idx & width) != 0
         place = (owner_idx % width).astype(jnp.float32)
         carry_in = jnp.where(upper, carry_in + jnp.exp(-span_rate * place) * other, carry_in)
         later = jnp.where(upper, group_total, other)
         earlier = jnp.where(upper, other, group_total)
         group_total = later + jnp.exp(-span_rate * width) * earlier
+        if level < pieces:
+            group_total, carry_in, chunk_out = lax.optimization_barrier((group_total, carry_in, chunk_out))
+            direct.append(chunk_out)
     modal_state = residue * group_total.T
-    local_part = jnp.sum(residue_t[:, :, None] * falling * running, axis=0)
+    falling = jnp.exp(-rate_t[:, :, None] * offsets[None, None, :])
     carry_coef = residue_t * jnp.exp(-rate_t) * carry_in
     carry_part = jnp.sum(carry_coef[:, :, None] * falling, axis=0)
-    convolved = local_part + carry_part
-    layer_out = (outer_gate.astype(jnp.float32) * (convolved + skip_gain[:, None] * driven)).astype(
-        jnp.bfloat16
-    )
+    convolved = jnp.concatenate(direct, axis=0) + carry_part
+    layer_out = (outer_gate.astype(jnp.float32) * convolved).astype(jnp.bfloat16)
     return (layer_out, modal_state)
 
 

time: 40.2 us -> 28.5 us (0.71); the launches traced: 39.6 us -> 28.3 us
  matrix products: 13.3 us -> 6.76 us
  other arithmetic: 10.8 us -> 8.01 us
  waiting for transfers between devices: 4.98 us -> 2.54 us
    dot_general x1 -> x4, matrix products: 7.92 us -> 2.11 us  [prefix_sum(): jnp.einsum('mcs,st->mct', upper, tri, preferred_element_type=jnp.float32)]
    ppermute x5, waiting for transfers between devices: 4.98 us -> 2.54 us  [on_device(): other = lax.ppermute(group_total, ('seq', 'chan'), pairs)]
    add x4, other arithmetic: 2.34 us -> 0.34 us  [local_chunk(): return local_part + skip_gain[:, None] * driven]
    neg x1 -> x2, other arithmetic: 0.76 us -> 0.02 us  [the longest x1 0.01 us: local_chunk(): falling = jnp.exp(-rate_t[:, :, None] * offsets[None, None, :])]
    dot_general x1 -> x4, matrix products: 5.39 us -> 4.65 us  [prefix_sum(): jnp.einsum('mcs,st->mct', lower, tri, preferred_element_type=jnp.float32)]
  transfers between devices with their start and end apart: 5 -> 5, of which waited for: 3 -> 3; matrix products, arithmetic and copies ran while one was open for 34% -> 25% of each run, Pallas kernels for 0% -> 0%
where the time goes in v2:
time: 28.5 us; the launch traced here: 28.3 us
  starting transfers between devices  10 us (35%)
  other arithmetic  8.01 us (28%)
  matrix products  6.76 us (24%)
  waiting for transfers between devices  2.54 us (9%)
  between operations  0.91 us (3%)
    ppermute x5, starting transfers between devices, on_device(): other = lax.ppermute(group_total, ('seq', 'chan'), pairs)  10 us
    dot_general x4, matrix products, prefix_sum(): jnp.einsum('mcs,st->mct', lower, tri, preferred_element_type=jnp.float32)  4.65 us
    ppermute x5, waiting for transfers between devices, on_device(): other = lax.ppermute(group_total, ('seq', 'chan'), pairs)  2.54 us
    reduce_sum x1, other arithmetic, on_device(): carry_part = jnp.sum(carry_coef[:, :, None] * falling, axis=0)  2.5 us
    reduce_sum x1, other arithmetic, on_device(): block_state = jnp.sum(to_end * driven[None, :, :], axis=2)  2.47 us
    dot_general x4, matrix products, prefix_sum(): jnp.einsum('mcs,st->mct', upper, tri, preferred_element_type=jnp.float32)  2.11 us
    convert_element_type x1, other arithmetic, on_device(): (inner_gate.astype(jnp.float32) * signal.astype(jnp.float32)).astype(jnp....  1.1 us
    convert_element_type x1, other arithmetic, on_device(): (outer_gate.astype(jnp.float32) * convolved).astype(jnp.bfloat16)  0.79 us
  transfers between devices with their start and end apart: 5, of which 3 were waited for; matrix products, arithmetic and copies ran while one was open for 25% of the time, Pallas kernels for 0%

profile of v2, /device:TPU:0, one launch (start us, length us, event | category | flops | bytes accessed | tf_op | source)
XLA Modules:
  0.0 28.3 jit_solution(15907280880785856676)
XLA Ops:
  0.6 1.1 %multiply_convert_fusion = bf16[512,256]{1,0:T(8,128)(2,1)S(1)} fusion(bf16[512,256]{1,0:T(8,128)(2,1)} %param.6, bf16[512,256]{1,0:T(8,128)(2,1)} %param.7), kind=kLoop, calls=%fused_computation.41 | loop fusion | flops 524288 | bytes 786432 | tf_op jit(solution)/shard_map/convert_element_type | solution.py:36
  1.9 2.5 %multiply_reduce_fusion.1 = f32[16,512]{1,0:T(8,128)S(1)} fusion(f32[512,256]{1,0:T(8,128)S(1)} %convert_element_type.75, f32[256]{0:T(256)S(1)} %iota_subtract_fusion, f32[16,512]{1,0:T(8,128)S(1)} %bitcast_negate_fusion), kind=kLoop, calls=%fused_computation.1 | loop fusion | flops 6283264 | bytes 590848 | tf_op jit(solution)/shard_map/reduce_sum | solution.py:42
  4.4 3.1 %collective-permute-start = (f32[16,512]{1,0:T(8,128)S(1)}, f32[16,512]{1,0:T(8,128)S(1)}, u32[]{:S(2)}, u32[]{:S(2)}) collective-permute-start(f32[16,512]{1,0:T(8,128)S(1)} %multiply_reduce_fusion.1), channel_id=1, source_target_pairs={{0,1},{1,0},{2,3},{3,2},{4,5},{5,4},{6,7},{7,6},{8,9},{9,8},{10,11... | collective-permute-start | bytes 98312 | tf_op jit(solution)/shard_map/ppermute | solution.py:57
  7.5 0.5 %fusion.4 = f32[16,128,256]{2,1,0:T(8,128)S(1)} fusion(f32[128,256]{1,0:T(8,128)S(1)} %get-tuple-element.23, f32[16,128]{1,0:T(8,128)S(1)} %get-tuple-element.63), kind=kOutput, calls=%fused_computation.18 | convolution fusion | flops 270073856 | bytes 2236416 | tf_op jit(solution)/shard_map/mcs,st->mct/dot_general | solution.py:15
  8.0 1.2 %multiply_reduce_fusion.5 = f32[128,256]{1,0:T(8,128)S(1)} fusion(f32[16,128,256]{2,1,0:T(8,128)S(1)} %fusion.4, f32[128,256]{1,0:T(8,128)S(1)} %get-tuple-element.23, f32[16,128]{1,0:T(8,128)S(1)} %get-tuple-element.63, f32[16,128]{1,0:T(8,128)S(1)} %get-tuple-element.59, f32[16,128]{1,0:T(8,128)S(1)} %get-tuple-element.70), kind=kOutput, calls=%fused_computation.14 | convolution fusion | flops 274235392 | bytes 2383872 | tf_op jit(solution)/shard_map/mcs,st->mct/dot_general | solution.py:16
  9.2 0.1 multiply_add_fusion.3
  9.4 3.1 %collective-permute-start.1 = (f32[16,512]{1,0:T(8,128)S(1)}, f32[16,512]{1,0:T(8,128)S(1)}, u32[]{:S(2)}, u32[]{:S(2)}) collective-permute-start(f32[16,512]{1,0:T(8,128)S(1)} %get-tuple-element.26), channel_id=1, source_target_pairs={{0,2},{1,3},{2,0},{3,1},{4,6},{5,7},{6,4},{7,5},{8,10},{9,11},{10,... | collective-permute-start | bytes 98312 | tf_op jit(solution)/shard_map/ppermute | solution.py:57
  12.5 0.5 %fusion.6 = f32[16,128,256]{2,1,0:T(8,128)S(1)} fusion(f32[128,256]{1,0:T(8,128)S(1)} %get-tuple-element.28, f32[16,128]{1,0:T(8,128)S(1)} %get-tuple-element.62), kind=kOutput, calls=%fused_computation.19 | convolution fusion | flops 270073856 | bytes 2236416 | tf_op jit(solution)/shard_map/mcs,st->mct/dot_general | solution.py:15
  13.0 1.1 %multiply_reduce_fusion.4 = f32[128,256]{1,0:T(8,128)S(1)} fusion(f32[16,128,256]{2,1,0:T(8,128)S(1)} %fusion.6, f32[128,256]{1,0:T(8,128)S(1)} %get-tuple-element.28, f32[16,128]{1,0:T(8,128)S(1)} %get-tuple-element.62, f32[16,128]{1,0:T(8,128)S(1)} %get-tuple-element.60, f32[16,128]{1,0:T(8,128)S(1)} %get-tuple-element.71), kind=kOutput, calls=%fused_computation.10 | convolution fusion | flops 274235392 | bytes 2383872 | tf_op jit(solution)/shard_map/mcs,st->mct/dot_general | solution.py:16
  14.1 0.1 multiply_add_fusion.2
  14.2 0.1 collective-permute-done.1
  14.5 0.5 %fusion.8 = f32[16,128,256]{2,1,0:T(8,128)S(1)} fusion(f32[128,256]{1,0:T(8,128)S(1)} %get-tuple-element.33, f32[16,128]{1,0:T(8,128)S(1)} %get-tuple-element.65), kind=kOutput, calls=%fused_computation.20 | convolution fusion | flops 270073856 | bytes 2236416 | tf_op jit(solution)/shard_map/mcs,st->mct/dot_general | solution.py:15
  15.0 1.2 %multiply_reduce_fusion.3 = f32[128,256]{1,0:T(8,128)S(1)} fusion(f32[16,128,256]{2,1,0:T(8,128)S(1)} %fusion.8, f32[128,256]{1,0:T(8,128)S(1)} %get-tuple-element.33, f32[16,128]{1,0:T(8,128)S(1)} %get-tuple-element.65, f32[16,128]{1,0:T(8,128)S(1)} %get-tuple-element.61, f32[16,128]{1,0:T(8,128)S(1)} %get-tuple-element.72), kind=kOutput, calls=%fused_computation.6 | convolution fusion | flops 274235392 | bytes 2383872 | tf_op jit(solution)/shard_map/mcs,st->mct/dot_general | solution.py:16
  16.2 0.1 multiply_add_fusion.1
  16.3 1.9 %collective-permute-start.3 = (f32[16,512]{1,0:T(8,128)S(1)}, f32[16,512]{1,0:T(8,128)S(1)}, u32[]{:S(2)}, u32[]{:S(2)}) collective-permute-start(f32[16,512]{1,0:T(8,128)S(1)} %get-tuple-element.36), channel_id=1, source_target_pairs={{0,8},{1,9},{2,10},{3,11},{4,12},{5,13},{6,14},{7,15},{8,0},{9,1},... | collective-permute-start | bytes 98312 | tf_op jit(solution)/shard_map/ppermute | solution.py:57
  18.2 0.5 %fusion.10 = f32[16,128,256]{2,1,0:T(8,128)S(1)} fusion(f32[128,256]{1,0:T(8,128)S(1)} %get-tuple-element.38, f32[16,128]{1,0:T(8,128)S(1)} %get-tuple-element.64), kind=kOutput, calls=%fused_computation.21 | convolution fusion | flops 270073856 | bytes 2236416 | tf_op jit(solution)/shard_map/mcs,st->mct/dot_general | solution.py:15
  18.8 1.1 %multiply_reduce_fusion.2 = f32[128,256]{1,0:T(8,128)S(1)} fusion(f32[16,128,256]{2,1,0:T(8,128)S(1)} %fusion.10, f32[128,256]{1,0:T(8,128)S(1)} %get-tuple-element.38, f32[16,128]{1,0:T(8,128)S(1)} %get-tuple-element.64, f32[16,128]{1,0:T(8,128)S(1)} %get-tuple-element.58, f32[16,128]{1,0:T(8,128)S(1)} %get-tuple-element.73), kind=kOutput, calls=%fused_computation.2 | convolution fusion | flops 274235392 | bytes 2383872 | tf_op jit(solution)/shard_map/mcs,st->mct/dot_general | solution.py:16
  19.9 0.1 multiply_add_fusion
  20.0 0.3 %collective-permute-done.3 = f32[16,512]{1,0:T(8,128)S(1)} collective-permute-done((f32[16,512]{1,0:T(8,128)S(1)}, f32[16,512]{1,0:T(8,128)S(1)}, u32[]{:S(2)}, u32[]{:S(2)}) %collective-permute-start.3) | collective-permute-done | bytes 32800 | tf_op jit(solution)/shard_map/ppermute | solution.py:57
  20.4 1.9 %collective-permute-start.4 = (f32[16,512]{1,0:T(8,128)S(1)}, f32[16,512]{1,0:T(8,128)S(1)}, u32[]{:S(2)}, u32[]{:S(2)}) collective-permute-start(f32[16,512]{1,0:T(8,128)S(1)} %get-tuple-element.41), channel_id=1, source_target_pairs={{0,16},{1,17},{2,18},{3,19},{4,20},{5,21},{6,22},{7,23},{8,24},{9,... | collective-permute-start | bytes 98312 | tf_op jit(solution)/shard_map/ppermute | solution.py:57
  22.3 2.1 %collective-permute-done.4 = f32[16,512]{1,0:T(8,128)S(1)} collective-permute-done((f32[16,512]{1,0:T(8,128)S(1)}, f32[16,512]{1,0:T(8,128)S(1)}, u32[]{:S(2)}, u32[]{:S(2)}) %collective-permute-start.4) | collective-permute-done | bytes 32800 | tf_op jit(solution)/shard_map/ppermute | solution.py:57
  24.4 2.5 %multiply_reduce_fusion = f32[512,256]{1,0:T(8,128)S(1)} fusion(f32[16,512]{1,0:T(8,128)S(1)} %fusion.39, f32[16,512]{1,0:T(8,128)S(1)} %bitcast_negate_fusion), kind=kLoop, calls=%fused_computation | loop fusion | flops 6160384 | bytes 589824 | tf_op jit(solution)/shard_map/reduce_sum | solution.py:74
  26.9 0.8 %fusion.29 = bf16[512,256]{1,0:T(8,128)(2,1)} fusion(f32[512,256]{1,0:T(8,128)S(1)} %multiply_reduce_fusion, f32[128,256]{1,0:T(8,128)S(1)} %multiply_add_fusion, f32[128,256]{1,0:T(8,128)S(1)} %multiply_add_fusion.1, f32[128,256]{1,0:T(8,128)S(1)} %multiply_add_fusion.2, f32[128,256]{1,0:T(8,128)S(1)} %multiply_add_fusion.3, bf16[512,256]{1,0:T(8,128)(2,1)S(1)} %copy-done.2), kind=kLoop, calls=%fused_computation.40 | loop fusion | flops 917504 | bytes 1572864 | tf_op jit(solution)/shard_map/convert_element_type | solution.py:76
  27.7 0.6 %bitcast_multiply_fusion = f32[512,16]{0,1:T(8,128)} fusion(f32[512,16]{0,1:T(8,128)S(1)} %copy-done.1, f32[16,512]{1,0:T(8,128)S(1)} %collective-permute-done.4, f32[16,512]{1,0:T(8,128)S(1)} %get-tuple-element.41, pred[]{:T(512)S(6)} %ne.42, f32[512,16]{0,1:T(8,128)S(1)} %copy-done), kind=kLoop, calls=%fused_computation.53 | loop fusion | flops 65536 | bytes 163841 | tf_op jit(solution)/shard_map/mul | solution.py:71
  (22 shorter events, 0.3 us)
Async XLA Ops:
  0.6 1.2 %copy-start = (f32[512,16]{0,1:T(8,128)S(1)}, f32[512,16]{0,1:T(8,128)}, u32[]{:S(2)}) copy-start(f32[512,16]{0,1:T(8,128)} %param.9) | copy-start | bytes 98308
  1.8 5.6 %copy-start.3 = (f32[512]{0:T(512)S(1)}, f32[512]{0:T(512)}, u32[]{:S(2)}) copy-start(f32[512]{0:T(512)} %param.11) | copy-start | bytes 6148
  1.8 5.6 %copy-start.1 = (f32[512,16]{0,1:T(8,128)S(1)}, f32[512,16]{0,1:T(8,128)}, u32[]{:S(2)}) copy-start(f32[512,16]{0,1:T(8,128)} %param.10) | copy-start | bytes 98308
  4.4 5.0 %collective-permute-start = (f32[16,512]{1,0:T(8,128)S(1)}, f32[16,512]{1,0:T(8,128)S(1)}, u32[]{:S(2)}, u32[]{:S(2)}) collective-permute-start(f32[16,512]{1,0:T(8,128)S(1)} %multiply_reduce_fusion.1), channel_id=1, source_target_pairs={{0,1},{1,0},{2,3},{3,2},{4,5},{5,4},{6,7},{7,6},{8,9},{9,8},{10,11... | collective-permute-start | bytes 98312 | tf_op jit(solution)/shard_map/ppermute | solution.py:57
  9.4 5.0 %collective-permute-start.1 = (f32[16,512]{1,0:T(8,128)S(1)}, f32[16,512]{1,0:T(8,128)S(1)}, u32[]{:S(2)}, u32[]{:S(2)}) collective-permute-start(f32[16,512]{1,0:T(8,128)S(1)} %get-tuple-element.26), channel_id=1, source_target_pairs={{0,2},{1,3},{2,0},{3,1},{4,6},{5,7},{6,4},{7,5},{8,10},{9,11},{10,... | collective-permute-start | bytes 98312 | tf_op jit(solution)/shard_map/ppermute | solution.py:57
  14.4 1.9 %collective-permute-start.2 = (f32[16,512]{1,0:T(8,128)S(1)}, f32[16,512]{1,0:T(8,128)S(1)}, u32[]{:S(2)}, u32[]{:S(2)}) collective-permute-start(f32[16,512]{1,0:T(8,128)S(1)} %get-tuple-element.31), channel_id=1, source_target_pairs={{0,4},{1,5},{2,6},{3,7},{4,0},{5,1},{6,2},{7,3},{8,12},{9,13},{10,... | collective-permute-start | bytes 98312 | tf_op jit(solution)/shard_map/ppermute | solution.py:57
  16.3 4.0 %collective-permute-start.3 = (f32[16,512]{1,0:T(8,128)S(1)}, f32[16,512]{1,0:T(8,128)S(1)}, u32[]{:S(2)}, u32[]{:S(2)}) collective-permute-start(f32[16,512]{1,0:T(8,128)S(1)} %get-tuple-element.36), channel_id=1, source_target_pairs={{0,8},{1,9},{2,10},{3,11},{4,12},{5,13},{6,14},{7,15},{8,0},{9,1},... | collective-permute-start | bytes 98312 | tf_op jit(solution)/shard_map/ppermute | solution.py:57
  20.4 6.5 %copy-start.2 = (bf16[512,256]{1,0:T(8,128)(2,1)S(1)}, bf16[512,256]{1,0:T(8,128)(2,1)}, u32[]{:S(2)}) copy-start(bf16[512,256]{1,0:T(8,128)(2,1)} %param.8) | copy-start | bytes 786436
  20.4 4.0 %collective-permute-start.4 = (f32[16,512]{1,0:T(8,128)S(1)}, f32[16,512]{1,0:T(8,128)S(1)}, u32[]{:S(2)}, u32[]{:S(2)}) collective-permute-start(f32[16,512]{1,0:T(8,128)S(1)} %get-tuple-element.41), channel_id=1, source_target_pairs={{0,16},{1,17},{2,18},{3,19},{4,20},{5,21},{6,22},{7,23},{8,24},{9,... | collective-permute-start | bytes 98312 | tf_op jit(solution)/shard_map/ppermute | solution.py:57

commit v3 on v2

--- a/solution.py
+++ b/solution.py
@@ -27,6 +27,19 @@
     return local_part + skip_gain[:, None] * driven
 
 
+def chunk_bounds(channels, pieces):
+    return [min(channels, (channels * i // pieces + 7) // 8 * 8) for i in range(pieces + 1)]
+
+
+def level_sizes(blocks):
+    rounds = blocks.bit_length() - 1
+    assert 1 << rounds == blocks
+    sizes = [4] * (rounds // 2)
+    if rounds % 2:
+        sizes.append(2)
+    return sizes
+
+
 def on_device(signal, inner_gate, outer_gate, decay_rate, residue, skip_gain):
     channels, tok_block = signal.shape
     seq_count = lax.axis_size("seq")
@@ -40,34 +53,39 @@
     offsets = jnp.arange(tok_block, dtype=jnp.float32)
     to_end = jnp.exp(-rate_t[:, :, None] * (tok_block - 1.0 - offsets)[None, None, :])
     block_state = jnp.sum(to_end * driven[None, :, :], axis=2)
-    rounds = blocks.bit_length() - 1
-    assert 1 << rounds == blocks
-    pieces = min(rounds, 4)
-    piece = channels // pieces
+    sizes = level_sizes(blocks)
+    bounds = chunk_bounds(channels, len(sizes))
     span_rate = rate_t * tok_block
     carry_in = jnp.zeros_like(block_state)
     group_total = block_state
     direct = []
-    for level in range(rounds):
-        width = 1 << level
-        if level < pieces:
-            lo = level * piece
-            group_total, chunk_in = lax.optimization_barrier((group_total, driven[lo:lo + piece]))
-        pairs = [(src_i, src_i ^ width) for src_i in range(blocks)]
-        other = lax.ppermute(group_total, ("seq", "chan"), pairs)
-        if level < pieces:
-            chunk_out = local_chunk(
-                chunk_in, rate_t[:, lo:lo + piece], residue_t[:, lo:lo + piece], skip_gain[lo:lo + piece]
-            )
-        upper = (owner_idx & width) != 0
-        place = (owner_idx % width).astype(jnp.float32)
-        carry_in = jnp.where(upper, carry_in + jnp.exp(-span_rate * place) * other, carry_in)
-        later = jnp.where(upper, group_total, other)
-        earlier = jnp.where(upper, other, group_total)
-        group_total = later + jnp.exp(-span_rate * width) * earlier
-        if level < pieces:
-            group_total, carry_in, chunk_out = lax.optimization_barrier((group_total, carry_in, chunk_out))
-            direct.append(chunk_out)
+    width = 1
+    for level, radix in enumerate(sizes):
+        lo, hi = bounds[level], bounds[level + 1]
+        group_total, chunk_in = lax.optimization_barrier((group_total, driven[lo:hi]))
+        span = width * radix
+        received = [group_total]
+        for shift in range(1, radix):
+            pairs = [
+                (src_i, src_i - src_i % span + ((src_i // width + shift) % radix) * width + src_i % width)
+                for src_i in range(blocks)
+            ]
+            received.append(lax.ppermute(group_total, ("seq", "chan"), pairs))
+        chunk_out = local_chunk(chunk_in, rate_t[:, lo:hi], residue_t[:, lo:hi], skip_gain[lo:hi])
+        stacked = jnp.stack(received)
+        place = owner_idx // width % radix
+        inner = (owner_idx % width).astype(jnp.float32)
+        new_total = jnp.zeros_like(group_total)
+        for part in range(radix):
+            value = lax.dynamic_index_in_dim(stacked, (place - part) % radix, 0, keepdims=False)
+            gap = jnp.maximum(place - 1 - part, 0).astype(jnp.float32) * width + inner
+            weight = jnp.where(part < place, jnp.exp(-span_rate * gap), 0.0)
+            carry_in = carry_in + weight * value
+            new_total = new_total + jnp.exp(-span_rate * ((radix - 1 - part) * width)) * value
+        group_total = new_total
+        group_total, carry_in, chunk_out = lax.optimization_barrier((group_total, carry_in, chunk_out))
+        direct.append(chunk_out)
+        width = span
     modal_state = residue * group_total.T
     falling = jnp.exp(-rate_t[:, :, None] * offsets[None, None, :])
     carry_coef = residue_t * jnp.exp(-rate_t) * carry_in

time: 28.5 us -> 29.2 us (1.025)
  waiting for transfers between devices: 2.54 us -> 0.02 us
  starting transfers between devices: 10 us -> 11.6 us
  other arithmetic: 8.01 us -> 8.86 us
  matrix products: 6.76 us -> 7.13 us
    ppermute x5 -> x7, waiting for transfers between devices: 2.54 us -> 0.02 us  [on_device(): received.append(lax.ppermute(group_total, ('seq', 'chan'), pairs))]
    ppermute x5 -> x7, starting transfers between devices: 10 us -> 11.6 us  [on_device(): received.append(lax.ppermute(group_total, ('seq', 'chan'), pairs))]
    neg x1, other arithmetic: 0.01 us -> 0.76 us  [on_device(): -rate_t[:, :, None] * (tok_block - 1.0 - offsets)[None, None, :]]
    dot_general x4 -> x3, matrix products: 4.65 us -> 4.99 us  [prefix_sum(): jnp.einsum('mcs,st->mct', lower, tri, preferred_element_type=jnp.float32)]
    dot_general x4 -> x3, matrix products: 2.11 us -> 2.14 us  [prefix_sum(): jnp.einsum('mcs,st->mct', upper, tri, preferred_element_type=jnp.float32)]
  transfers between devices with their start and end apart: 5 -> 7, of which waited for: 3 -> 0; matrix products, arithmetic and copies ran while one was open for 25% -> 26% of each run, Pallas kernels for 0% -> 0%
where the time goes in v3:
time: 29.2 us; the launch traced here: 29 us
  starting transfers between devices  11.6 us (40%)
  other arithmetic  8.86 us (30%)
  matrix products  7.13 us (24%)
  between operations  1.2 us (4%)
    ppermute x7, starting transfers between devices, on_device(): received.append(lax.ppermute(group_total, ('seq', 'chan'), pairs))  11.6 us
    dot_general x3, matrix products, prefix_sum(): jnp.einsum('mcs,st->mct', lower, tri, preferred_element_type=jnp.float32)  4.99 us
    reduce_sum x1, other arithmetic, on_device(): carry_part = jnp.sum(carry_coef[:, :, None] * falling, axis=0)  2.5 us
    reduce_sum x1, other arithmetic, on_device(): block_state = jnp.sum(to_end * driven[None, :, :], axis=2)  2.45 us
    dot_general x3, matrix products, prefix_sum(): jnp.einsum('mcs,st->mct', upper, tri, preferred_element_type=jnp.float32)  2.14 us
    convert_element_type x1, other arithmetic, on_device(): (inner_gate.astype(jnp.float32) * signal.astype(jnp.float32)).astype(jnp....  1.1 us
    convert_element_type x1, other arithmetic, on_device(): (outer_gate.astype(jnp.float32) * convolved).astype(jnp.bfloat16)  0.81 us
    neg x1, other arithmetic, on_device(): -rate_t[:, :, None] * (tok_block - 1.0 - offsets)[None, None, :]  0.76 us
  transfers between devices with their start and end apart: 7, of which 0 were waited for; matrix products, arithmetic and copies ran while one was open for 26% of the time, Pallas kernels for 0%

profile of v3, /device:TPU:0, one launch (start us, length us, event | category | flops | bytes accessed | tf_op | source)
XLA Modules:
  0.0 29.0 jit_solution(10666974385676883515)
XLA Ops:
  0.6 1.1 %multiply_convert_fusion = bf16[512,256]{1,0:T(8,128)(2,1)S(1)} fusion(bf16[512,256]{1,0:T(8,128)(2,1)} %param.6, bf16[512,256]{1,0:T(8,128)(2,1)} %param.7), kind=kLoop, calls=%fused_computation.32 | loop fusion | flops 524288 | bytes 786432 | tf_op jit(solution)/shard_map/convert_element_type | solution.py:49
  1.8 0.8 %bitcast_negate_fusion = f32[16,512]{1,0:T(8,128)S(1)} fusion(f32[512,16]{0,1:T(8,128)} %param.9), kind=kLoop, calls=%fused_computation.84 | loop fusion | flops 8192 | bytes 65536 | tf_op jit(solution)/shard_map/neg | solution.py:54
  2.6 2.5 %multiply_reduce_fusion.1 = f32[16,512]{1,0:T(8,128)S(1)} fusion(f32[512,256]{1,0:T(8,128)S(1)} %convert_element_type.89, f32[256]{0:T(256)S(1)} %iota_subtract_fusion, f32[16,512]{1,0:T(8,128)S(1)} %bitcast_negate_fusion), kind=kLoop, calls=%fused_computation.1 | loop fusion | flops 6283264 | bytes 590848 | tf_op jit(solution)/shard_map/reduce_sum | solution.py:55
  5.1 3.1 %collective-permute-start = (f32[16,512]{1,0:T(8,128)S(1)}, f32[16,512]{1,0:T(8,128)S(1)}, u32[]{:S(2)}, u32[]{:S(2)}) collective-permute-start(f32[16,512]{1,0:T(8,128)S(1)} %multiply_reduce_fusion.1), channel_id=1, source_target_pairs={{0,1},{1,2},{2,3},{3,0},{4,5},{5,6},{6,7},{7,4},{8,9},{9,10},{10,1... | collective-permute-start | bytes 98312 | tf_op jit(solution)/shard_map/ppermute | solution.py:73
  8.1 2.6 %collective-permute-start.1 = (f32[16,512]{1,0:T(8,128)S(1)}, f32[16,512]{1,0:T(8,128)S(1)}, u32[]{:S(2)}, u32[]{:S(2)}) collective-permute-start(f32[16,512]{1,0:T(8,128)S(1)} %multiply_reduce_fusion.1), channel_id=1, source_target_pairs={{0,2},{1,3},{2,0},{3,1},{4,6},{5,7},{6,4},{7,5},{8,10},{9,11},{10,... | collective-permute-start | bytes 98312 | tf_op jit(solution)/shard_map/ppermute | solution.py:73
  10.7 1.3 %collective-permute-start.2 = (f32[16,512]{1,0:T(8,128)S(1)}, f32[16,512]{1,0:T(8,128)S(1)}, u32[]{:S(2)}, u32[]{:S(2)}) collective-permute-start(f32[16,512]{1,0:T(8,128)S(1)} %multiply_reduce_fusion.1), channel_id=1, source_target_pairs={{0,3},{1,0},{2,1},{3,2},{4,7},{5,4},{6,5},{7,6},{8,11},{9,8},{10,9... | collective-permute-start | bytes 98312 | tf_op jit(solution)/shard_map/ppermute | solution.py:73
  12.1 0.1 slice_negate_fusion
  12.2 0.7 %fusion.3 = f32[16,176,256]{2,1,0:T(8,128)S(1)} fusion(f32[176,256]{1,0:T(8,128)S(1)} %slice.48, f32[16,176]{1,0:T(8,128)S(1)} %get-tuple-element.47), kind=kOutput, calls=%fused_computation.14 | convolution fusion | flops 371326976 | bytes 3075072 | tf_op jit(solution)/shard_map/mcs,st->mct/dot_general | solution.py:15
  12.9 1.9 %multiply_reduce_fusion.2 = f32[176,256]{1,0:T(8,128)S(1)} fusion(f32[16,176,256]{2,1,0:T(8,128)S(1)} %fusion.3, f32[176,256]{1,0:T(8,128)S(1)} %slice.48, f32[16,176]{1,0:T(8,128)S(1)} %get-tuple-element.47, f32[16,176]{1,0:T(8,128)S(1)} %get-tuple-element.46, f32[16,176]{1,0:T(8,128)S(1)} %slice.49), kind=kOutput, calls=%fused_computation.2 | convolution fusion | flops 377049088 | bytes 3277824 | tf_op jit(solution)/shard_map/mcs,st->mct/dot_general | solution.py:16
  14.8 0.1 multiply_add_fusion
  14.9 0.1 fusion.49
  15.5 1.5 %collective-permute-start.4 = (f32[16,512]{1,0:T(8,128)S(1)}, f32[16,512]{1,0:T(8,128)S(1)}, u32[]{:S(2)}, u32[]{:S(2)}) collective-permute-start(f32[16,512]{1,0:T(8,128)S(1)} %get-tuple-element.21), channel_id=1, source_target_pairs={{0,8},{1,9},{2,10},{3,11},{4,12},{5,13},{6,14},{7,15},{8,0},{9,1},... | collective-permute-start | bytes 98312 | tf_op jit(solution)/shard_map/ppermute | solution.py:73
  17.0 1.4 %collective-permute-start.5 = (f32[16,512]{1,0:T(8,128)S(1)}, f32[16,512]{1,0:T(8,128)S(1)}, u32[]{:S(2)}, u32[]{:S(2)}) collective-permute-start(f32[16,512]{1,0:T(8,128)S(1)} %get-tuple-element.21), channel_id=1, source_target_pairs={{0,12},{1,13},{2,14},{3,15},{4,0},{5,1},{6,2},{7,3},{8,4},{9,5},{1... | collective-permute-start | bytes 98312 | tf_op jit(solution)/shard_map/ppermute | solution.py:73
  18.4 0.7 %fusion.5 = f32[16,168,256]{2,1,0:T(8,128)S(1)} fusion(f32[168,256]{1,0:T(8,128)S(1)} %get-tuple-element.23, f32[16,168]{1,0:T(8,128)S(1)} %get-tuple-element.45), kind=kOutput, calls=%fused_computation.15 | convolution fusion | flops 354451456 | bytes 2935296 | tf_op jit(solution)/shard_map/mcs,st->mct/dot_general | solution.py:15
  19.1 1.6 %multiply_reduce_fusion.4 = f32[168,256]{1,0:T(8,128)S(1)} fusion(f32[16,168,256]{2,1,0:T(8,128)S(1)} %fusion.5, f32[168,256]{1,0:T(8,128)S(1)} %get-tuple-element.23, f32[16,168]{1,0:T(8,128)S(1)} %get-tuple-element.45, f32[16,168]{1,0:T(8,128)S(1)} %get-tuple-element.43, f32[16,168]{1,0:T(8,128)S(1)} %get-tuple-element.50), kind=kOutput, calls=%fused_computation.10 | convolution fusion | flops 359913472 | bytes 3128832 | tf_op jit(solution)/shard_map/mcs,st->mct/dot_general | solution.py:16
  20.7 0.1 multiply_add_fusion.2
  20.8 0.1 fusion.35
  20.9 1.6 %collective-permute-start.6 = (f32[16,512]{1,0:T(8,128)S(1)}, f32[16,512]{1,0:T(8,128)S(1)}, u32[]{:S(2)}, u32[]{:S(2)}) collective-permute-start(f32[16,512]{1,0:T(8,128)S(1)} %get-tuple-element.26), channel_id=1, source_target_pairs={{0,16},{1,17},{2,18},{3,19},{4,20},{5,21},{6,22},{7,23},{8,24},{9,... | collective-permute-start | bytes 98312 | tf_op jit(solution)/shard_map/ppermute | solution.py:73
  22.5 0.7 %fusion.7 = f32[16,168,256]{2,1,0:T(8,128)S(1)} fusion(f32[168,256]{1,0:T(8,128)S(1)} %get-tuple-element.28, f32[16,168]{1,0:T(8,128)S(1)} %get-tuple-element.44), kind=kOutput, calls=%fused_computation.16 | convolution fusion | flops 354451456 | bytes 2935296 | tf_op jit(solution)/shard_map/mcs,st->mct/dot_general | solution.py:15
  23.3 1.5 %multiply_reduce_fusion.3 = f32[168,256]{1,0:T(8,128)S(1)} fusion(f32[16,168,256]{2,1,0:T(8,128)S(1)} %fusion.7, f32[168,256]{1,0:T(8,128)S(1)} %get-tuple-element.28, f32[16,168]{1,0:T(8,128)S(1)} %get-tuple-element.44, f32[16,168]{1,0:T(8,128)S(1)} %get-tuple-element.42, f32[16,168]{1,0:T(8,128)S(1)} %get-tuple-element.51), kind=kOutput, calls=%fused_computation.6 | convolution fusion | flops 359913472 | bytes 3128832 | tf_op jit(solution)/shard_map/mcs,st->mct/dot_general | solution.py:16
  24.8 0.1 multiply_add_fusion.1
  25.0 2.5 %multiply_reduce_fusion = f32[512,256]{1,0:T(8,128)S(1)} fusion(f32[16,512]{1,0:T(8,128)S(1)} %multiply_multiply_fusion, f32[16,512]{1,0:T(8,128)S(1)} %bitcast_negate_fusion), kind=kLoop, calls=%fused_computation | loop fusion | flops 6160384 | bytes 589824 | tf_op jit(solution)/shard_map/reduce_sum | solution.py:92
  27.5 0.6 %bitcast_multiply_fusion = f32[512,16]{0,1:T(8,128)} fusion(f32[512,16]{0,1:T(8,128)S(1)} %copy-done.1, f32[16,512]{1,0:T(8,128)S(1)} %get-tuple-element.31), kind=kLoop, calls=%fused_computation.48 | loop fusion | flops 8192 | bytes 98304 | tf_op jit(solution)/shard_map/mul | solution.py:89
  28.1 0.8 %fusion.22 = bf16[512,256]{1,0:T(8,128)(2,1)} fusion(f32[512,256]{1,0:T(8,128)S(1)} %multiply_reduce_fusion, f32[168,256]{1,0:T(8,128)S(1)} %multiply_add_fusion.1, f32[168,256]{1,0:T(8,128)S(1)} %multiply_add_fusion.2, f32[176,256]{1,0:T(8,128)S(1)} %multiply_add_fusion, bf16[512,256]{1,0:T(8,128)(2,1)S(1)} %copy-done.2), kind=kLoop, calls=%fused_computation.31 | loop fusion | flops 786432 | bytes 1572864 | tf_op jit(solution)/shard_map/convert_element_type | solution.py:94
  (29 shorter events, 0.3 us)
Async XLA Ops:
  1.7 10.4 %copy-start = (f32[512,16]{0,1:T(8,128)S(1)}, f32[512,16]{0,1:T(8,128)}, u32[]{:S(2)}) copy-start(f32[512,16]{0,1:T(8,128)} %param.9) | copy-start | bytes 98308
  1.8 10.3 %copy-start.1 = (f32[512,16]{0,1:T(8,128)S(1)}, f32[512,16]{0,1:T(8,128)}, u32[]{:S(2)}) copy-start(f32[512,16]{0,1:T(8,128)} %param.10) | copy-start | bytes 98308
  5.1 10.2 %collective-permute-start = (f32[16,512]{1,0:T(8,128)S(1)}, f32[16,512]{1,0:T(8,128)S(1)}, u32[]{:S(2)}, u32[]{:S(2)}) collective-permute-start(f32[16,512]{1,0:T(8,128)S(1)} %multiply_reduce_fusion.1), channel_id=1, source_target_pairs={{0,1},{1,2},{2,3},{3,0},{4,5},{5,6},{6,7},{7,4},{8,9},{9,10},{10,1... | collective-permute-start | bytes 98312 | tf_op jit(solution)/shard_map/ppermute | solution.py:73
  8.1 7.2 %collective-permute-start.1 = (f32[16,512]{1,0:T(8,128)S(1)}, f32[16,512]{1,0:T(8,128)S(1)}, u32[]{:S(2)}, u32[]{:S(2)}) collective-permute-start(f32[16,512]{1,0:T(8,128)S(1)} %multiply_reduce_fusion.1), channel_id=1, source_target_pairs={{0,2},{1,3},{2,0},{3,1},{4,6},{5,7},{6,4},{7,5},{8,10},{9,11},{10,... | collective-permute-start | bytes 98312 | tf_op jit(solution)/shard_map/ppermute | solution.py:73
  10.7 4.6 %collective-permute-start.2 = (f32[16,512]{1,0:T(8,128)S(1)}, f32[16,512]{1,0:T(8,128)S(1)}, u32[]{:S(2)}, u32[]{:S(2)}) collective-permute-start(f32[16,512]{1,0:T(8,128)S(1)} %multiply_reduce_fusion.1), channel_id=1, source_target_pairs={{0,3},{1,0},{2,1},{3,2},{4,7},{5,4},{6,5},{7,6},{8,11},{9,8},{10,9... | collective-permute-start | bytes 98312 | tf_op jit(solution)/shard_map/ppermute | solution.py:73
  12.9 1.9 %slice-start = ((f32[512]{0:T(512)}), f32[176]{0:T(256)S(1)}, s32[]{:S(2)}) async-start(f32[512]{0:T(512)} %param.11), calls=%async_computation | async-start | bytes 2048 | tf_op jit(solution)/shard_map/slice | solution.py:74
  12.9 2.0 %copy-start.3 = (f32[512]{0:T(512)S(1)}, f32[512]{0:T(512)}, u32[]{:S(2)}) copy-start(f32[512]{0:T(512)} %param.11) | copy-start | bytes 6148
  15.4 5.4 %collective-permute-start.3 = (f32[16,512]{1,0:T(8,128)S(1)}, f32[16,512]{1,0:T(8,128)S(1)}, u32[]{:S(2)}, u32[]{:S(2)}) collective-permute-start(f32[16,512]{1,0:T(8,128)S(1)} %get-tuple-element.21), channel_id=1, source_target_pairs={{0,4},{1,5},{2,6},{3,7},{4,8},{5,9},{6,10},{7,11},{8,12},{9,13},{1... | collective-permute-start | bytes 98312 | tf_op jit(solution)/shard_map/ppermute | solution.py:73
  15.5 5.3 %collective-permute-start.4 = (f32[16,512]{1,0:T(8,128)S(1)}, f32[16,512]{1,0:T(8,128)S(1)}, u32[]{:S(2)}, u32[]{:S(2)}) collective-permute-start(f32[16,512]{1,0:T(8,128)S(1)} %get-tuple-element.21), channel_id=1, source_target_pairs={{0,8},{1,9},{2,10},{3,11},{4,12},{5,13},{6,14},{7,15},{8,0},{9,1},... | collective-permute-start | bytes 98312 | tf_op jit(solution)/shard_map/ppermute | solution.py:73
  17.0 3.8 %collective-permute-start.5 = (f32[16,512]{1,0:T(8,128)S(1)}, f32[16,512]{1,0:T(8,128)S(1)}, u32[]{:S(2)}, u32[]{:S(2)}) collective-permute-start(f32[16,512]{1,0:T(8,128)S(1)} %get-tuple-element.21), channel_id=1, source_target_pairs={{0,12},{1,13},{2,14},{3,15},{4,0},{5,1},{6,2},{7,3},{8,4},{9,5},{1... | collective-permute-start | bytes 98312 | tf_op jit(solution)/shard_map/ppermute | solution.py:73
  20.9 4.0 %collective-permute-start.6 = (f32[16,512]{1,0:T(8,128)S(1)}, f32[16,512]{1,0:T(8,128)S(1)}, u32[]{:S(2)}, u32[]{:S(2)}) collective-permute-start(f32[16,512]{1,0:T(8,128)S(1)} %get-tuple-element.26), channel_id=1, source_target_pairs={{0,16},{1,17},{2,18},{3,19},{4,20},{5,21},{6,22},{7,23},{8,24},{9,... | collective-permute-start | bytes 98312 | tf_op jit(solution)/shard_map/ppermute | solution.py:73
  24.8 3.3 %copy-start.2 = (bf16[512,256]{1,0:T(8,128)(2,1)S(1)}, bf16[512,256]{1,0:T(8,128)(2,1)}, u32[]{:S(2)}) copy-start(bf16[512,256]{1,0:T(8,128)(2,1)} %param.8) | copy-start | bytes 786436

commit v4 on v2

--- a/solution.py
+++ b/solution.py
@@ -38,8 +38,10 @@
     rate_t = decay_rate.T
     residue_t = residue.T
     offsets = jnp.arange(tok_block, dtype=jnp.float32)
-    to_end = jnp.exp(-rate_t[:, :, None] * (tok_block - 1.0 - offsets)[None, None, :])
-    block_state = jnp.sum(to_end * driven[None, :, :], axis=2)
+    half = tok_block // 2
+    folded = driven[None, :, :half] * jnp.exp(-rate_t * half)[:, :, None] + driven[None, :, half:]
+    to_end = jnp.exp(-rate_t[:, :, None] * (half - 1.0 - offsets[:half])[None, None, :])
+    block_state = jnp.sum(to_end * folded, axis=2)
     rounds = blocks.bit_length() - 1
     assert 1 << rounds == blocks
     pieces = min(rounds, 4)
@@ -69,10 +71,11 @@
             group_total, carry_in, chunk_out = lax.optimization_barrier((group_total, carry_in, chunk_out))
             direct.append(chunk_out)
     modal_state = residue * group_total.T
-    falling = jnp.exp(-rate_t[:, :, None] * offsets[None, None, :])
     carry_coef = residue_t * jnp.exp(-rate_t) * carry_in
-    carry_part = jnp.sum(carry_coef[:, :, None] * falling, axis=0)
-    convolved = jnp.concatenate(direct, axis=0) + carry_part
+    convolved = jnp.concatenate(direct, axis=0)
+    for mode in range(rate_t.shape[0]):
+        falling = jnp.exp(-rate_t[mode][:, None] * offsets[None, :])
+        convolved = convolved + carry_coef[mode][:, None] * falling
     layer_out = (outer_gate.astype(jnp.float32) * convolved).astype(jnp.bfloat16)
     return (layer_out, modal_state)
 

time: 28.5 us -> 30.7 us (1.077)
  other arithmetic: 8.01 us -> 10.2 us
    convert_element_type x1, other arithmetic: 0.79 us -> 4.29 us  [on_device(): (outer_gate.astype(jnp.float32) * convolved).astype(jnp.bfloat16)]
    reduce_sum x2 -> x1, other arithmetic: 4.97 us -> 3.63 us  [on_device(): block_state = jnp.sum(to_end * folded, axis=2)]
  transfers between devices with their start and end apart: 5 -> 5, of which waited for: 3 -> 3; matrix products, arithmetic and copies ran while one was open for 25% -> 23% of each run, Pallas kernels for 0% -> 0%
where the time goes in v4:
time: 30.7 us; the launch traced here: 30.5 us
  other arithmetic  10.2 us (33%)
  starting transfers between devices  10 us (33%)
  matrix products  6.76 us (22%)
  waiting for transfers between devices  2.48 us (8%)
  between operations  0.94 us (3%)
    ppermute x5, starting transfers between devices, on_device(): other = lax.ppermute(group_total, ('seq', 'chan'), pairs)  10 us
    dot_general x4, matrix products, prefix_sum(): jnp.einsum('mcs,st->mct', lower, tri, preferred_element_type=jnp.float32)  4.65 us
    convert_element_type x1, other arithmetic, on_device(): (outer_gate.astype(jnp.float32) * convolved).astype(jnp.bfloat16)  4.29 us
    reduce_sum x1, other arithmetic, on_device(): block_state = jnp.sum(to_end * folded, axis=2)  3.63 us
    ppermute x5, waiting for transfers between devices, on_device(): other = lax.ppermute(group_total, ('seq', 'chan'), pairs)  2.48 us
    dot_general x4, matrix products, prefix_sum(): jnp.einsum('mcs,st->mct', upper, tri, preferred_element_type=jnp.float32)  2.12 us
    convert_element_type x1, other arithmetic, on_device(): (inner_gate.astype(jnp.float32) * signal.astype(jnp.float32)).astype(jnp....  1.1 us
    mul x1, other arithmetic, on_device(): modal_state = residue * group_total.T  0.63 us
  transfers between devices with their start and end apart: 5, of which 3 were waited for; matrix products, arithmetic and copies ran while one was open for 23% of the time, Pallas kernels for 0%

profile of v4, /device:TPU:0, one launch (start us, length us, event | category | flops | bytes accessed | tf_op | source)
XLA Modules:
  0.0 30.5 jit_solution(5700355522354128749)
XLA Ops:
  0.6 1.1 %multiply_convert_fusion = bf16[512,256]{1,0:T(8,128)(2,1)S(1)} fusion(bf16[512,256]{1,0:T(8,128)(2,1)} %param.6, bf16[512,256]{1,0:T(8,128)(2,1)} %param.7), kind=kLoop, calls=%fused_computation.54 | loop fusion | flops 524288 | bytes 786432 | tf_op jit(solution)/shard_map/convert_element_type | solution.py:36
  1.9 3.6 %multiply_reduce_fusion = f32[16,512]{1,0:T(8,128)S(1)} fusion(f32[512,128]{1,0:T(8,128)S(1)} %get-tuple-element.47, f32[16,512]{1,0:T(8,128)S(1)} %get-tuple-element.101, f32[512,128]{1,0:T(8,128)S(1)} %get-tuple-element.46, f32[128]{0:T(128)S(1)} %slice_subtract_fusion, f32[16,512]{1,0:T(8,128)S(1)} %get-tuple-element.100), kind=kLoop, calls=%fused_computation | loop fusion | flops 5234688 | bytes 623104 | tf_op jit(solution)/shard_map/reduce_sum | solution.py:44
  5.6 3.1 %collective-permute-start = (f32[16,512]{1,0:T(8,128)S(1)}, f32[16,512]{1,0:T(8,128)S(1)}, u32[]{:S(2)}, u32[]{:S(2)}) collective-permute-start(f32[16,512]{1,0:T(8,128)S(1)} %multiply_reduce_fusion), channel_id=1, source_target_pairs={{0,1},{1,0},{2,3},{3,2},{4,5},{5,4},{6,7},{7,6},{8,9},{9,8},{10,11... | collective-permute-start | bytes 98312 | tf_op jit(solution)/shard_map/ppermute | solution.py:59
  8.7 0.5 %fusion.4 = f32[16,128,256]{2,1,0:T(8,128)S(1)} fusion(f32[128,256]{1,0:T(8,128)S(1)} %get-tuple-element.23, f32[16,128]{1,0:T(8,128)S(1)} %get-tuple-element.99), kind=kOutput, calls=%fused_computation.17 | convolution fusion | flops 270073856 | bytes 2236416 | tf_op jit(solution)/shard_map/mcs,st->mct/dot_general | solution.py:15
  9.2 1.2 %multiply_reduce_fusion.4 = f32[128,256]{1,0:T(8,128)S(1)} fusion(f32[16,128,256]{2,1,0:T(8,128)S(1)} %fusion.4, f32[128,256]{1,0:T(8,128)S(1)} %get-tuple-element.23, f32[16,128]{1,0:T(8,128)S(1)} %get-tuple-element.99, f32[16,128]{1,0:T(8,128)S(1)} %get-tuple-element.93, f32[16,128]{1,0:T(8,128)S(1)} %get-tuple-element.106), kind=kOutput, calls=%fused_computation.13 | convolution fusion | flops 274235392 | bytes 2383872 | tf_op jit(solution)/shard_map/mcs,st->mct/dot_general | solution.py:16
  10.4 0.1 multiply_add_fusion.3
  10.6 3.1 %collective-permute-start.1 = (f32[16,512]{1,0:T(8,128)S(1)}, f32[16,512]{1,0:T(8,128)S(1)}, u32[]{:S(2)}, u32[]{:S(2)}) collective-permute-start(f32[16,512]{1,0:T(8,128)S(1)} %get-tuple-element.26), channel_id=1, source_target_pairs={{0,2},{1,3},{2,0},{3,1},{4,6},{5,7},{6,4},{7,5},{8,10},{9,11},{10,... | collective-permute-start | bytes 98312 | tf_op jit(solution)/shard_map/ppermute | solution.py:59
  13.7 0.5 %fusion.6 = f32[16,128,256]{2,1,0:T(8,128)S(1)} fusion(f32[128,256]{1,0:T(8,128)S(1)} %get-tuple-element.28, f32[16,128]{1,0:T(8,128)S(1)} %get-tuple-element.98), kind=kOutput, calls=%fused_computation.18 | convolution fusion | flops 270073856 | bytes 2236416 | tf_op jit(solution)/shard_map/mcs,st->mct/dot_general | solution.py:15
  14.2 1.1 %multiply_reduce_fusion.3 = f32[128,256]{1,0:T(8,128)S(1)} fusion(f32[16,128,256]{2,1,0:T(8,128)S(1)} %fusion.6, f32[128,256]{1,0:T(8,128)S(1)} %get-tuple-element.28, f32[16,128]{1,0:T(8,128)S(1)} %get-tuple-element.98, f32[16,128]{1,0:T(8,128)S(1)} %get-tuple-element.94, f32[16,128]{1,0:T(8,128)S(1)} %get-tuple-element.107), kind=kOutput, calls=%fused_computation.9 | convolution fusion | flops 274235392 | bytes 2383872 | tf_op jit(solution)/shard_map/mcs,st->mct/dot_general | solution.py:16
  15.3 0.1 multiply_add_fusion.2
  15.4 0.1 collective-permute-done.1
  15.6 0.1 collective-permute-start.2
  15.7 0.5 %fusion.8 = f32[16,128,256]{2,1,0:T(8,128)S(1)} fusion(f32[128,256]{1,0:T(8,128)S(1)} %get-tuple-element.33, f32[16,128]{1,0:T(8,128)S(1)} %get-tuple-element.97), kind=kOutput, calls=%fused_computation.19 | convolution fusion | flops 270073856 | bytes 2236416 | tf_op jit(solution)/shard_map/mcs,st->mct/dot_general | solution.py:15
  16.2 1.2 %multiply_reduce_fusion.2 = f32[128,256]{1,0:T(8,128)S(1)} fusion(f32[16,128,256]{2,1,0:T(8,128)S(1)} %fusion.8, f32[128,256]{1,0:T(8,128)S(1)} %get-tuple-element.33, f32[16,128]{1,0:T(8,128)S(1)} %get-tuple-element.97, f32[16,128]{1,0:T(8,128)S(1)} %get-tuple-element.95, f32[16,128]{1,0:T(8,128)S(1)} %get-tuple-element.108), kind=kOutput, calls=%fused_computation.5 | convolution fusion | flops 274235392 | bytes 2383872 | tf_op jit(solution)/shard_map/mcs,st->mct/dot_general | solution.py:16
  17.4 0.1 multiply_add_fusion.1
  17.5 1.9 %collective-permute-start.3 = (f32[16,512]{1,0:T(8,128)S(1)}, f32[16,512]{1,0:T(8,128)S(1)}, u32[]{:S(2)}, u32[]{:S(2)}) collective-permute-start(f32[16,512]{1,0:T(8,128)S(1)} %get-tuple-element.36), channel_id=1, source_target_pairs={{0,8},{1,9},{2,10},{3,11},{4,12},{5,13},{6,14},{7,15},{8,0},{9,1},... | collective-permute-start | bytes 98312 | tf_op jit(solution)/shard_map/ppermute | solution.py:59
  19.4 0.5 %fusion.10 = f32[16,128,256]{2,1,0:T(8,128)S(1)} fusion(f32[128,256]{1,0:T(8,128)S(1)} %get-tuple-element.38, f32[16,128]{1,0:T(8,128)S(1)} %get-tuple-element.96), kind=kOutput, calls=%fused_computation.20 | convolution fusion | flops 270073856 | bytes 2236416 | tf_op jit(solution)/shard_map/mcs,st->mct/dot_general | solution.py:15
  20.0 1.1 %multiply_reduce_fusion.1 = f32[128,256]{1,0:T(8,128)S(1)} fusion(f32[16,128,256]{2,1,0:T(8,128)S(1)} %fusion.10, f32[128,256]{1,0:T(8,128)S(1)} %get-tuple-element.38, f32[16,128]{1,0:T(8,128)S(1)} %get-tuple-element.96, f32[16,128]{1,0:T(8,128)S(1)} %get-tuple-element.92, f32[16,128]{1,0:T(8,128)S(1)} %get-tuple-element.109), kind=kOutput, calls=%fused_computation.1 | convolution fusion | flops 274235392 | bytes 2383872 | tf_op jit(solution)/shard_map/mcs,st->mct/dot_general | solution.py:16
  21.1 0.1 multiply_add_fusion
  21.2 0.3 %collective-permute-done.3 = f32[16,512]{1,0:T(8,128)S(1)} collective-permute-done((f32[16,512]{1,0:T(8,128)S(1)}, f32[16,512]{1,0:T(8,128)S(1)}, u32[]{:S(2)}, u32[]{:S(2)}) %collective-permute-start.3) | collective-permute-done | bytes 32800 | tf_op jit(solution)/shard_map/ppermute | solution.py:59
  21.5 1.9 %collective-permute-start.4 = (f32[16,512]{1,0:T(8,128)S(1)}, f32[16,512]{1,0:T(8,128)S(1)}, u32[]{:S(2)}, u32[]{:S(2)}) collective-permute-start(f32[16,512]{1,0:T(8,128)S(1)} %get-tuple-element.41), channel_id=1, source_target_pairs={{0,16},{1,17},{2,18},{3,19},{4,20},{5,21},{6,22},{7,23},{8,24},{9,... | collective-permute-start | bytes 98312 | tf_op jit(solution)/shard_map/ppermute | solution.py:59
  23.5 2.0 %collective-permute-done.4 = f32[16,512]{1,0:T(8,128)S(1)} collective-permute-done((f32[16,512]{1,0:T(8,128)S(1)}, f32[16,512]{1,0:T(8,128)S(1)}, u32[]{:S(2)}, u32[]{:S(2)}) %collective-permute-start.4) | collective-permute-done | bytes 32800 | tf_op jit(solution)/shard_map/ppermute | solution.py:59
  25.6 4.3 %fusion.44 = bf16[512,256]{1,0:T(8,128)(2,1)} fusion(f32[128,256]{1,0:T(8,128)S(1)} %multiply_add_fusion, f32[128,256]{1,0:T(8,128)S(1)} %multiply_add_fusion.1, f32[128,256]{1,0:T(8,128)S(1)} %multiply_add_fusion.2, f32[128,256]{1,0:T(8,128)S(1)} %multiply_add_fusion.3, bf16[512,256]{1,0:T(8,128)(2,1)S(1)} %copy-done.3, f32[512]{0:T(512)S(1)} %bitcast.90, ...), kind=kLoop, calls=%fused_computation.55 | loop fusion | flops 7077888 | bytes 1114112 | tf_op jit(solution)/shard_map/convert_element_type | solution.py:79
  29.9 0.6 %bitcast_multiply_fusion = f32[512,16]{0,1:T(8,128)} fusion(f32[512,16]{0,1:T(8,128)S(1)} %copy-done.1, f32[16,512]{1,0:T(8,128)S(1)} %collective-permute-done.4, f32[16,512]{1,0:T(8,128)S(1)} %get-tuple-element.41, pred[]{:T(512)S(6)} %ne.42, f32[512,16]{0,1:T(8,128)S(1)} %copy-done), kind=kLoop, calls=%fused_computation.67 | loop fusion | flops 65536 | bytes 163841 | tf_op jit(solution)/shard_map/mul | solution.py:73
  (24 shorter events, 0.3 us)
Async XLA Ops:
  0.6 1.2 %copy-start = (f32[512,16]{0,1:T(8,128)S(1)}, f32[512,16]{0,1:T(8,128)}, u32[]{:S(2)}) copy-start(f32[512,16]{0,1:T(8,128)} %param.9) | copy-start | bytes 98308
  1.7 6.9 %copy-start.2 = (f32[512]{0:T(512)S(1)}, f32[512]{0:T(512)}, u32[]{:S(2)}) copy-start(f32[512]{0:T(512)} %param.11) | copy-start | bytes 6148
  1.8 6.9 %copy-start.1 = (f32[512,16]{0,1:T(8,128)S(1)}, f32[512,16]{0,1:T(8,128)}, u32[]{:S(2)}) copy-start(f32[512,16]{0,1:T(8,128)} %param.10) | copy-start | bytes 98308
  5.6 5.0 %collective-permute-start = (f32[16,512]{1,0:T(8,128)S(1)}, f32[16,512]{1,0:T(8,128)S(1)}, u32[]{:S(2)}, u32[]{:S(2)}) collective-permute-start(f32[16,512]{1,0:T(8,128)S(1)} %multiply_reduce_fusion), channel_id=1, source_target_pairs={{0,1},{1,0},{2,3},{3,2},{4,5},{5,4},{6,7},{7,6},{8,9},{9,8},{10,11... | collective-permute-start | bytes 98312 | tf_op jit(solution)/shard_map/ppermute | solution.py:59
  10.6 5.0 %collective-permute-start.1 = (f32[16,512]{1,0:T(8,128)S(1)}, f32[16,512]{1,0:T(8,128)S(1)}, u32[]{:S(2)}, u32[]{:S(2)}) collective-permute-start(f32[16,512]{1,0:T(8,128)S(1)} %get-tuple-element.26), channel_id=1, source_target_pairs={{0,2},{1,3},{2,0},{3,1},{4,6},{5,7},{6,4},{7,5},{8,10},{9,11},{10,... | collective-permute-start | bytes 98312 | tf_op jit(solution)/shard_map/ppermute | solution.py:59
  15.6 1.9 %collective-permute-start.2 = (f32[16,512]{1,0:T(8,128)S(1)}, f32[16,512]{1,0:T(8,128)S(1)}, u32[]{:S(2)}, u32[]{:S(2)}) collective-permute-start(f32[16,512]{1,0:T(8,128)S(1)} %get-tuple-element.31), channel_id=1, source_target_pairs={{0,4},{1,5},{2,6},{3,7},{4,0},{5,1},{6,2},{7,3},{8,12},{9,13},{10,... | collective-permute-start | bytes 98312 | tf_op jit(solution)/shard_map/ppermute | solution.py:59
  17.5 4.0 %collective-permute-start.3 = (f32[16,512]{1,0:T(8,128)S(1)}, f32[16,512]{1,0:T(8,128)S(1)}, u32[]{:S(2)}, u32[]{:S(2)}) collective-permute-start(f32[16,512]{1,0:T(8,128)S(1)} %get-tuple-element.36), channel_id=1, source_target_pairs={{0,8},{1,9},{2,10},{3,11},{4,12},{5,13},{6,14},{7,15},{8,0},{9,1},... | collective-permute-start | bytes 98312 | tf_op jit(solution)/shard_map/ppermute | solution.py:59
  19.9 5.6 %copy-start.3 = (bf16[512,256]{1,0:T(8,128)(2,1)S(1)}, bf16[512,256]{1,0:T(8,128)(2,1)}, u32[]{:S(2)}) copy-start(bf16[512,256]{1,0:T(8,128)(2,1)} %param.8) | copy-start | bytes 786436
  21.5 4.0 %collective-permute-start.4 = (f32[16,512]{1,0:T(8,128)S(1)}, f32[16,512]{1,0:T(8,128)S(1)}, u32[]{:S(2)}, u32[]{:S(2)}) collective-permute-start(f32[16,512]{1,0:T(8,128)S(1)} %get-tuple-element.41), channel_id=1, source_target_pairs={{0,16},{1,17},{2,18},{3,19},{4,20},{5,21},{6,22},{7,23},{8,24},{9,... | collective-permute-start | bytes 98312 | tf_op jit(solution)/shard_map/ppermute | solution.py:59

commit v5 on v2

--- a/solution.py
+++ b/solution.py
@@ -38,7 +38,10 @@
     rate_t = decay_rate.T
     residue_t = residue.T
     offsets = jnp.arange(tok_block, dtype=jnp.float32)
-    to_end = jnp.exp(-rate_t[:, :, None] * (tok_block - 1.0 - offsets)[None, None, :])
+    half = tok_block // 2
+    half_span = jnp.exp(-rate_t * half)[:, :, None]
+    near_end = jnp.exp(-rate_t[:, :, None] * (half - 1.0 - offsets[:half])[None, None, :])
+    to_end = jnp.concatenate([near_end * half_span, near_end], axis=2)
     block_state = jnp.sum(to_end * driven[None, :, :], axis=2)
     rounds = blocks.bit_length() - 1
     assert 1 << rounds == blocks
@@ -69,9 +72,11 @@
             group_total, carry_in, chunk_out = lax.optimization_barrier((group_total, carry_in, chunk_out))
             direct.append(chunk_out)
     modal_state = residue * group_total.T
-    falling = jnp.exp(-rate_t[:, :, None] * offsets[None, None, :])
-    carry_coef = residue_t * jnp.exp(-rate_t) * carry_in
-    carry_part = jnp.sum(carry_coef[:, :, None] * falling, axis=0)
+    near_start = jnp.exp(-rate_t[:, :, None] * offsets[None, None, :half])
+    carry_coef = (residue_t * jnp.exp(-rate_t) * carry_in)[:, :, None]
+    carry_part = jnp.concatenate(
+        [jnp.sum(carry_coef * near_start, axis=0), jnp.sum(carry_coef * half_span * near_start, axis=0)], axis=1
+    )
     convolved = jnp.concatenate(direct, axis=0) + carry_part
     layer_out = (outer_gate.astype(jnp.float32) * convolved).astype(jnp.bfloat16)
     return (layer_out, modal_state)

time: 28.5 us -> 31 us (1.088)
  other arithmetic: 8.01 us -> 10.6 us
    mul x1 -> x2, other arithmetic: 0.02 us -> 2.36 us  [the longest x1 2.33 us: on_device(): to_end = jnp.concatenate([near_end * half_span, near_end], axis=2)]
    reduce_sum x1, other arithmetic: 2.5 us -> 3.9 us  [on_device(): jnp.sum(carry_coef * near_start, axis=0)]
    reduce_sum x1, other arithmetic: 2.47 us -> 1.31 us  [on_device(): block_state = jnp.sum(to_end * driven[None, :, :], axis=2)]
  transfers between devices with their start and end apart: 5 -> 5, of which waited for: 3 -> 3; matrix products, arithmetic and copies ran while one was open for 25% -> 23% of each run, Pallas kernels for 0% -> 0%
where the time goes in v5:
time: 31 us; the launch traced here: 30.9 us
  other arithmetic  10.6 us (34%)
  starting transfers between devices  10 us (32%)
  matrix products  6.76 us (22%)
  waiting for transfers between devices  2.52 us (8%)
  between operations  0.92 us (3%)
    ppermute x5, starting transfers between devices, on_device(): other = lax.ppermute(group_total, ('seq', 'chan'), pairs)  10 us
    dot_general x4, matrix products, prefix_sum(): jnp.einsum('mcs,st->mct', lower, tri, preferred_element_type=jnp.float32)  4.65 us
    reduce_sum x1, other arithmetic, on_device(): jnp.sum(carry_coef * near_start, axis=0)  3.9 us
    ppermute x5, waiting for transfers between devices, on_device(): other = lax.ppermute(group_total, ('seq', 'chan'), pairs)  2.52 us
    mul x1, other arithmetic, on_device(): to_end = jnp.concatenate([near_end * half_span, near_end], axis=2)  2.33 us
    dot_general x4, matrix products, prefix_sum(): jnp.einsum('mcs,st->mct', upper, tri, preferred_element_type=jnp.float32)  2.11 us
    reduce_sum x1, other arithmetic, on_device(): block_state = jnp.sum(to_end * driven[None, :, :], axis=2)  1.31 us
    convert_element_type x1, other arithmetic, on_device(): (inner_gate.astype(jnp.float32) * signal.astype(jnp.float32)).astype(jnp....  1.1 us
  transfers between devices with their start and end apart: 5, of which 3 were waited for; matrix products, arithmetic and copies ran while one was open for 23% of the time, Pallas kernels for 0%

profile of v5, /device:TPU:0, one launch (start us, length us, event | category | flops | bytes accessed | tf_op | source)
XLA Modules:
  0.0 30.9 jit_solution(17325799565837490268)
XLA Ops:
  0.6 1.1 %multiply_convert_fusion = bf16[512,256]{1,0:T(8,128)(2,1)S(1)} fusion(bf16[512,256]{1,0:T(8,128)(2,1)} %param.6, bf16[512,256]{1,0:T(8,128)(2,1)} %param.7), kind=kLoop, calls=%fused_computation.46 | loop fusion | flops 524288 | bytes 786432 | tf_op jit(solution)/shard_map/convert_element_type | solution.py:36
  1.9 2.3 %broadcast_multiply_fusion = (f32[16,512,128]{2,1,0:T(8,128)S(1)}, f32[16,512,128]{2,1,0:T(8,128)S(1)}) fusion(f32[16,512]{1,0:T(8,128)S(1)} %get-tuple-element.72, f32[128]{0:T(128)S(1)} %get-tuple-element.79, f32[16,512]{1,0:T(8,128)S(1)} %get-tuple-element.73), kind=kLoop, calls=%fused_computation.22 | loop fusion | flops 2097152 | bytes 8454656 | tf_op jit(solution)/shard_map/mul | solution.py:44
  4.3 1.3 %fusion = f32[16,512]{1,0:T(8,128)S(1)} fusion(f32[16,512,128]{2,1,0:T(8,128)S(1)} %get-tuple-element.59, f32[16,512,128]{2,1,0:T(8,128)S(1)} %get-tuple-element.58, f32[512,256]{1,0:T(8,128)S(1)} %convert_element_type.75), kind=kLoop, calls=%fused_computation.1 | loop fusion | flops 6283264 | bytes 8945664 | tf_op jit(solution)/shard_map/reduce_sum | solution.py:45
  5.6 3.1 %collective-permute-start = (f32[16,512]{1,0:T(8,128)S(1)}, f32[16,512]{1,0:T(8,128)S(1)}, u32[]{:S(2)}, u32[]{:S(2)}) collective-permute-start(f32[16,512]{1,0:T(8,128)S(1)} %fusion), channel_id=1, source_target_pairs={{0,1},{1,0},{2,3},{3,2},{4,5},{5,4},{6,7},{7,6},{8,9},{9,8},{10,11... | collective-permute-start | bytes 98312 | tf_op jit(solution)/shard_map/ppermute | solution.py:60
  8.7 0.5 %fusion.5 = f32[16,128,256]{2,1,0:T(8,128)S(1)} fusion(f32[128,256]{1,0:T(8,128)S(1)} %get-tuple-element.23, f32[16,128]{1,0:T(8,128)S(1)} %get-tuple-element.69), kind=kOutput, calls=%fused_computation.23 | convolution fusion | flops 270073856 | bytes 2236416 | tf_op jit(solution)/shard_map/mcs,st->mct/dot_general | solution.py:15
  9.2 1.2 %multiply_reduce_fusion.5 = f32[128,256]{1,0:T(8,128)S(1)} fusion(f32[16,128,256]{2,1,0:T(8,128)S(1)} %fusion.5, f32[128,256]{1,0:T(8,128)S(1)} %get-tuple-element.23, f32[16,128]{1,0:T(8,128)S(1)} %get-tuple-element.69, f32[16,128]{1,0:T(8,128)S(1)} %get-tuple-element.65, f32[16,128]{1,0:T(8,128)S(1)} %get-tuple-element.80), kind=kOutput, calls=%fused_computation.18 | convolution fusion | flops 274235392 | bytes 2383872 | tf_op jit(solution)/shard_map/mcs,st->mct/dot_general | solution.py:16
  10.4 0.1 multiply_add_fusion.3
  10.6 3.1 %collective-permute-start.1 = (f32[16,512]{1,0:T(8,128)S(1)}, f32[16,512]{1,0:T(8,128)S(1)}, u32[]{:S(2)}, u32[]{:S(2)}) collective-permute-start(f32[16,512]{1,0:T(8,128)S(1)} %get-tuple-element.26), channel_id=1, source_target_pairs={{0,2},{1,3},{2,0},{3,1},{4,6},{5,7},{6,4},{7,5},{8,10},{9,11},{10,... | collective-permute-start | bytes 98312 | tf_op jit(solution)/shard_map/ppermute | solution.py:60
  13.7 0.5 %fusion.7 = f32[16,128,256]{2,1,0:T(8,128)S(1)} fusion(f32[128,256]{1,0:T(8,128)S(1)} %get-tuple-element.28, f32[16,128]{1,0:T(8,128)S(1)} %get-tuple-element.68), kind=kOutput, calls=%fused_computation.24 | convolution fusion | flops 270073856 | bytes 2236416 | tf_op jit(solution)/shard_map/mcs,st->mct/dot_general | solution.py:15
  14.2 1.1 %multiply_reduce_fusion.4 = f32[128,256]{1,0:T(8,128)S(1)} fusion(f32[16,128,256]{2,1,0:T(8,128)S(1)} %fusion.7, f32[128,256]{1,0:T(8,128)S(1)} %get-tuple-element.28, f32[16,128]{1,0:T(8,128)S(1)} %get-tuple-element.68, f32[16,128]{1,0:T(8,128)S(1)} %get-tuple-element.66, f32[16,128]{1,0:T(8,128)S(1)} %get-tuple-element.81), kind=kOutput, calls=%fused_computation.14 | convolution fusion | flops 274235392 | bytes 2383872 | tf_op jit(solution)/shard_map/mcs,st->mct/dot_general | solution.py:16
  15.3 0.1 multiply_add_fusion.2
  15.4 0.1 collective-permute-done.1
  15.7 0.5 %fusion.9 = f32[16,128,256]{2,1,0:T(8,128)S(1)} fusion(f32[128,256]{1,0:T(8,128)S(1)} %get-tuple-element.33, f32[16,128]{1,0:T(8,128)S(1)} %get-tuple-element.71), kind=kOutput, calls=%fused_computation.25 | convolution fusion | flops 270073856 | bytes 2236416 | tf_op jit(solution)/shard_map/mcs,st->mct/dot_general | solution.py:15
  16.2 1.2 %multiply_reduce_fusion.3 = f32[128,256]{1,0:T(8,128)S(1)} fusion(f32[16,128,256]{2,1,0:T(8,128)S(1)} %fusion.9, f32[128,256]{1,0:T(8,128)S(1)} %get-tuple-element.33, f32[16,128]{1,0:T(8,128)S(1)} %get-tuple-element.71, f32[16,128]{1,0:T(8,128)S(1)} %get-tuple-element.67, f32[16,128]{1,0:T(8,128)S(1)} %get-tuple-element.82), kind=kOutput, calls=%fused_computation.10 | convolution fusion | flops 274235392 | bytes 2383872 | tf_op jit(solution)/shard_map/mcs,st->mct/dot_general | solution.py:16
  17.4 0.1 multiply_add_fusion.1
  17.5 1.9 %collective-permute-start.3 = (f32[16,512]{1,0:T(8,128)S(1)}, f32[16,512]{1,0:T(8,128)S(1)}, u32[]{:S(2)}, u32[]{:S(2)}) collective-permute-start(f32[16,512]{1,0:T(8,128)S(1)} %get-tuple-element.36), channel_id=1, source_target_pairs={{0,8},{1,9},{2,10},{3,11},{4,12},{5,13},{6,14},{7,15},{8,0},{9,1},... | collective-permute-start | bytes 98312 | tf_op jit(solution)/shard_map/ppermute | solution.py:60
  19.4 0.5 %fusion.11 = f32[16,128,256]{2,1,0:T(8,128)S(1)} fusion(f32[128,256]{1,0:T(8,128)S(1)} %get-tuple-element.38, f32[16,128]{1,0:T(8,128)S(1)} %get-tuple-element.70), kind=kOutput, calls=%fused_computation.26 | convolution fusion | flops 270073856 | bytes 2236416 | tf_op jit(solution)/shard_map/mcs,st->mct/dot_general | solution.py:15
  20.0 1.1 %multiply_reduce_fusion.2 = f32[128,256]{1,0:T(8,128)S(1)} fusion(f32[16,128,256]{2,1,0:T(8,128)S(1)} %fusion.11, f32[128,256]{1,0:T(8,128)S(1)} %get-tuple-element.38, f32[16,128]{1,0:T(8,128)S(1)} %get-tuple-element.70, f32[16,128]{1,0:T(8,128)S(1)} %get-tuple-element.64, f32[16,128]{1,0:T(8,128)S(1)} %get-tuple-element.83), kind=kOutput, calls=%fused_computation.6 | convolution fusion | flops 274235392 | bytes 2383872 | tf_op jit(solution)/shard_map/mcs,st->mct/dot_general | solution.py:16
  21.2 0.3 %collective-permute-done.3 = f32[16,512]{1,0:T(8,128)S(1)} collective-permute-done((f32[16,512]{1,0:T(8,128)S(1)}, f32[16,512]{1,0:T(8,128)S(1)}, u32[]{:S(2)}, u32[]{:S(2)}) %collective-permute-start.3) | collective-permute-done | bytes 32800 | tf_op jit(solution)/shard_map/ppermute | solution.py:60
  21.5 1.9 %collective-permute-start.4 = (f32[16,512]{1,0:T(8,128)S(1)}, f32[16,512]{1,0:T(8,128)S(1)}, u32[]{:S(2)}, u32[]{:S(2)}) collective-permute-start(f32[16,512]{1,0:T(8,128)S(1)} %get-tuple-element.41), channel_id=1, source_target_pairs={{0,16},{1,17},{2,18},{3,19},{4,20},{5,21},{6,22},{7,23},{8,24},{9,... | collective-permute-start | bytes 98312 | tf_op jit(solution)/shard_map/ppermute | solution.py:60
  23.5 2.1 %collective-permute-done.4 = f32[16,512]{1,0:T(8,128)S(1)} collective-permute-done((f32[16,512]{1,0:T(8,128)S(1)}, f32[16,512]{1,0:T(8,128)S(1)}, u32[]{:S(2)}, u32[]{:S(2)}) %collective-permute-start.4) | collective-permute-done | bytes 32800 | tf_op jit(solution)/shard_map/ppermute | solution.py:60
  25.6 3.9 %multiply_reduce_fusion.1 = (f32[512,128]{1,0:T(8,128)S(1)}, f32[512,128]{1,0:T(8,128)S(1)}) fusion(f32[128]{0:T(128)S(1)} %get-tuple-element.78, f32[16,512]{1,0:T(8,128)S(1)} %get-tuple-element.45, f32[16,512]{1,0:T(8,128)S(1)} %get-tuple-element.73, f32[16,512]{1,0:T(8,128)S(1)} %get-tuple-element.44), kind=kLoop, calls=%fused_computation.3 | loop fusion | flops 5111808 | bytes 623104 | tf_op jit(solution)/shard_map/reduce_sum | solution.py:78
  29.5 0.8 %fusion.30 = bf16[512,256]{1,0:T(8,128)(2,1)} fusion(f32[128,256]{1,0:T(8,128)S(1)} %multiply_add_fusion, f32[128,256]{1,0:T(8,128)S(1)} %multiply_add_fusion.1, f32[128,256]{1,0:T(8,128)S(1)} %multiply_add_fusion.2, f32[128,256]{1,0:T(8,128)S(1)} %multiply_add_fusion.3, f32[512,128]{1,0:T(8,128)S(1)} %get-tuple-element.43, ...), kind=kLoop, calls=%fused_computation.45 | loop fusion | flops 1048576 | bytes 1572864 | tf_op jit(solution)/shard_map/convert_element_type | solution.py:81
  30.3 0.6 %bitcast_multiply_fusion = f32[512,16]{0,1:T(8,128)} fusion(f32[512,16]{0,1:T(8,128)S(1)} %copy-done.1, f32[16,512]{1,0:T(8,128)S(1)} %collective-permute-done.4, f32[16,512]{1,0:T(8,128)S(1)} %get-tuple-element.41, pred[]{:T(512)S(6)} %ne.42, f32[512,16]{0,1:T(8,128)S(1)} %copy-done), kind=kLoop, calls=%fused_computation.58 | loop fusion | flops 65536 | bytes 163841 | tf_op jit(solution)/shard_map/mul | solution.py:74
  (24 shorter events, 0.4 us)
Async XLA Ops:
  0.6 1.2 %copy-start = (f32[512,16]{0,1:T(8,128)S(1)}, f32[512,16]{0,1:T(8,128)}, u32[]{:S(2)}) copy-start(f32[512,16]{0,1:T(8,128)} %param.9) | copy-start | bytes 98308
  4.2 4.4 %copy-start.3 = (f32[512]{0:T(512)S(1)}, f32[512]{0:T(512)}, u32[]{:S(2)}) copy-start(f32[512]{0:T(512)} %param.11) | copy-start | bytes 6148
  4.2 4.4 %copy-start.1 = (f32[512,16]{0,1:T(8,128)S(1)}, f32[512,16]{0,1:T(8,128)}, u32[]{:S(2)}) copy-start(f32[512,16]{0,1:T(8,128)} %param.10) | copy-start | bytes 98308
  5.6 5.0 %collective-permute-start = (f32[16,512]{1,0:T(8,128)S(1)}, f32[16,512]{1,0:T(8,128)S(1)}, u32[]{:S(2)}, u32[]{:S(2)}) collective-permute-start(f32[16,512]{1,0:T(8,128)S(1)} %fusion), channel_id=1, source_target_pairs={{0,1},{1,0},{2,3},{3,2},{4,5},{5,4},{6,7},{7,6},{8,9},{9,8},{10,11... | collective-permute-start | bytes 98312 | tf_op jit(solution)/shard_map/ppermute | solution.py:60
  10.6 5.0 %collective-permute-start.1 = (f32[16,512]{1,0:T(8,128)S(1)}, f32[16,512]{1,0:T(8,128)S(1)}, u32[]{:S(2)}, u32[]{:S(2)}) collective-permute-start(f32[16,512]{1,0:T(8,128)S(1)} %get-tuple-element.26), channel_id=1, source_target_pairs={{0,2},{1,3},{2,0},{3,1},{4,6},{5,7},{6,4},{7,5},{8,10},{9,11},{10,... | collective-permute-start | bytes 98312 | tf_op jit(solution)/shard_map/ppermute | solution.py:60
  15.6 1.9 %collective-permute-start.2 = (f32[16,512]{1,0:T(8,128)S(1)}, f32[16,512]{1,0:T(8,128)S(1)}, u32[]{:S(2)}, u32[]{:S(2)}) collective-permute-start(f32[16,512]{1,0:T(8,128)S(1)} %get-tuple-element.31), channel_id=1, source_target_pairs={{0,4},{1,5},{2,6},{3,7},{4,0},{5,1},{6,2},{7,3},{8,12},{9,13},{10,... | collective-permute-start | bytes 98312 | tf_op jit(solution)/shard_map/ppermute | solution.py:60
  17.5 4.0 %collective-permute-start.3 = (f32[16,512]{1,0:T(8,128)S(1)}, f32[16,512]{1,0:T(8,128)S(1)}, u32[]{:S(2)}, u32[]{:S(2)}) collective-permute-start(f32[16,512]{1,0:T(8,128)S(1)} %get-tuple-element.36), channel_id=1, source_target_pairs={{0,8},{1,9},{2,10},{3,11},{4,12},{5,13},{6,14},{7,15},{8,0},{9,1},... | collective-permute-start | bytes 98312 | tf_op jit(solution)/shard_map/ppermute | solution.py:60
  21.1 8.4 %copy-start.2 = (bf16[512,256]{1,0:T(8,128)(2,1)S(1)}, bf16[512,256]{1,0:T(8,128)(2,1)}, u32[]{:S(2)}) copy-start(bf16[512,256]{1,0:T(8,128)(2,1)} %param.8) | copy-start | bytes 786436
  21.5 4.0 %collective-permute-start.4 = (f32[16,512]{1,0:T(8,128)S(1)}, f32[16,512]{1,0:T(8,128)S(1)}, u32[]{:S(2)}, u32[]{:S(2)}) collective-permute-start(f32[16,512]{1,0:T(8,128)S(1)} %get-tuple-element.41), channel_id=1, source_target_pairs={{0,16},{1,17},{2,18},{3,19},{4,20},{5,21},{6,22},{7,23},{8,24},{9,... | collective-permute-start | bytes 98312 | tf_op jit(solution)/shard_map/ppermute | solution.py:60

commit v6 on v2

--- a/solution.py
+++ b/solution.py
@@ -1,6 +1,8 @@
 import jax
 import jax.numpy as jnp
 from jax import lax
+from jax.experimental import pallas as pl
+from jax.experimental.pallas import tpu as pltpu
 from jax.sharding import PartitionSpec as P
 
 
@@ -25,6 +27,51 @@
     running = prefix_sum(rising * driven[None, :, :], prefix_matrix(tok_block))
     local_part = jnp.sum(residue_t[:, :, None] * falling * running, axis=0)
     return local_part + skip_gain[:, None] * driven
+
+
+def finish_kernel(*refs):
+    coef_ref, rate_ref, total_ref, residue_ref, outer_ref = refs[:5]
+    direct_refs = refs[5:-2]
+    out_ref, modal_ref = refs[-2:]
+    piece, tok_block = direct_refs[0].shape
+    modes = coef_ref.shape[0]
+    half = tok_block // 2
+    lanes = lax.broadcasted_iota(jnp.int32, (1, half), 1).astype(jnp.float32)
+    for index, direct_ref in enumerate(direct_refs):
+        rows = slice(index * piece, (index + 1) * piece)
+        coef = coef_ref[:, rows].T
+        rate = rate_ref[:, rows].T
+        modal_ref[rows, :] = residue_ref[rows, :] * total_ref[:, rows].T
+        low = direct_ref[:, :half]
+        high = direct_ref[:, half:]
+        for mode in range(modes):
+            rate_m = rate[:, mode:mode + 1]
+            coef_m = coef[:, mode:mode + 1]
+            power = jnp.exp(-rate_m * lanes)
+            low = low + coef_m * power
+            high = high + (coef_m * jnp.exp(-rate_m * half)) * power
+        out_ref[rows, :half] = (outer_ref[rows, :half].astype(jnp.float32) * low).astype(out_ref.dtype)
+        out_ref[rows, half:] = (outer_ref[rows, half:].astype(jnp.float32) * high).astype(out_ref.dtype)
+
+
+def finish(carry_coef, rate_t, group_total, residue, outer_gate, direct):
+    channels, tok_block = outer_gate.shape
+    modes = rate_t.shape[0]
+    whole = pl.BlockSpec(memory_space=pltpu.VMEM)
+    return pl.pallas_call(
+        finish_kernel,
+        out_shape=(
+            jax.ShapeDtypeStruct((channels, tok_block), jnp.bfloat16),
+            jax.ShapeDtypeStruct((channels, modes), jnp.float32),
+        ),
+        in_specs=[whole] * (5 + len(direct)),
+        out_specs=(whole, whole),
+        cost_estimate=pl.CostEstimate(
+            flops=4 * modes * channels * tok_block,
+            transcendentals=modes * channels * tok_block // 2,
+            bytes_accessed=10 * channels * tok_block,
+        ),
+    )(carry_coef, rate_t, group_total, residue, outer_gate, *direct)
 
 
 def on_device(signal, inner_gate, outer_gate, decay_rate, residue, skip_gain):
@@ -68,12 +115,8 @@
         if level < pieces:
             group_total, carry_in, chunk_out = lax.optimization_barrier((group_total, carry_in, chunk_out))
             direct.append(chunk_out)
-    modal_state = residue * group_total.T
-    falling = jnp.exp(-rate_t[:, :, None] * offsets[None, None, :])
     carry_coef = residue_t * jnp.exp(-rate_t) * carry_in
-    carry_part = jnp.sum(carry_coef[:, :, None] * falling, axis=0)
-    convolved = jnp.concatenate(direct, axis=0) + carry_part
-    layer_out = (outer_gate.astype(jnp.float32) * convolved).astype(jnp.bfloat16)
+    layer_out, modal_state = finish(carry_coef, rate_t, group_total, residue, outer_gate, direct)
     return (layer_out, modal_state)
 
 

time: 28.5 us -> 33.9 us (1.19)
  Pallas kernels: 0 us -> 5.76 us
  local copies, waits for them, and re-layouts: 0.07 us -> 2.55 us
  starting transfers between devices: 10 us -> 8.95 us
  waiting for transfers between devices: 2.54 us -> 1.6 us
  other arithmetic: 8.01 us -> 7.32 us
    pallas_call x0 -> x1, Pallas kernels: none -> 5.76 us  [finish(): pl.pallas_call(finish_kernel, out_shape=(jax.ShapeDtypeStruct((channels,...]
    add x4, other arithmetic: 0.34 us -> 2.95 us  [local_chunk(): return local_part + skip_gain[:, None] * driven]
    reduce_sum x1 -> x0, other arithmetic: 2.5 us -> none  [on_device(): carry_part = jnp.sum(carry_coef[:, :, None] * falling, axis=0)]
    pallas_call x0 -> x1, local copies, waits for them, and re-layouts: none -> 1.67 us  [finish(): pl.pallas_call(finish_kernel, out_shape=(jax.ShapeDtypeStruct((channels,...]
    ppermute x5, starting transfers between devices: 10 us -> 8.95 us  [on_device(): other = lax.ppermute(group_total, ('seq', 'chan'), pairs)]
    ppermute x5, waiting for transfers between devices: 2.54 us -> 1.6 us  [on_device(): other = lax.ppermute(group_total, ('seq', 'chan'), pairs)]
    unnamed x8 -> x7, local copies, waits for them, and re-layouts: 0.02 us -> 0.84 us
    convert_element_type x1 -> x0, other arithmetic: 0.79 us -> none  [on_device(): (outer_gate.astype(jnp.float32) * convolved).astype(jnp.bfloat16)]
  transfers between devices with their start and end apart: 5 -> 5, of which waited for: 3 -> 1; matrix products, arithmetic and copies ran while one was open for 25% -> 31% of each run, Pallas kernels for 0% -> 0%
where the time goes in v6:
time: 33.9 us; the launch traced here: 33.7 us
  starting transfers between devices  8.95 us (26%)
  other arithmetic  7.32 us (22%)
  matrix products  6.79 us (20%)
  Pallas kernels  5.76 us (17%)
  local copies, waits for them, and re-layouts  2.55 us (8%)
  waiting for transfers between devices  1.6 us (5%)
  between operations  0.79 us (2%)
    ppermute x5, starting transfers between devices, on_device(): other = lax.ppermute(group_total, ('seq', 'chan'), pairs)  8.95 us
    pallas_call x1, Pallas kernels, finish(): pl.pallas_call(finish_kernel, out_shape=(jax.ShapeDtypeStruct((channels,...  5.76 us
    dot_general x4, matrix products, prefix_sum(): jnp.einsum('mcs,st->mct', lower, tri, preferred_element_type=jnp.float32)  4.68 us
    add x4, other arithmetic, local_chunk(): return local_part + skip_gain[:, None] * driven  2.95 us
    reduce_sum x1, other arithmetic, on_device(): block_state = jnp.sum(to_end * driven[None, :, :], axis=2)  2.47 us
    dot_general x4, matrix products, prefix_sum(): jnp.einsum('mcs,st->mct', upper, tri, preferred_element_type=jnp.float32)  2.11 us
    pallas_call x1, local copies, waits for them, and re-layouts, finish(): pl.pallas_call(finish_kernel, out_shape=(jax.ShapeDtypeStruct((channels,...  1.67 us
    ppermute x5, waiting for transfers between devices, on_device(): other = lax.ppermute(group_total, ('seq', 'chan'), pairs)  1.6 us
  transfers between devices with their start and end apart: 5, of which 1 were waited for; matrix products, arithmetic and copies ran while one was open for 31% of the time, Pallas kernels for 0%

profile of v6, /device:TPU:0, one launch (start us, length us, event | category | flops | bytes accessed | tf_op | source)
XLA Modules:
  0.0 33.7 jit_solution(17783152663151872061)
XLA Ops:
  0.6 1.1 %multiply_convert_fusion = bf16[512,256]{1,0:T(8,128)(2,1)S(1)} fusion(bf16[512,256]{1,0:T(8,128)(2,1)} %param.6, bf16[512,256]{1,0:T(8,128)(2,1)} %param.7), kind=kLoop, calls=%fused_computation.37 | loop fusion | flops 524288 | bytes 786432 | tf_op jit(solution)/shard_map/convert_element_type | solution.py:83
  1.9 2.5 %multiply_reduce_fusion = f32[16,512]{1,0:T(8,128)S(1)} fusion(f32[512,256]{1,0:T(8,128)S(1)} %convert_element_type.68, f32[256]{0:T(256)S(1)} %iota_subtract_fusion, f32[16,512]{1,0:T(8,128)S(1)} %bitcast_negate_fusion), kind=kLoop, calls=%fused_computation | loop fusion | flops 6283264 | bytes 590848 | tf_op jit(solution)/shard_map/reduce_sum | solution.py:89
  4.4 3.1 %collective-permute-start = (f32[16,512]{1,0:T(8,128)S(1)}, f32[16,512]{1,0:T(8,128)S(1)}, u32[]{:S(2)}, u32[]{:S(2)}) collective-permute-start(f32[16,512]{1,0:T(8,128)S(1)} %multiply_reduce_fusion), channel_id=1, source_target_pairs={{0,1},{1,0},{2,3},{3,2},{4,5},{5,4},{6,7},{7,6},{8,9},{9,8},{10,11... | collective-permute-start | bytes 98312 | tf_op jit(solution)/shard_map/ppermute | solution.py:104
  7.5 0.5 %fusion.4 = f32[16,128,256]{2,1,0:T(8,128)S(1)} fusion(f32[128,256]{1,0:T(8,128)S(1)} %get-tuple-element.23, f32[16,128]{1,0:T(8,128)S(1)} %get-tuple-element.70), kind=kOutput, calls=%fused_computation.17 | convolution fusion | flops 270073856 | bytes 2236416 | tf_op jit(solution)/shard_map/mcs,st->mct/dot_general | solution.py:17
  8.0 1.2 %multiply_reduce_fusion.4 = f32[128,256]{1,0:T(8,128)S(1)} fusion(f32[16,128,256]{2,1,0:T(8,128)S(1)} %fusion.4, f32[128,256]{1,0:T(8,128)S(1)} %get-tuple-element.23, f32[16,128]{1,0:T(8,128)S(1)} %get-tuple-element.70, f32[16,128]{1,0:T(8,128)S(1)} %get-tuple-element.65, f32[16,128]{1,0:T(8,128)S(1)} %get-tuple-element.76), kind=kOutput, calls=%fused_computation.13 | convolution fusion | flops 274235392 | bytes 2383872 | tf_op jit(solution)/shard_map/mcs,st->mct/dot_general | solution.py:18
  9.3 0.7 %multiply_add_fusion.3.refs_5_ = f32[128,256]{1,0:T(8,128)} fusion(f32[128,256]{1,0:T(8,128)S(1)} %multiply_reduce_fusion.4, f32[128,256]{1,0:T(8,128)S(1)} %get-tuple-element.23, f32[128]{0:T(128)S(1)} %get-tuple-element.74), kind=kLoop, calls=%fused_computation.43 | loop fusion | flops 65536 | bytes 393728 | tf_op jit(solution)/shard_map/add | solution.py:29
  10.0 2.7 %collective-permute-start.1 = (f32[16,512]{1,0:T(8,128)S(1)}, f32[16,512]{1,0:T(8,128)S(1)}, u32[]{:S(2)}, u32[]{:S(2)}) collective-permute-start(f32[16,512]{1,0:T(8,128)S(1)} %get-tuple-element.25), channel_id=1, source_target_pairs={{0,2},{1,3},{2,0},{3,1},{4,6},{5,7},{6,4},{7,5},{8,10},{9,11},{10,... | collective-permute-start | bytes 98312 | tf_op jit(solution)/shard_map/ppermute | solution.py:104
  12.7 0.5 %fusion.6 = f32[16,128,256]{2,1,0:T(8,128)S(1)} fusion(f32[128,256]{1,0:T(8,128)S(1)} %get-tuple-element.27, f32[16,128]{1,0:T(8,128)S(1)} %get-tuple-element.69), kind=kOutput, calls=%fused_computation.18 | convolution fusion | flops 270073856 | bytes 2236416 | tf_op jit(solution)/shard_map/mcs,st->mct/dot_general | solution.py:17
  13.2 1.1 %multiply_reduce_fusion.3 = f32[128,256]{1,0:T(8,128)S(1)} fusion(f32[16,128,256]{2,1,0:T(8,128)S(1)} %fusion.6, f32[128,256]{1,0:T(8,128)S(1)} %get-tuple-element.27, f32[16,128]{1,0:T(8,128)S(1)} %get-tuple-element.69, f32[16,128]{1,0:T(8,128)S(1)} %get-tuple-element.66, f32[16,128]{1,0:T(8,128)S(1)} %get-tuple-element.77), kind=kOutput, calls=%fused_computation.9 | convolution fusion | flops 274235392 | bytes 2383872 | tf_op jit(solution)/shard_map/mcs,st->mct/dot_general | solution.py:18
  14.3 0.7 %multiply_add_fusion.2.refs_6_ = f32[128,256]{1,0:T(8,128)} fusion(f32[128,256]{1,0:T(8,128)S(1)} %multiply_reduce_fusion.3, f32[128,256]{1,0:T(8,128)S(1)} %get-tuple-element.27, f32[128]{0:T(128)S(1)} %get-tuple-element.73), kind=kLoop, calls=%fused_computation.42 | loop fusion | flops 65536 | bytes 393728 | tf_op jit(solution)/shard_map/add | solution.py:29
  15.1 0.1 collective-permute-start.2
  15.2 0.5 %fusion.8 = f32[16,128,256]{2,1,0:T(8,128)S(1)} fusion(f32[128,256]{1,0:T(8,128)S(1)} %get-tuple-element.31, f32[16,128]{1,0:T(8,128)S(1)} %get-tuple-element.68), kind=kOutput, calls=%fused_computation.19 | convolution fusion | flops 270073856 | bytes 2236416 | tf_op jit(solution)/shard_map/mcs,st->mct/dot_general | solution.py:17
  15.7 1.2 %multiply_reduce_fusion.2 = f32[128,256]{1,0:T(8,128)S(1)} fusion(f32[16,128,256]{2,1,0:T(8,128)S(1)} %fusion.8, f32[128,256]{1,0:T(8,128)S(1)} %get-tuple-element.31, f32[16,128]{1,0:T(8,128)S(1)} %get-tuple-element.68, f32[16,128]{1,0:T(8,128)S(1)} %get-tuple-element.67, f32[16,128]{1,0:T(8,128)S(1)} %get-tuple-element.78), kind=kOutput, calls=%fused_computation.5 | convolution fusion | flops 274235392 | bytes 2383872 | tf_op jit(solution)/shard_map/mcs,st->mct/dot_general | solution.py:18
  16.9 0.7 %multiply_add_fusion.1.refs_7_ = f32[128,256]{1,0:T(8,128)} fusion(f32[128,256]{1,0:T(8,128)S(1)} %multiply_reduce_fusion.2, f32[128,256]{1,0:T(8,128)S(1)} %get-tuple-element.31, f32[128]{0:T(128)S(1)} %get-tuple-element.75), kind=kLoop, calls=%fused_computation.41 | loop fusion | flops 65536 | bytes 393728 | tf_op jit(solution)/shard_map/add | solution.py:29
  17.7 1.6 %collective-permute-start.3 = (f32[16,512]{1,0:T(8,128)S(1)}, f32[16,512]{1,0:T(8,128)S(1)}, u32[]{:S(2)}, u32[]{:S(2)}) collective-permute-start(f32[16,512]{1,0:T(8,128)S(1)} %get-tuple-element.33), channel_id=1, source_target_pairs={{0,8},{1,9},{2,10},{3,11},{4,12},{5,13},{6,14},{7,15},{8,0},{9,1},... | collective-permute-start | bytes 98312 | tf_op jit(solution)/shard_map/ppermute | solution.py:104
  19.2 0.5 %fusion.10 = f32[16,128,256]{2,1,0:T(8,128)S(1)} fusion(f32[128,256]{1,0:T(8,128)S(1)} %get-tuple-element.35, f32[16,128]{1,0:T(8,128)S(1)} %get-tuple-element.71), kind=kOutput, calls=%fused_computation.20 | convolution fusion | flops 270073856 | bytes 2236416 | tf_op jit(solution)/shard_map/mcs,st->mct/dot_general | solution.py:17
  19.8 1.1 %multiply_reduce_fusion.1 = f32[128,256]{1,0:T(8,128)S(1)} fusion(f32[16,128,256]{2,1,0:T(8,128)S(1)} %fusion.10, f32[128,256]{1,0:T(8,128)S(1)} %get-tuple-element.35, f32[16,128]{1,0:T(8,128)S(1)} %get-tuple-element.71, f32[16,128]{1,0:T(8,128)S(1)} %get-tuple-element.64, f32[16,128]{1,0:T(8,128)S(1)} %get-tuple-element.79), kind=kOutput, calls=%fused_computation.1 | convolution fusion | flops 274235392 | bytes 2383872 | tf_op jit(solution)/shard_map/mcs,st->mct/dot_general | solution.py:18
  20.9 0.7 %multiply_add_fusion.refs_8_ = f32[128,256]{1,0:T(8,128)} fusion(f32[128,256]{1,0:T(8,128)S(1)} %multiply_reduce_fusion.1, f32[128,256]{1,0:T(8,128)S(1)} %get-tuple-element.35, f32[128]{0:T(128)S(1)} %get-tuple-element.72), kind=kLoop, calls=%fused_computation.40 | loop fusion | flops 65536 | bytes 393728 | tf_op jit(solution)/shard_map/add | solution.py:29
  21.7 1.6 %collective-permute-start.4 = (f32[16,512]{1,0:T(8,128)S(1)}, f32[16,512]{1,0:T(8,128)S(1)}, u32[]{:S(2)}, u32[]{:S(2)}) collective-permute-start(f32[16,512]{1,0:T(8,128)S(1)} %get-tuple-element.37), channel_id=1, source_target_pairs={{0,16},{1,17},{2,18},{3,19},{4,20},{5,21},{6,22},{7,23},{8,24},{9,... | collective-permute-start | bytes 98312 | tf_op jit(solution)/shard_map/ppermute | solution.py:104
  23.3 0.8 %copy.10.refs_3_ = f32[512,16]{1,0:T(8,128)} copy(f32[512,16]{0,1:T(8,128)S(1)} %copy-done.1) | data formatting | bytes 65536 | tf_op args[4]
  24.1 1.6 %collective-permute-done.4 = f32[16,512]{1,0:T(8,128)S(1)} collective-permute-done((f32[16,512]{1,0:T(8,128)S(1)}, f32[16,512]{1,0:T(8,128)S(1)}, u32[]{:S(2)}, u32[]{:S(2)}) %collective-permute-start.4) | collective-permute-done | bytes 32800 | tf_op jit(solution)/shard_map/ppermute | solution.py:104
  25.7 0.7 %multiply_add_fusion.4 = (f32[16,512]{1,0:T(8,128)}, f32[16,512]{1,0:T(8,128)}) fusion(f32[16,512]{1,0:T(8,128)S(1)} %collective-permute-done.4, f32[16,512]{1,0:T(8,128)S(1)} %get-tuple-element.37, pred[]{:T(512)S(6)} %ne.35, f32[512,16]{0,1:T(8,128)S(1)} %copy-done, f32[16,512]{1,0:T(8,128)S(1)} %get-tuple-element.36, f32[]{:T(128)S(6)} %convert_element_type.84, ...), kind=kLoop, calls=%fused_computation.49 | loop fusion | flops 114688 | bytes 229381 | tf_op jit(solution)/shard_map/add | solution.py:114
  26.3 5.8 %shard_map.77 = (bf16[512,256]{1,0:T(8,128)(2,1)}, f32[512,16]{1,0:T(8,128)}) custom-call(f32[16,512]{1,0:T(8,128)} %get-tuple-element.51.refs_0_, f32[16,512]{1,0:T(8,128)} %bitcast.37, f32[16,512]{1,0:T(8,128)} %get-tuple-element.50.refs_2_, f32[512,16]{1,0:T(8,128)} %copy.10.refs_3_, bf16[512,256]{1,0:T(8,128)(2,1)} %refs_4_.1, ...), custom_call_target="tpu_custom_call" | custom-call | flops 8388608 | bytes 1310720 | tf_op jit(solution)/shard_map/pallas_call | solution.py:61
  32.1 1.7 %copy.11 = f32[512,16]{0,1:T(8,128)} copy(f32[512,16]{1,0:T(8,128)} %get-tuple-element.45) | data formatting | bytes 65536 | tf_op jit(solution)/shard_map/pallas_call | solution.py:61
  (20 shorter events, 0.2 us)
Async XLA Ops:
  0.6 1.2 %copy-start = (f32[512,16]{0,1:T(8,128)S(1)}, f32[512,16]{0,1:T(8,128)}, u32[]{:S(2)}) copy-start(f32[512,16]{0,1:T(8,128)} %param.9) | copy-start | bytes 98308
  1.8 5.6 %copy-start.2 = (f32[512]{0:T(512)S(1)}, f32[512]{0:T(512)}, u32[]{:S(2)}) copy-start(f32[512]{0:T(512)} %param.11) | copy-start | bytes 6148
  1.8 5.6 %copy-start.1 = (f32[512,16]{0,1:T(8,128)S(1)}, f32[512,16]{0,1:T(8,128)}, u32[]{:S(2)}) copy-start(f32[512,16]{0,1:T(8,128)} %param.10) | copy-start | bytes 98308
  4.4 5.6 %collective-permute-start = (f32[16,512]{1,0:T(8,128)S(1)}, f32[16,512]{1,0:T(8,128)S(1)}, u32[]{:S(2)}, u32[]{:S(2)}) collective-permute-start(f32[16,512]{1,0:T(8,128)S(1)} %multiply_reduce_fusion), channel_id=1, source_target_pairs={{0,1},{1,0},{2,3},{3,2},{4,5},{5,4},{6,7},{7,6},{8,9},{9,8},{10,11... | collective-permute-start | bytes 98312 | tf_op jit(solution)/shard_map/ppermute | solution.py:104
  10.0 5.1 %collective-permute-start.1 = (f32[16,512]{1,0:T(8,128)S(1)}, f32[16,512]{1,0:T(8,128)S(1)}, u32[]{:S(2)}, u32[]{:S(2)}) collective-permute-start(f32[16,512]{1,0:T(8,128)S(1)} %get-tuple-element.25), channel_id=1, source_target_pairs={{0,2},{1,3},{2,0},{3,1},{4,6},{5,7},{6,4},{7,5},{8,10},{9,11},{10,... | collective-permute-start | bytes 98312 | tf_op jit(solution)/shard_map/ppermute | solution.py:104
  15.1 2.5 %collective-permute-start.2 = (f32[16,512]{1,0:T(8,128)S(1)}, f32[16,512]{1,0:T(8,128)S(1)}, u32[]{:S(2)}, u32[]{:S(2)}) collective-permute-start(f32[16,512]{1,0:T(8,128)S(1)} %get-tuple-element.29), channel_id=1, source_target_pairs={{0,4},{1,5},{2,6},{3,7},{4,0},{5,1},{6,2},{7,3},{8,12},{9,13},{10,... | collective-permute-start | bytes 98312 | tf_op jit(solution)/shard_map/ppermute | solution.py:104
  17.7 4.0 %collective-permute-start.3 = (f32[16,512]{1,0:T(8,128)S(1)}, f32[16,512]{1,0:T(8,128)S(1)}, u32[]{:S(2)}, u32[]{:S(2)}) collective-permute-start(f32[16,512]{1,0:T(8,128)S(1)} %get-tuple-element.33), channel_id=1, source_target_pairs={{0,8},{1,9},{2,10},{3,11},{4,12},{5,13},{6,14},{7,15},{8,0},{9,1},... | collective-permute-start | bytes 98312 | tf_op jit(solution)/shard_map/ppermute | solution.py:104
  21.7 4.0 %collective-permute-start.4 = (f32[16,512]{1,0:T(8,128)S(1)}, f32[16,512]{1,0:T(8,128)S(1)}, u32[]{:S(2)}, u32[]{:S(2)}) collective-permute-start(f32[16,512]{1,0:T(8,128)S(1)} %get-tuple-element.37), channel_id=1, source_target_pairs={{0,16},{1,17},{2,18},{3,19},{4,20},{5,21},{6,22},{7,23},{8,24},{9,... | collective-permute-start | bytes 98312 | tf_op jit(solution)/shard_map/ppermute | solution.py:104

commit v7 on v2

--- a/solution.py
+++ b/solution.py
@@ -34,7 +34,7 @@
     blocks = seq_count * chan_count
     owner_idx = lax.axis_index("seq") * chan_count + lax.axis_index("chan")
     gated_in = (inner_gate.astype(jnp.float32) * signal.astype(jnp.float32)).astype(jnp.bfloat16)
-    driven = lax.optimization_barrier(gated_in).astype(jnp.float32)
+    driven = gated_in.astype(jnp.float32)
     rate_t = decay_rate.T
     residue_t = residue.T
     offsets = jnp.arange(tok_block, dtype=jnp.float32)

time: 28.5 us -> 28.4 us (level)
    convert_element_type x2 -> x1, other arithmetic: 1.14 us -> 1.09 us  [on_device(): driven = gated_in.astype(jnp.float32)]
where the time goes in v7:
time: 28.4 us; the launch traced here: 28.3 us
  starting transfers between devices  10 us (35%)
  other arithmetic  7.96 us (28%)
  matrix products  6.76 us (24%)
  waiting for transfers between devices  2.54 us (9%)
  between operations  0.9 us (3%)
    ppermute x5, starting transfers between devices, on_device(): other = lax.ppermute(group_total, ('seq', 'chan'), pairs)  10 us
    dot_general x4, matrix products, prefix_sum(): jnp.einsum('mcs,st->mct', lower, tri, preferred_element_type=jnp.float32)  4.65 us
    ppermute x5, waiting for transfers between devices, on_device(): other = lax.ppermute(group_total, ('seq', 'chan'), pairs)  2.54 us
    reduce_sum x1, other arithmetic, on_device(): carry_part = jnp.sum(carry_coef[:, :, None] * falling, axis=0)  2.5 us
    reduce_sum x1, other arithmetic, on_device(): block_state = jnp.sum(to_end * driven[None, :, :], axis=2)  2.47 us
    dot_general x4, matrix products, prefix_sum(): jnp.einsum('mcs,st->mct', upper, tri, preferred_element_type=jnp.float32)  2.11 us
    convert_element_type x1, other arithmetic, on_device(): driven = gated_in.astype(jnp.float32)  1.09 us
    convert_element_type x1, other arithmetic, on_device(): (outer_gate.astype(jnp.float32) * convolved).astype(jnp.bfloat16)  0.79 us
  transfers between devices with their start and end apart: 5, of which 3 were waited for; matrix products, arithmetic and copies ran while one was open for 25% of the time, Pallas kernels for 0%

profile of v7, /device:TPU:0, one launch (start us, length us, event | category | flops | bytes accessed | tf_op | source)
XLA Modules:
  0.0 28.3 jit_solution(11328269538072411041)
XLA Ops:
  0.7 1.1 %fusion.30 = f32[512,256]{1,0:T(8,128)S(1)} fusion(bf16[512,256]{1,0:T(8,128)(2,1)} %param.6, bf16[512,256]{1,0:T(8,128)(2,1)} %param.7), kind=kLoop, calls=%fused_computation.42 | loop fusion | flops 655360 | bytes 1048576 | tf_op jit(solution)/shard_map/convert_element_type | solution.py:37
  1.8 2.5 %multiply_reduce_fusion.1 = f32[16,512]{1,0:T(8,128)S(1)} fusion(f32[512,256]{1,0:T(8,128)S(1)} %fusion.30, f32[256]{0:T(256)S(1)} %iota_subtract_fusion, f32[16,512]{1,0:T(8,128)S(1)} %bitcast_negate_fusion), kind=kLoop, calls=%fused_computation.1 | loop fusion | flops 6283264 | bytes 590848 | tf_op jit(solution)/shard_map/reduce_sum | solution.py:42
  4.3 3.1 %collective-permute-start = (f32[16,512]{1,0:T(8,128)S(1)}, f32[16,512]{1,0:T(8,128)S(1)}, u32[]{:S(2)}, u32[]{:S(2)}) collective-permute-start(f32[16,512]{1,0:T(8,128)S(1)} %multiply_reduce_fusion.1), channel_id=1, source_target_pairs={{0,1},{1,0},{2,3},{3,2},{4,5},{5,4},{6,7},{7,6},{8,9},{9,8},{10,11... | collective-permute-start | bytes 98312 | tf_op jit(solution)/shard_map/ppermute | solution.py:57
  7.4 0.5 %fusion.4 = f32[16,128,256]{2,1,0:T(8,128)S(1)} fusion(f32[128,256]{1,0:T(8,128)S(1)} %get-tuple-element.23, f32[16,128]{1,0:T(8,128)S(1)} %get-tuple-element.63), kind=kOutput, calls=%fused_computation.18 | convolution fusion | flops 270073856 | bytes 2236416 | tf_op jit(solution)/shard_map/mcs,st->mct/dot_general | solution.py:15
  8.0 1.2 %multiply_reduce_fusion.5 = f32[128,256]{1,0:T(8,128)S(1)} fusion(f32[16,128,256]{2,1,0:T(8,128)S(1)} %fusion.4, f32[128,256]{1,0:T(8,128)S(1)} %get-tuple-element.23, f32[16,128]{1,0:T(8,128)S(1)} %get-tuple-element.63, f32[16,128]{1,0:T(8,128)S(1)} %get-tuple-element.59, f32[16,128]{1,0:T(8,128)S(1)} %get-tuple-element.70), kind=kOutput, calls=%fused_computation.14 | convolution fusion | flops 274235392 | bytes 2383872 | tf_op jit(solution)/shard_map/mcs,st->mct/dot_general | solution.py:16
  9.2 0.1 multiply_add_fusion.3
  9.3 3.1 %collective-permute-start.1 = (f32[16,512]{1,0:T(8,128)S(1)}, f32[16,512]{1,0:T(8,128)S(1)}, u32[]{:S(2)}, u32[]{:S(2)}) collective-permute-start(f32[16,512]{1,0:T(8,128)S(1)} %get-tuple-element.26), channel_id=1, source_target_pairs={{0,2},{1,3},{2,0},{3,1},{4,6},{5,7},{6,4},{7,5},{8,10},{9,11},{10,... | collective-permute-start | bytes 98312 | tf_op jit(solution)/shard_map/ppermute | solution.py:57
  12.4 0.5 %fusion.6 = f32[16,128,256]{2,1,0:T(8,128)S(1)} fusion(f32[128,256]{1,0:T(8,128)S(1)} %get-tuple-element.28, f32[16,128]{1,0:T(8,128)S(1)} %get-tuple-element.62), kind=kOutput, calls=%fused_computation.19 | convolution fusion | flops 270073856 | bytes 2236416 | tf_op jit(solution)/shard_map/mcs,st->mct/dot_general | solution.py:15
  13.0 1.1 %multiply_reduce_fusion.4 = f32[128,256]{1,0:T(8,128)S(1)} fusion(f32[16,128,256]{2,1,0:T(8,128)S(1)} %fusion.6, f32[128,256]{1,0:T(8,128)S(1)} %get-tuple-element.28, f32[16,128]{1,0:T(8,128)S(1)} %get-tuple-element.62, f32[16,128]{1,0:T(8,128)S(1)} %get-tuple-element.60, f32[16,128]{1,0:T(8,128)S(1)} %get-tuple-element.71), kind=kOutput, calls=%fused_computation.10 | convolution fusion | flops 274235392 | bytes 2383872 | tf_op jit(solution)/shard_map/mcs,st->mct/dot_general | solution.py:16
  14.1 0.1 multiply_add_fusion.2
  14.2 0.1 collective-permute-done.1
  14.4 0.5 %fusion.8 = f32[16,128,256]{2,1,0:T(8,128)S(1)} fusion(f32[128,256]{1,0:T(8,128)S(1)} %get-tuple-element.33, f32[16,128]{1,0:T(8,128)S(1)} %get-tuple-element.65), kind=kOutput, calls=%fused_computation.20 | convolution fusion | flops 270073856 | bytes 2236416 | tf_op jit(solution)/shard_map/mcs,st->mct/dot_general | solution.py:15
  15.0 1.2 %multiply_reduce_fusion.3 = f32[128,256]{1,0:T(8,128)S(1)} fusion(f32[16,128,256]{2,1,0:T(8,128)S(1)} %fusion.8, f32[128,256]{1,0:T(8,128)S(1)} %get-tuple-element.33, f32[16,128]{1,0:T(8,128)S(1)} %get-tuple-element.65, f32[16,128]{1,0:T(8,128)S(1)} %get-tuple-element.61, f32[16,128]{1,0:T(8,128)S(1)} %get-tuple-element.72), kind=kOutput, calls=%fused_computation.6 | convolution fusion | flops 274235392 | bytes 2383872 | tf_op jit(solution)/shard_map/mcs,st->mct/dot_general | solution.py:16
  16.2 0.1 multiply_add_fusion.1
  16.3 1.9 %collective-permute-start.3 = (f32[16,512]{1,0:T(8,128)S(1)}, f32[16,512]{1,0:T(8,128)S(1)}, u32[]{:S(2)}, u32[]{:S(2)}) collective-permute-start(f32[16,512]{1,0:T(8,128)S(1)} %get-tuple-element.36), channel_id=1, source_target_pairs={{0,8},{1,9},{2,10},{3,11},{4,12},{5,13},{6,14},{7,15},{8,0},{9,1},... | collective-permute-start | bytes 98312 | tf_op jit(solution)/shard_map/ppermute | solution.py:57
  18.2 0.5 %fusion.10 = f32[16,128,256]{2,1,0:T(8,128)S(1)} fusion(f32[128,256]{1,0:T(8,128)S(1)} %get-tuple-element.38, f32[16,128]{1,0:T(8,128)S(1)} %get-tuple-element.64), kind=kOutput, calls=%fused_computation.21 | convolution fusion | flops 270073856 | bytes 2236416 | tf_op jit(solution)/shard_map/mcs,st->mct/dot_general | solution.py:15
  18.7 1.1 %multiply_reduce_fusion.2 = f32[128,256]{1,0:T(8,128)S(1)} fusion(f32[16,128,256]{2,1,0:T(8,128)S(1)} %fusion.10, f32[128,256]{1,0:T(8,128)S(1)} %get-tuple-element.38, f32[16,128]{1,0:T(8,128)S(1)} %get-tuple-element.64, f32[16,128]{1,0:T(8,128)S(1)} %get-tuple-element.58, f32[16,128]{1,0:T(8,128)S(1)} %get-tuple-element.73), kind=kOutput, calls=%fused_computation.2 | convolution fusion | flops 274235392 | bytes 2383872 | tf_op jit(solution)/shard_map/mcs,st->mct/dot_general | solution.py:16
  19.8 0.1 multiply_add_fusion
  19.9 0.3 %collective-permute-done.3 = f32[16,512]{1,0:T(8,128)S(1)} collective-permute-done((f32[16,512]{1,0:T(8,128)S(1)}, f32[16,512]{1,0:T(8,128)S(1)}, u32[]{:S(2)}, u32[]{:S(2)}) %collective-permute-start.3) | collective-permute-done | bytes 32800 | tf_op jit(solution)/shard_map/ppermute | solution.py:57
  20.3 1.9 %collective-permute-start.4 = (f32[16,512]{1,0:T(8,128)S(1)}, f32[16,512]{1,0:T(8,128)S(1)}, u32[]{:S(2)}, u32[]{:S(2)}) collective-permute-start(f32[16,512]{1,0:T(8,128)S(1)} %get-tuple-element.41), channel_id=1, source_target_pairs={{0,16},{1,17},{2,18},{3,19},{4,20},{5,21},{6,22},{7,23},{8,24},{9,... | collective-permute-start | bytes 98312 | tf_op jit(solution)/shard_map/ppermute | solution.py:57
  22.2 2.1 %collective-permute-done.4 = f32[16,512]{1,0:T(8,128)S(1)} collective-permute-done((f32[16,512]{1,0:T(8,128)S(1)}, f32[16,512]{1,0:T(8,128)S(1)}, u32[]{:S(2)}, u32[]{:S(2)}) %collective-permute-start.4) | collective-permute-done | bytes 32800 | tf_op jit(solution)/shard_map/ppermute | solution.py:57
  24.3 2.5 %multiply_reduce_fusion = f32[512,256]{1,0:T(8,128)S(1)} fusion(f32[16,512]{1,0:T(8,128)S(1)} %fusion.40, f32[16,512]{1,0:T(8,128)S(1)} %bitcast_negate_fusion), kind=kLoop, calls=%fused_computation | loop fusion | flops 6160384 | bytes 589824 | tf_op jit(solution)/shard_map/reduce_sum | solution.py:74
  26.8 0.8 %fusion.29 = bf16[512,256]{1,0:T(8,128)(2,1)} fusion(f32[512,256]{1,0:T(8,128)S(1)} %multiply_reduce_fusion, f32[128,256]{1,0:T(8,128)S(1)} %multiply_add_fusion, f32[128,256]{1,0:T(8,128)S(1)} %multiply_add_fusion.1, f32[128,256]{1,0:T(8,128)S(1)} %multiply_add_fusion.2, f32[128,256]{1,0:T(8,128)S(1)} %multiply_add_fusion.3, bf16[512,256]{1,0:T(8,128)(2,1)S(1)} %copy-done.2), kind=kLoop, calls=%fused_computation.40 | loop fusion | flops 917504 | bytes 1572864 | tf_op jit(solution)/shard_map/convert_element_type | solution.py:76
  27.6 0.6 %bitcast_multiply_fusion = f32[512,16]{0,1:T(8,128)} fusion(f32[512,16]{0,1:T(8,128)S(1)} %copy-done.1, f32[16,512]{1,0:T(8,128)S(1)} %collective-permute-done.4, f32[16,512]{1,0:T(8,128)S(1)} %get-tuple-element.41, pred[]{:T(512)S(6)} %ne.42, f32[512,16]{0,1:T(8,128)S(1)} %copy-done), kind=kLoop, calls=%fused_computation.54 | loop fusion | flops 65536 | bytes 163841 | tf_op jit(solution)/shard_map/mul | solution.py:71
  (21 shorter events, 0.3 us)
Async XLA Ops:
  0.6 1.2 %copy-start = (f32[512,16]{0,1:T(8,128)S(1)}, f32[512,16]{0,1:T(8,128)}, u32[]{:S(2)}) copy-start(f32[512,16]{0,1:T(8,128)} %param.9) | copy-start | bytes 98308
  1.8 5.6 %copy-start.3 = (f32[512]{0:T(512)S(1)}, f32[512]{0:T(512)}, u32[]{:S(2)}) copy-start(f32[512]{0:T(512)} %param.11) | copy-start | bytes 6148
  1.8 5.6 %copy-start.1 = (f32[512,16]{0,1:T(8,128)S(1)}, f32[512,16]{0,1:T(8,128)}, u32[]{:S(2)}) copy-start(f32[512,16]{0,1:T(8,128)} %param.10) | copy-start | bytes 98308
  4.3 5.0 %collective-permute-start = (f32[16,512]{1,0:T(8,128)S(1)}, f32[16,512]{1,0:T(8,128)S(1)}, u32[]{:S(2)}, u32[]{:S(2)}) collective-permute-start(f32[16,512]{1,0:T(8,128)S(1)} %multiply_reduce_fusion.1), channel_id=1, source_target_pairs={{0,1},{1,0},{2,3},{3,2},{4,5},{5,4},{6,7},{7,6},{8,9},{9,8},{10,11... | collective-permute-start | bytes 98312 | tf_op jit(solution)/shard_map/ppermute | solution.py:57
  9.3 5.0 %collective-permute-start.1 = (f32[16,512]{1,0:T(8,128)S(1)}, f32[16,512]{1,0:T(8,128)S(1)}, u32[]{:S(2)}, u32[]{:S(2)}) collective-permute-start(f32[16,512]{1,0:T(8,128)S(1)} %get-tuple-element.26), channel_id=1, source_target_pairs={{0,2},{1,3},{2,0},{3,1},{4,6},{5,7},{6,4},{7,5},{8,10},{9,11},{10,... | collective-permute-start | bytes 98312 | tf_op jit(solution)/shard_map/ppermute | solution.py:57
  14.3 1.9 %collective-permute-start.2 = (f32[16,512]{1,0:T(8,128)S(1)}, f32[16,512]{1,0:T(8,128)S(1)}, u32[]{:S(2)}, u32[]{:S(2)}) collective-permute-start(f32[16,512]{1,0:T(8,128)S(1)} %get-tuple-element.31), channel_id=1, source_target_pairs={{0,4},{1,5},{2,6},{3,7},{4,0},{5,1},{6,2},{7,3},{8,12},{9,13},{10,... | collective-permute-start | bytes 98312 | tf_op jit(solution)/shard_map/ppermute | solution.py:57
  16.3 4.0 %collective-permute-start.3 = (f32[16,512]{1,0:T(8,128)S(1)}, f32[16,512]{1,0:T(8,128)S(1)}, u32[]{:S(2)}, u32[]{:S(2)}) collective-permute-start(f32[16,512]{1,0:T(8,128)S(1)} %get-tuple-element.36), channel_id=1, source_target_pairs={{0,8},{1,9},{2,10},{3,11},{4,12},{5,13},{6,14},{7,15},{8,0},{9,1},... | collective-permute-start | bytes 98312 | tf_op jit(solution)/shard_map/ppermute | solution.py:57
  20.3 6.5 %copy-start.2 = (bf16[512,256]{1,0:T(8,128)(2,1)S(1)}, bf16[512,256]{1,0:T(8,128)(2,1)}, u32[]{:S(2)}) copy-start(bf16[512,256]{1,0:T(8,128)(2,1)} %param.8) | copy-start | bytes 786436
  20.3 4.0 %collective-permute-start.4 = (f32[16,512]{1,0:T(8,128)S(1)}, f32[16,512]{1,0:T(8,128)S(1)}, u32[]{:S(2)}, u32[]{:S(2)}) collective-permute-start(f32[16,512]{1,0:T(8,128)S(1)} %get-tuple-element.41), channel_id=1, source_target_pairs={{0,16},{1,17},{2,18},{3,19},{4,20},{5,21},{6,22},{7,23},{8,24},{9,... | collective-permute-start | bytes 98312 | tf_op jit(solution)/shard_map/ppermute | solution.py:57

commit v8 on v2

--- a/solution.py
+++ b/solution.py
@@ -42,8 +42,8 @@
     block_state = jnp.sum(to_end * driven[None, :, :], axis=2)
     rounds = blocks.bit_length() - 1
     assert 1 << rounds == blocks
-    pieces = min(rounds, 4)
-    piece = channels // pieces
+    pieces = rounds
+    bounds = [min(channels, (channels * i // pieces + 7) // 8 * 8) for i in range(pieces + 1)]
     span_rate = rate_t * tok_block
     carry_in = jnp.zeros_like(block_state)
     group_total = block_state
@@ -51,13 +51,13 @@
     for level in range(rounds):
         width = 1 << level
         if level < pieces:
-            lo = level * piece
-            group_total, chunk_in = lax.optimization_barrier((group_total, driven[lo:lo + piece]))
+            lo, hi = bounds[level], bounds[level + 1]
+            group_total, chunk_in = lax.optimization_barrier((group_total, driven[lo:hi]))
         pairs = [(src_i, src_i ^ width) for src_i in range(blocks)]
         other = lax.ppermute(group_total, ("seq", "chan"), pairs)
         if level < pieces:
             chunk_out = local_chunk(
-                chunk_in, rate_t[:, lo:lo + piece], residue_t[:, lo:lo + piece], skip_gain[lo:lo + piece]
+                chunk_in, rate_t[:, lo:hi], residue_t[:, lo:hi], skip_gain[lo:hi]
             )
         upper = (owner_idx & width) != 0
         place = (owner_idx % width).astype(jnp.float32)

time: 28.5 us -> 28.2 us (0.989)
  waiting for transfers between devices: 2.54 us -> 1.48 us
  matrix products: 6.76 us -> 7.16 us
    ppermute x5, waiting for transfers between devices: 2.54 us -> 1.48 us  [on_device(): other = lax.ppermute(group_total, ('seq', 'chan'), pairs)]
    dot_general x4 -> x5, matrix products: 2.11 us -> 2.47 us  [prefix_sum(): jnp.einsum('mcs,st->mct', upper, tri, preferred_element_type=jnp.float32)]
    dot_general x4 -> x5, matrix products: 4.65 us -> 4.69 us  [prefix_sum(): jnp.einsum('mcs,st->mct', lower, tri, preferred_element_type=jnp.float32)]
  transfers between devices with their start and end apart: 5 -> 5, of which waited for: 3 -> 3; matrix products, arithmetic and copies ran while one was open for 25% -> 28% of each run, Pallas kernels for 0% -> 0%
where the time goes in v8:
time: 28.2 us; the launch traced here: 28.1 us
  starting transfers between devices  9.96 us (35%)
  other arithmetic  8.23 us (29%)
  matrix products  7.16 us (25%)
  waiting for transfers between devices  1.48 us (5%)
  between operations  0.9 us (3%)
  local copies, waits for them, and re-layouts  0.33 us (1%)
    ppermute x5, starting transfers between devices, on_device(): other = lax.ppermute(group_total, ('seq', 'chan'), pairs)  9.96 us
    dot_general x5, matrix products, prefix_sum(): jnp.einsum('mcs,st->mct', lower, tri, preferred_element_type=jnp.float32)  4.69 us
    reduce_sum x1, other arithmetic, on_device(): carry_part = jnp.sum(carry_coef[:, :, None] * falling, axis=0)  2.5 us
    reduce_sum x1, other arithmetic, on_device(): block_state = jnp.sum(to_end * driven[None, :, :], axis=2)  2.47 us
    dot_general x5, matrix products, prefix_sum(): jnp.einsum('mcs,st->mct', upper, tri, preferred_element_type=jnp.float32)  2.47 us
    ppermute x5, waiting for transfers between devices, on_device(): other = lax.ppermute(group_total, ('seq', 'chan'), pairs)  1.48 us
    convert_element_type x1, other arithmetic, on_device(): (inner_gate.astype(jnp.float32) * signal.astype(jnp.float32)).astype(jnp....  1.1 us
    convert_element_type x1, other arithmetic, on_device(): (outer_gate.astype(jnp.float32) * convolved).astype(jnp.bfloat16)  0.79 us
  transfers between devices with their start and end apart: 5, of which 3 were waited for; matrix products, arithmetic and copies ran while one was open for 28% of the time, Pallas kernels for 0%

profile of v8, /device:TPU:0, one launch (start us, length us, event | category | flops | bytes accessed | tf_op | source)
XLA Modules:
  0.0 28.1 jit_solution(3565183398823243930)
XLA Ops:
  0.6 1.1 %multiply_convert_fusion.1 = bf16[512,256]{1,0:T(8,128)(2,1)S(1)} fusion(bf16[512,256]{1,0:T(8,128)(2,1)} %param.6, bf16[512,256]{1,0:T(8,128)(2,1)} %param.7), kind=kLoop, calls=%fused_computation.48 | loop fusion | flops 524288 | bytes 786432 | tf_op jit(solution)/shard_map/convert_element_type | solution.py:36
  1.9 2.5 %multiply_reduce_fusion.1 = f32[16,512]{1,0:T(8,128)S(1)} fusion(f32[512,256]{1,0:T(8,128)S(1)} %convert_element_type.85, f32[256]{0:T(256)S(1)} %iota_subtract_fusion, f32[16,512]{1,0:T(8,128)S(1)} %bitcast_negate_fusion), kind=kLoop, calls=%fused_computation.1 | loop fusion | flops 6283264 | bytes 590848 | tf_op jit(solution)/shard_map/reduce_sum | solution.py:42
  4.4 3.1 %collective-permute-start = (f32[16,512]{1,0:T(8,128)S(1)}, f32[16,512]{1,0:T(8,128)S(1)}, u32[]{:S(2)}, u32[]{:S(2)}) collective-permute-start(f32[16,512]{1,0:T(8,128)S(1)} %multiply_reduce_fusion.1), channel_id=1, source_target_pairs={{0,1},{1,0},{2,3},{3,2},{4,5},{5,4},{6,7},{7,6},{8,9},{9,8},{10,11... | collective-permute-start | bytes 98312 | tf_op jit(solution)/shard_map/ppermute | solution.py:57
  7.6 0.5 %fusion.5 = f32[16,104,256]{2,1,0:T(8,128)S(1)} fusion(f32[104,256]{1,0:T(8,128)S(1)} %get-tuple-element.28, f32[16,104]{1,0:T(8,128)S(1)} %get-tuple-element.78), kind=kOutput, calls=%fused_computation.22 | convolution fusion | flops 219447296 | bytes 1817088 | tf_op jit(solution)/shard_map/mcs,st->mct/dot_general | solution.py:15
  8.1 1.0 %multiply_reduce_fusion.5 = f32[104,256]{1,0:T(8,128)S(1)} fusion(f32[16,104,256]{2,1,0:T(8,128)S(1)} %fusion.5, f32[104,256]{1,0:T(8,128)S(1)} %get-tuple-element.28, f32[16,104]{1,0:T(8,128)S(1)} %get-tuple-element.78, f32[16,104]{1,0:T(8,128)S(1)} %get-tuple-element.73, f32[16,104]{1,0:T(8,128)S(1)} %get-tuple-element.84), kind=kOutput, calls=%fused_computation.14 | convolution fusion | flops 222828544 | bytes 1936896 | tf_op jit(solution)/shard_map/mcs,st->mct/dot_general | solution.py:16
  9.1 0.1 multiply_add_fusion.3
  9.5 3.0 %collective-permute-start.1 = (f32[16,512]{1,0:T(8,128)S(1)}, f32[16,512]{1,0:T(8,128)S(1)}, u32[]{:S(2)}, u32[]{:S(2)}) collective-permute-start(f32[16,512]{1,0:T(8,128)S(1)} %get-tuple-element.31), channel_id=1, source_target_pairs={{0,2},{1,3},{2,0},{3,1},{4,6},{5,7},{6,4},{7,5},{8,10},{9,11},{10,... | collective-permute-start | bytes 98312 | tf_op jit(solution)/shard_map/ppermute | solution.py:57
  12.5 0.5 %fusion.7 = f32[16,104,256]{2,1,0:T(8,128)S(1)} fusion(f32[104,256]{1,0:T(8,128)S(1)} %get-tuple-element.33, f32[16,104]{1,0:T(8,128)S(1)} %get-tuple-element.77), kind=kOutput, calls=%fused_computation.23 | convolution fusion | flops 219447296 | bytes 1817088 | tf_op jit(solution)/shard_map/mcs,st->mct/dot_general | solution.py:15
  13.0 0.9 %multiply_reduce_fusion.4 = f32[104,256]{1,0:T(8,128)S(1)} fusion(f32[16,104,256]{2,1,0:T(8,128)S(1)} %fusion.7, f32[104,256]{1,0:T(8,128)S(1)} %get-tuple-element.33, f32[16,104]{1,0:T(8,128)S(1)} %get-tuple-element.77, f32[16,104]{1,0:T(8,128)S(1)} %get-tuple-element.74, f32[16,104]{1,0:T(8,128)S(1)} %get-tuple-element.85), kind=kOutput, calls=%fused_computation.10 | convolution fusion | flops 222828544 | bytes 1936896 | tf_op jit(solution)/shard_map/mcs,st->mct/dot_general | solution.py:16
  14.0 0.3 %collective-permute-done.1 = f32[16,512]{1,0:T(8,128)S(1)} collective-permute-done((f32[16,512]{1,0:T(8,128)S(1)}, f32[16,512]{1,0:T(8,128)S(1)}, u32[]{:S(2)}, u32[]{:S(2)}) %collective-permute-start.1) | collective-permute-done | bytes 32800 | tf_op jit(solution)/shard_map/ppermute | solution.py:57
  14.5 0.5 %fusion.9 = f32[16,104,256]{2,1,0:T(8,128)S(1)} fusion(f32[104,256]{1,0:T(8,128)S(1)} %get-tuple-element.38, f32[16,104]{1,0:T(8,128)S(1)} %get-tuple-element.76), kind=kOutput, calls=%fused_computation.24 | convolution fusion | flops 219447296 | bytes 1817088 | tf_op jit(solution)/shard_map/mcs,st->mct/dot_general | solution.py:15
  15.0 0.9 %multiply_reduce_fusion.3 = f32[104,256]{1,0:T(8,128)S(1)} fusion(f32[16,104,256]{2,1,0:T(8,128)S(1)} %fusion.9, f32[104,256]{1,0:T(8,128)S(1)} %get-tuple-element.38, f32[16,104]{1,0:T(8,128)S(1)} %get-tuple-element.76, f32[16,104]{1,0:T(8,128)S(1)} %get-tuple-element.75, f32[16,104]{1,0:T(8,128)S(1)} %get-tuple-element.86), kind=kOutput, calls=%fused_computation.6 | convolution fusion | flops 222828544 | bytes 1936896 | tf_op jit(solution)/shard_map/mcs,st->mct/dot_general | solution.py:16
  15.9 0.1 multiply_add_fusion.1
  16.1 1.9 %collective-permute-start.3 = (f32[16,512]{1,0:T(8,128)S(1)}, f32[16,512]{1,0:T(8,128)S(1)}, u32[]{:S(2)}, u32[]{:S(2)}) collective-permute-start(f32[16,512]{1,0:T(8,128)S(1)} %get-tuple-element.41), channel_id=1, source_target_pairs={{0,8},{1,9},{2,10},{3,11},{4,12},{5,13},{6,14},{7,15},{8,0},{9,1},... | collective-permute-start | bytes 98312 | tf_op jit(solution)/shard_map/ppermute | solution.py:57
  18.0 0.5 %fusion.11 = f32[16,104,256]{2,1,0:T(8,128)S(1)} fusion(f32[104,256]{1,0:T(8,128)S(1)} %get-tuple-element.43, f32[16,104]{1,0:T(8,128)S(1)} %get-tuple-element.79), kind=kOutput, calls=%fused_computation.25 | convolution fusion | flops 219447296 | bytes 1817088 | tf_op jit(solution)/shard_map/mcs,st->mct/dot_general | solution.py:15
  18.5 1.0 %multiply_reduce_fusion.2 = f32[104,256]{1,0:T(8,128)S(1)} fusion(f32[16,104,256]{2,1,0:T(8,128)S(1)} %fusion.11, f32[104,256]{1,0:T(8,128)S(1)} %get-tuple-element.43, f32[16,104]{1,0:T(8,128)S(1)} %get-tuple-element.79, f32[16,104]{1,0:T(8,128)S(1)} %get-tuple-element.72, f32[16,104]{1,0:T(8,128)S(1)} %get-tuple-element.87), kind=kOutput, calls=%fused_computation.2 | convolution fusion | flops 222828544 | bytes 1936896 | tf_op jit(solution)/shard_map/mcs,st->mct/dot_general | solution.py:16
  19.6 0.5 %collective-permute-done.3 = f32[16,512]{1,0:T(8,128)S(1)} collective-permute-done((f32[16,512]{1,0:T(8,128)S(1)}, f32[16,512]{1,0:T(8,128)S(1)}, u32[]{:S(2)}, u32[]{:S(2)}) %collective-permute-start.3) | collective-permute-done | bytes 32800 | tf_op jit(solution)/shard_map/ppermute | solution.py:57
  20.1 1.9 %collective-permute-start.4 = (f32[16,512]{1,0:T(8,128)S(1)}, f32[16,512]{1,0:T(8,128)S(1)}, u32[]{:S(2)}, u32[]{:S(2)}) collective-permute-start(f32[16,512]{1,0:T(8,128)S(1)} %get-tuple-element.46), channel_id=1, source_target_pairs={{0,16},{1,17},{2,18},{3,19},{4,20},{5,21},{6,22},{7,23},{8,24},{9,... | collective-permute-start | bytes 98312 | tf_op jit(solution)/shard_map/ppermute | solution.py:57
  22.0 0.4 %fusion.13 = f32[16,96,256]{2,1,0:T(8,128)S(1)} fusion(f32[96,256]{1,0:T(8,128)S(1)} %slice.92, f32[16,96]{1,0:T(8,128)S(1)} %get-tuple-element.67), kind=kOutput, calls=%fused_computation.26 | convolution fusion | flops 202571776 | bytes 1677312 | tf_op jit(solution)/shard_map/mcs,st->mct/dot_general | solution.py:15
  22.4 0.9 %multiply_reduce_fusion.6 = f32[96,256]{1,0:T(8,128)S(1)} fusion(f32[16,96,256]{2,1,0:T(8,128)S(1)} %fusion.13, f32[96,256]{1,0:T(8,128)S(1)} %slice.92, f32[16,96]{1,0:T(8,128)S(1)} %get-tuple-element.67, f32[16,96]{1,0:T(8,128)S(1)} %get-tuple-element.66, f32[16,96]{1,0:T(8,128)S(1)} %slice.93), kind=kOutput, calls=%fused_computation.18 | convolution fusion | flops 205692928 | bytes 1787904 | tf_op jit(solution)/shard_map/mcs,st->mct/dot_general | solution.py:16
  23.4 0.6 %collective-permute-done.4 = f32[16,512]{1,0:T(8,128)S(1)} collective-permute-done((f32[16,512]{1,0:T(8,128)S(1)}, f32[16,512]{1,0:T(8,128)S(1)}, u32[]{:S(2)}, u32[]{:S(2)}) %collective-permute-start.4) | collective-permute-done | bytes 32800 | tf_op jit(solution)/shard_map/ppermute | solution.py:57
  24.1 2.5 %multiply_reduce_fusion = f32[512,256]{1,0:T(8,128)S(1)} fusion(f32[16,512]{1,0:T(8,128)S(1)} %multiply_multiply_fusion, f32[16,512]{1,0:T(8,128)S(1)} %bitcast_negate_fusion), kind=kLoop, calls=%fused_computation | loop fusion | flops 6160384 | bytes 589824 | tf_op jit(solution)/shard_map/reduce_sum | solution.py:74
  26.6 0.6 %bitcast_multiply_fusion = f32[512,16]{0,1:T(8,128)} fusion(f32[512,16]{0,1:T(8,128)S(1)} %copy-done.1, f32[16,512]{1,0:T(8,128)S(1)} %get-tuple-element.51), kind=kLoop, calls=%fused_computation.60 | loop fusion | flops 8192 | bytes 98304 | tf_op jit(solution)/shard_map/mul | solution.py:71
  27.3 0.8 %multiply_convert_fusion = bf16[512,256]{1,0:T(8,128)(2,1)} fusion(f32[512,256]{1,0:T(8,128)S(1)} %constant_dynamic-update-slice_fusion, f32[512,256]{1,0:T(8,128)S(1)} %multiply_reduce_fusion, bf16[512,256]{1,0:T(8,128)(2,1)S(1)} %copy-done.2), kind=kLoop, calls=%fused_computation.47 | loop fusion | flops 524288 | bytes 1572864 | tf_op jit(solution)/shard_map/convert_element_type | solution.py:76
  (35 shorter events, 1.0 us)
Async XLA Ops:
  0.6 1.2 %copy-start = (f32[512,16]{0,1:T(8,128)S(1)}, f32[512,16]{0,1:T(8,128)}, u32[]{:S(2)}) copy-start(f32[512,16]{0,1:T(8,128)} %param.9) | copy-start | bytes 98308
  1.9 5.6 %copy-start.3 = (f32[512]{0:T(512)S(1)}, f32[512]{0:T(512)}, u32[]{:S(2)}) copy-start(f32[512]{0:T(512)} %param.11) | copy-start | bytes 6148
  1.9 5.7 %copy-start.1 = (f32[512,16]{0,1:T(8,128)S(1)}, f32[512,16]{0,1:T(8,128)}, u32[]{:S(2)}) copy-start(f32[512,16]{0,1:T(8,128)} %param.10) | copy-start | bytes 98308
  4.4 5.1 %collective-permute-start = (f32[16,512]{1,0:T(8,128)S(1)}, f32[16,512]{1,0:T(8,128)S(1)}, u32[]{:S(2)}, u32[]{:S(2)}) collective-permute-start(f32[16,512]{1,0:T(8,128)S(1)} %multiply_reduce_fusion.1), channel_id=1, source_target_pairs={{0,1},{1,0},{2,3},{3,2},{4,5},{5,4},{6,7},{7,6},{8,9},{9,8},{10,11... | collective-permute-start | bytes 98312 | tf_op jit(solution)/shard_map/ppermute | solution.py:57
  9.5 4.9 %collective-permute-start.1 = (f32[16,512]{1,0:T(8,128)S(1)}, f32[16,512]{1,0:T(8,128)S(1)}, u32[]{:S(2)}, u32[]{:S(2)}) collective-permute-start(f32[16,512]{1,0:T(8,128)S(1)} %get-tuple-element.31), channel_id=1, source_target_pairs={{0,2},{1,3},{2,0},{3,1},{4,6},{5,7},{6,4},{7,5},{8,10},{9,11},{10,... | collective-permute-start | bytes 98312 | tf_op jit(solution)/shard_map/ppermute | solution.py:57
  14.4 1.6 %collective-permute-start.2 = (f32[16,512]{1,0:T(8,128)S(1)}, f32[16,512]{1,0:T(8,128)S(1)}, u32[]{:S(2)}, u32[]{:S(2)}) collective-permute-start(f32[16,512]{1,0:T(8,128)S(1)} %get-tuple-element.36), channel_id=1, source_target_pairs={{0,4},{1,5},{2,6},{3,7},{4,0},{5,1},{6,2},{7,3},{8,12},{9,13},{10,... | collective-permute-start | bytes 98312 | tf_op jit(solution)/shard_map/ppermute | solution.py:57
  16.1 4.0 %collective-permute-start.3 = (f32[16,512]{1,0:T(8,128)S(1)}, f32[16,512]{1,0:T(8,128)S(1)}, u32[]{:S(2)}, u32[]{:S(2)}) collective-permute-start(f32[16,512]{1,0:T(8,128)S(1)} %get-tuple-element.41), channel_id=1, source_target_pairs={{0,8},{1,9},{2,10},{3,11},{4,12},{5,13},{6,14},{7,15},{8,0},{9,1},... | collective-permute-start | bytes 98312 | tf_op jit(solution)/shard_map/ppermute | solution.py:57
  20.1 4.0 %collective-permute-start.4 = (f32[16,512]{1,0:T(8,128)S(1)}, f32[16,512]{1,0:T(8,128)S(1)}, u32[]{:S(2)}, u32[]{:S(2)}) collective-permute-start(f32[16,512]{1,0:T(8,128)S(1)} %get-tuple-element.46), channel_id=1, source_target_pairs={{0,16},{1,17},{2,18},{3,19},{4,20},{5,21},{6,22},{7,23},{8,24},{9,... | collective-permute-start | bytes 98312 | tf_op jit(solution)/shard_map/ppermute | solution.py:57
  24.1 3.2 %copy-start.2 = (bf16[512,256]{1,0:T(8,128)(2,1)S(1)}, bf16[512,256]{1,0:T(8,128)(2,1)}, u32[]{:S(2)}) copy-start(bf16[512,256]{1,0:T(8,128)(2,1)} %param.8) | copy-start | bytes 786436

commit v9 on v7

--- a/solution.py
+++ b/solution.py
@@ -17,6 +17,11 @@
     return first + second
 
 
+def gate(signal, inner_gate):
+    product = inner_gate.astype(jnp.float32) * signal.astype(jnp.float32)
+    return lax.reduce_precision(product, exponent_bits=8, mantissa_bits=7)
+
+
 def local_chunk(driven, rate_t, residue_t, skip_gain):
     tok_block = driven.shape[1]
     offsets = jnp.arange(tok_block, dtype=jnp.float32)
@@ -33,8 +38,7 @@
     chan_count = lax.axis_size("chan")
     blocks = seq_count * chan_count
     owner_idx = lax.axis_index("seq") * chan_count + lax.axis_index("chan")
-    gated_in = (inner_gate.astype(jnp.float32) * signal.astype(jnp.float32)).astype(jnp.bfloat16)
-    driven = gated_in.astype(jnp.float32)
+    driven = gate(signal, inner_gate)
     rate_t = decay_rate.T
     residue_t = residue.T
     offsets = jnp.arange(tok_block, dtype=jnp.float32)
@@ -52,7 +56,10 @@
         width = 1 << level
         if level < pieces:
             lo = level * piece
-            group_total, chunk_in = lax.optimization_barrier((group_total, driven[lo:lo + piece]))
+            group_total, sig_in, inner_in = lax.optimization_barrier(
+                (group_total, signal[lo:lo + piece], inner_gate[lo:lo + piece])
+            )
+            chunk_in = gate(sig_in, inner_in)
         pairs = [(src_i, src_i ^ width) for src_i in range(blocks)]
         other = lax.ppermute(group_total, ("seq", "chan"), pairs)
         if level < pieces:

time: 28.4 us -> 29.6 us (1.042)
  local copies, waits for them, and re-layouts: 0.06 us -> 1.13 us
    reduce_precision x0 -> x5, other arithmetic: none -> 1.19 us  [gate(): return lax.reduce_precision(product, exponent_bits=8, mantissa_bits=7)]
    convert_element_type x1 -> x0, other arithmetic: 1.09 us -> none  [on_device(): driven = gated_in.astype(jnp.float32)]
    slice x1, local copies, waits for them, and re-layouts: 0.04 us -> 1.1 us  [on_device(): inner_gate[lo:lo + piece]]
where the time goes in v9:
time: 29.6 us; the launch traced here: 29.4 us
  starting transfers between devices  10 us (34%)
  other arithmetic  8.08 us (27%)
  matrix products  6.76 us (23%)
  waiting for transfers between devices  2.48 us (8%)
  local copies, waits for them, and re-layouts  1.13 us (4%)
  between operations  0.9 us (3%)
    ppermute x5, starting transfers between devices, on_device(): other = lax.ppermute(group_total, ('seq', 'chan'), pairs)  10 us
    dot_general x4, matrix products, prefix_sum(): jnp.einsum('mcs,st->mct', lower, tri, preferred_element_type=jnp.float32)  4.65 us
    reduce_sum x1, other arithmetic, on_device(): carry_part = jnp.sum(carry_coef[:, :, None] * falling, axis=0)  2.5 us
    ppermute x5, waiting for transfers between devices, on_device(): other = lax.ppermute(group_total, ('seq', 'chan'), pairs)  2.48 us
    reduce_sum x1, other arithmetic, on_device(): block_state = jnp.sum(to_end * driven[None, :, :], axis=2)  2.47 us
    dot_general x4, matrix products, prefix_sum(): jnp.einsum('mcs,st->mct', upper, tri, preferred_element_type=jnp.float32)  2.11 us
    reduce_precision x5, other arithmetic, gate(): return lax.reduce_precision(product, exponent_bits=8, mantissa_bits=7)  1.19 us
    slice x1, local copies, waits for them, and re-layouts, on_device(): inner_gate[lo:lo + piece]  1.1 us
  transfers between devices with their start and end apart: 5, of which 3 were waited for; matrix products, arithmetic and copies ran while one was open for 25% of the time, Pallas kernels for 0%

profile of v9, /device:TPU:0, one launch (start us, length us, event | category | flops | bytes accessed | tf_op | source)
XLA Modules:
  0.0 29.4 jit_solution(1586392959364046854)
XLA Ops:
  0.6 1.1 %fusion.40 = (bf16[128,256]{1,0:T(8,128)(2,1)S(1)}, bf16[128,256]{1,0:T(8,128)(2,1)S(1)}, bf16[128,256]{1,0:T(8,128)(2,1)S(1)}, bf16[128,256]{1,0:T(8,128)(2,1)S...) fusion(bf16[512,256]{1,0:T(8,128)(2,1)} %param.7, ...), kind=kLoop, calls=%fused_computation.70 | loop fusion | bytes 1048576 | tf_op jit(solution)/shard_map/slice | solution.py:60
  1.7 1.1 %multiply_reduce-precision_fusion = f32[512,256]{1,0:T(8,128)S(1)} fusion(bf16[512,256]{1,0:T(8,128)(2,1)} %param.6, bf16[512,256]{1,0:T(8,128)(2,1)} %param.7), kind=kLoop, calls=%fused_computation.41 | loop fusion | flops 524288 | bytes 1048576 | tf_op jit(solution)/shard_map/reduce_precision | solution.py:22
  2.9 2.5 %multiply_reduce_fusion.1 = f32[16,512]{1,0:T(8,128)S(1)} fusion(f32[512,256]{1,0:T(8,128)S(1)} %multiply_reduce-precision_fusion, f32[256]{0:T(256)S(1)} %iota_subtract_fusion, f32[16,512]{1,0:T(8,128)S(1)} %bitcast_negate_fusion), kind=kLoop, calls=%fused_computation.1 | loop fusion | flops 6283264 | bytes 590848 | tf_op jit(solution)/shard_map/reduce_sum | solution.py:46
  5.4 3.1 %collective-permute-start = (f32[16,512]{1,0:T(8,128)S(1)}, f32[16,512]{1,0:T(8,128)S(1)}, u32[]{:S(2)}, u32[]{:S(2)}) collective-permute-start(f32[16,512]{1,0:T(8,128)S(1)} %multiply_reduce_fusion.1), channel_id=1, source_target_pairs={{0,1},{1,0},{2,3},{3,2},{4,5},{5,4},{6,7},{7,6},{8,9},{9,8},{10,11... | collective-permute-start | bytes 98312 | tf_op jit(solution)/shard_map/ppermute | solution.py:64
  8.5 0.5 %fusion.4 = f32[16,128,256]{2,1,0:T(8,128)S(1)} fusion(f32[128,256]{1,0:T(8,128)S(1)} %multiply_reduce-precision_fusion.4, f32[16,128]{1,0:T(8,128)S(1)} %get-tuple-element.75), kind=kOutput, calls=%fused_computation.18 | convolution fusion | flops 270073856 | bytes 2236416 | tf_op jit(solution)/shard_map/mcs,st->mct/dot_general | solution.py:15
  9.1 1.2 %multiply_reduce_fusion.5 = f32[128,256]{1,0:T(8,128)S(1)} fusion(f32[16,128,256]{2,1,0:T(8,128)S(1)} %fusion.4, f32[128,256]{1,0:T(8,128)S(1)} %multiply_reduce-precision_fusion.4, f32[16,128]{1,0:T(8,128)S(1)} %get-tuple-element.75, f32[16,128]{1,0:T(8,128)S(1)} %get-tuple-element.71, f32[16,128]{1,0:T(8,128)S(1)} %get-tuple-element.86), kind=kOutput, calls=%fused_computation.14 | convolution fusion | flops 274235392 | bytes 2383872 | tf_op jit(solution)/shard_map/mcs,st->mct/dot_general | solution.py:16
  10.3 0.1 multiply_add_fusion.3
  10.5 3.0 %collective-permute-start.1 = (f32[16,512]{1,0:T(8,128)S(1)}, f32[16,512]{1,0:T(8,128)S(1)}, u32[]{:S(2)}, u32[]{:S(2)}) collective-permute-start(f32[16,512]{1,0:T(8,128)S(1)} %get-tuple-element.31), channel_id=1, source_target_pairs={{0,2},{1,3},{2,0},{3,1},{4,6},{5,7},{6,4},{7,5},{8,10},{9,11},{10,... | collective-permute-start | bytes 98312 | tf_op jit(solution)/shard_map/ppermute | solution.py:64
  13.5 0.5 %fusion.6 = f32[16,128,256]{2,1,0:T(8,128)S(1)} fusion(f32[128,256]{1,0:T(8,128)S(1)} %multiply_reduce-precision_fusion.3, f32[16,128]{1,0:T(8,128)S(1)} %get-tuple-element.74), kind=kOutput, calls=%fused_computation.19 | convolution fusion | flops 270073856 | bytes 2236416 | tf_op jit(solution)/shard_map/mcs,st->mct/dot_general | solution.py:15
  14.0 1.1 %multiply_reduce_fusion.4 = f32[128,256]{1,0:T(8,128)S(1)} fusion(f32[16,128,256]{2,1,0:T(8,128)S(1)} %fusion.6, f32[128,256]{1,0:T(8,128)S(1)} %multiply_reduce-precision_fusion.3, f32[16,128]{1,0:T(8,128)S(1)} %get-tuple-element.74, f32[16,128]{1,0:T(8,128)S(1)} %get-tuple-element.72, f32[16,128]{1,0:T(8,128)S(1)} %get-tuple-element.87), kind=kOutput, calls=%fused_computation.10 | convolution fusion | flops 274235392 | bytes 2383872 | tf_op jit(solution)/shard_map/mcs,st->mct/dot_general | solution.py:16
  15.2 0.1 multiply_add_fusion.2
  15.3 0.1 collective-permute-done.1
  15.5 0.5 %fusion.8 = f32[16,128,256]{2,1,0:T(8,128)S(1)} fusion(f32[128,256]{1,0:T(8,128)S(1)} %multiply_reduce-precision_fusion.2, f32[16,128]{1,0:T(8,128)S(1)} %get-tuple-element.77), kind=kOutput, calls=%fused_computation.20 | convolution fusion | flops 270073856 | bytes 2236416 | tf_op jit(solution)/shard_map/mcs,st->mct/dot_general | solution.py:15
  16.1 1.2 %multiply_reduce_fusion.3 = f32[128,256]{1,0:T(8,128)S(1)} fusion(f32[16,128,256]{2,1,0:T(8,128)S(1)} %fusion.8, f32[128,256]{1,0:T(8,128)S(1)} %multiply_reduce-precision_fusion.2, f32[16,128]{1,0:T(8,128)S(1)} %get-tuple-element.77, f32[16,128]{1,0:T(8,128)S(1)} %get-tuple-element.73, f32[16,128]{1,0:T(8,128)S(1)} %get-tuple-element.88), kind=kOutput, calls=%fused_computation.6 | convolution fusion | flops 274235392 | bytes 2383872 | tf_op jit(solution)/shard_map/mcs,st->mct/dot_general | solution.py:16
  17.3 0.1 multiply_add_fusion.1
  17.4 1.9 %collective-permute-start.3 = (f32[16,512]{1,0:T(8,128)S(1)}, f32[16,512]{1,0:T(8,128)S(1)}, u32[]{:S(2)}, u32[]{:S(2)}) collective-permute-start(f32[16,512]{1,0:T(8,128)S(1)} %get-tuple-element.43), channel_id=1, source_target_pairs={{0,8},{1,9},{2,10},{3,11},{4,12},{5,13},{6,14},{7,15},{8,0},{9,1},... | collective-permute-start | bytes 98312 | tf_op jit(solution)/shard_map/ppermute | solution.py:64
  19.3 0.5 %fusion.10 = f32[16,128,256]{2,1,0:T(8,128)S(1)} fusion(f32[128,256]{1,0:T(8,128)S(1)} %multiply_reduce-precision_fusion.1, f32[16,128]{1,0:T(8,128)S(1)} %get-tuple-element.76), kind=kOutput, calls=%fused_computation.21 | convolution fusion | flops 270073856 | bytes 2236416 | tf_op jit(solution)/shard_map/mcs,st->mct/dot_general | solution.py:15
  19.8 1.1 %multiply_reduce_fusion.2 = f32[128,256]{1,0:T(8,128)S(1)} fusion(f32[16,128,256]{2,1,0:T(8,128)S(1)} %fusion.10, f32[128,256]{1,0:T(8,128)S(1)} %multiply_reduce-precision_fusion.1, f32[16,128]{1,0:T(8,128)S(1)} %get-tuple-element.76, f32[16,128]{1,0:T(8,128)S(1)} %get-tuple-element.70, f32[16,128]{1,0:T(8,128)S(1)} %get-tuple-element.89), kind=kOutput, calls=%fused_computation.2 | convolution fusion | flops 274235392 | bytes 2383872 | tf_op jit(solution)/shard_map/mcs,st->mct/dot_general | solution.py:16
  21.1 0.3 %collective-permute-done.3 = f32[16,512]{1,0:T(8,128)S(1)} collective-permute-done((f32[16,512]{1,0:T(8,128)S(1)}, f32[16,512]{1,0:T(8,128)S(1)}, u32[]{:S(2)}, u32[]{:S(2)}) %collective-permute-start.3) | collective-permute-done | bytes 32800 | tf_op jit(solution)/shard_map/ppermute | solution.py:64
  21.4 1.9 %collective-permute-start.4 = (f32[16,512]{1,0:T(8,128)S(1)}, f32[16,512]{1,0:T(8,128)S(1)}, u32[]{:S(2)}, u32[]{:S(2)}) collective-permute-start(f32[16,512]{1,0:T(8,128)S(1)} %get-tuple-element.49), channel_id=1, source_target_pairs={{0,16},{1,17},{2,18},{3,19},{4,20},{5,21},{6,22},{7,23},{8,24},{9,... | collective-permute-start | bytes 98312 | tf_op jit(solution)/shard_map/ppermute | solution.py:64
  23.3 2.1 %collective-permute-done.4 = f32[16,512]{1,0:T(8,128)S(1)} collective-permute-done((f32[16,512]{1,0:T(8,128)S(1)}, f32[16,512]{1,0:T(8,128)S(1)}, u32[]{:S(2)}, u32[]{:S(2)}) %collective-permute-start.4) | collective-permute-done | bytes 32800 | tf_op jit(solution)/shard_map/ppermute | solution.py:64
  25.4 2.5 %multiply_reduce_fusion = f32[512,256]{1,0:T(8,128)S(1)} fusion(f32[16,512]{1,0:T(8,128)S(1)} %fusion.39, f32[16,512]{1,0:T(8,128)S(1)} %bitcast_negate_fusion), kind=kLoop, calls=%fused_computation | loop fusion | flops 6160384 | bytes 589824 | tf_op jit(solution)/shard_map/reduce_sum | solution.py:81
  27.9 0.8 %fusion.29 = bf16[512,256]{1,0:T(8,128)(2,1)} fusion(f32[512,256]{1,0:T(8,128)S(1)} %multiply_reduce_fusion, f32[128,256]{1,0:T(8,128)S(1)} %multiply_add_fusion, f32[128,256]{1,0:T(8,128)S(1)} %multiply_add_fusion.1, f32[128,256]{1,0:T(8,128)S(1)} %multiply_add_fusion.2, f32[128,256]{1,0:T(8,128)S(1)} %multiply_add_fusion.3, bf16[512,256]{1,0:T(8,128)(2,1)S(1)} %copy-done.2), kind=kLoop, calls=%fused_computation.40 | loop fusion | flops 917504 | bytes 1572864 | tf_op jit(solution)/shard_map/convert_element_type | solution.py:83
  28.7 0.6 %bitcast_multiply_fusion = f32[512,16]{0,1:T(8,128)} fusion(f32[512,16]{0,1:T(8,128)S(1)} %copy-done.1, f32[16,512]{1,0:T(8,128)S(1)} %collective-permute-done.4, f32[16,512]{1,0:T(8,128)S(1)} %get-tuple-element.49, pred[]{:T(512)S(6)} %ne.42, f32[512,16]{0,1:T(8,128)S(1)} %copy-done), kind=kLoop, calls=%fused_computation.57 | loop fusion | flops 65536 | bytes 163841 | tf_op jit(solution)/shard_map/mul | solution.py:78
  (25 shorter events, 0.4 us)
Async XLA Ops:
  0.6 2.2 %copy-start = (f32[512,16]{0,1:T(8,128)S(1)}, f32[512,16]{0,1:T(8,128)}, u32[]{:S(2)}) copy-start(f32[512,16]{0,1:T(8,128)} %param.9) | copy-start | bytes 98308
  2.9 5.6 %copy-start.3 = (f32[512]{0:T(512)S(1)}, f32[512]{0:T(512)}, u32[]{:S(2)}) copy-start(f32[512]{0:T(512)} %param.11) | copy-start | bytes 6148
  2.9 5.6 %copy-start.1 = (f32[512,16]{0,1:T(8,128)S(1)}, f32[512,16]{0,1:T(8,128)}, u32[]{:S(2)}) copy-start(f32[512,16]{0,1:T(8,128)} %param.10) | copy-start | bytes 98308
  5.4 5.0 %collective-permute-start = (f32[16,512]{1,0:T(8,128)S(1)}, f32[16,512]{1,0:T(8,128)S(1)}, u32[]{:S(2)}, u32[]{:S(2)}) collective-permute-start(f32[16,512]{1,0:T(8,128)S(1)} %multiply_reduce_fusion.1), channel_id=1, source_target_pairs={{0,1},{1,0},{2,3},{3,2},{4,5},{5,4},{6,7},{7,6},{8,9},{9,8},{10,11... | collective-permute-start | bytes 98312 | tf_op jit(solution)/shard_map/ppermute | solution.py:64
  10.5 4.9 %collective-permute-start.1 = (f32[16,512]{1,0:T(8,128)S(1)}, f32[16,512]{1,0:T(8,128)S(1)}, u32[]{:S(2)}, u32[]{:S(2)}) collective-permute-start(f32[16,512]{1,0:T(8,128)S(1)} %get-tuple-element.31), channel_id=1, source_target_pairs={{0,2},{1,3},{2,0},{3,1},{4,6},{5,7},{6,4},{7,5},{8,10},{9,11},{10,... | collective-permute-start | bytes 98312 | tf_op jit(solution)/shard_map/ppermute | solution.py:64
  15.4 1.9 %collective-permute-start.2 = (f32[16,512]{1,0:T(8,128)S(1)}, f32[16,512]{1,0:T(8,128)S(1)}, u32[]{:S(2)}, u32[]{:S(2)}) collective-permute-start(f32[16,512]{1,0:T(8,128)S(1)} %get-tuple-element.37), channel_id=1, source_target_pairs={{0,4},{1,5},{2,6},{3,7},{4,0},{5,1},{6,2},{7,3},{8,12},{9,13},{10,... | collective-permute-start | bytes 98312 | tf_op jit(solution)/shard_map/ppermute | solution.py:64
  17.4 4.0 %collective-permute-start.3 = (f32[16,512]{1,0:T(8,128)S(1)}, f32[16,512]{1,0:T(8,128)S(1)}, u32[]{:S(2)}, u32[]{:S(2)}) collective-permute-start(f32[16,512]{1,0:T(8,128)S(1)} %get-tuple-element.43), channel_id=1, source_target_pairs={{0,8},{1,9},{2,10},{3,11},{4,12},{5,13},{6,14},{7,15},{8,0},{9,1},... | collective-permute-start | bytes 98312 | tf_op jit(solution)/shard_map/ppermute | solution.py:64
  21.4 6.5 %copy-start.2 = (bf16[512,256]{1,0:T(8,128)(2,1)S(1)}, bf16[512,256]{1,0:T(8,128)(2,1)}, u32[]{:S(2)}) copy-start(bf16[512,256]{1,0:T(8,128)(2,1)} %param.8) | copy-start | bytes 786436
  21.4 4.0 %collective-permute-start.4 = (f32[16,512]{1,0:T(8,128)S(1)}, f32[16,512]{1,0:T(8,128)S(1)}, u32[]{:S(2)}, u32[]{:S(2)}) collective-permute-start(f32[16,512]{1,0:T(8,128)S(1)} %get-tuple-element.49), channel_id=1, source_target_pairs={{0,16},{1,17},{2,18},{3,19},{4,20},{5,21},{6,22},{7,23},{8,24},{9,... | collective-permute-start | bytes 98312 | tf_op jit(solution)/shard_map/ppermute | solution.py:64

commit v10 on v2

--- a/solution.py
+++ b/solution.py
@@ -15,6 +15,15 @@
     first = jnp.einsum("mcs,st->mct", upper, tri, preferred_element_type=jnp.float32)
     second = jnp.einsum("mcs,st->mct", lower, tri, preferred_element_type=jnp.float32)
     return first + second
+
+
+def power_table(rate_t, first, step):
+    modes, channels = rate_t.shape
+    coarse = jnp.arange(16, dtype=jnp.float32) * (16.0 * step)
+    fine = first + jnp.arange(16, dtype=jnp.float32) * step
+    high = jnp.exp(-rate_t[:, :, None] * coarse[None, None, :])
+    low = jnp.exp(-rate_t[:, :, None] * fine[None, None, :])
+    return (high[:, :, :, None] * low[:, :, None, :]).reshape(modes, channels, 256)
 
 
 def local_chunk(driven, rate_t, residue_t, skip_gain):
@@ -38,7 +47,7 @@
     rate_t = decay_rate.T
     residue_t = residue.T
     offsets = jnp.arange(tok_block, dtype=jnp.float32)
-    to_end = jnp.exp(-rate_t[:, :, None] * (tok_block - 1.0 - offsets)[None, None, :])
+    to_end = power_table(rate_t, tok_block - 1.0, -1.0)
     block_state = jnp.sum(to_end * driven[None, :, :], axis=2)
     rounds = blocks.bit_length() - 1
     assert 1 << rounds == blocks
@@ -69,7 +78,7 @@
             group_total, carry_in, chunk_out = lax.optimization_barrier((group_total, carry_in, chunk_out))
             direct.append(chunk_out)
     modal_state = residue * group_total.T
-    falling = jnp.exp(-rate_t[:, :, None] * offsets[None, None, :])
+    falling = power_table(rate_t, 0.0, 1.0)
     carry_coef = residue_t * jnp.exp(-rate_t) * carry_in
     carry_part = jnp.sum(carry_coef[:, :, None] * falling, axis=0)
     convolved = jnp.concatenate(direct, axis=0) + carry_part

time: 28.5 us -> 26.3 us (0.923)
  other arithmetic: 8.01 us -> 5.45 us
  local copies, waits for them, and re-layouts: 0.07 us -> 0.4 us
    reduce_sum x1, other arithmetic: 2.5 us -> 1.01 us  [on_device(): carry_part = jnp.sum(carry_coef[:, :, None] * falling, axis=0)]
    reduce_sum x1, other arithmetic: 2.47 us -> 1.09 us  [on_device(): block_state = jnp.sum(to_end * driven[None, :, :], axis=2)]
    exp x0 -> x1, other arithmetic: none -> 0.35 us  [power_table(): high = jnp.exp(-rate_t[:, :, None] * coarse[None, None, :])]
  transfers between devices with their start and end apart: 5 -> 5, of which waited for: 3 -> 4; matrix products, arithmetic and copies ran while one was open for 25% -> 27% of each run, Pallas kernels for 0% -> 0%
where the time goes in v10:
time: 26.3 us; the launch traced here: 26.1 us
  starting transfers between devices  10.1 us (38%)
  matrix products  6.7 us (25%)
  other arithmetic  5.45 us (21%)
  waiting for transfers between devices  2.58 us (10%)
  between operations  0.91 us (3%)
  local copies, waits for them, and re-layouts  0.4 us (2%)
    ppermute x5, starting transfers between devices, on_device(): other = lax.ppermute(group_total, ('seq', 'chan'), pairs)  10.1 us
    dot_general x4, matrix products, prefix_sum(): jnp.einsum('mcs,st->mct', lower, tri, preferred_element_type=jnp.float32)  4.58 us
    ppermute x5, waiting for transfers between devices, on_device(): other = lax.ppermute(group_total, ('seq', 'chan'), pairs)  2.58 us
    dot_general x4, matrix products, prefix_sum(): jnp.einsum('mcs,st->mct', upper, tri, preferred_element_type=jnp.float32)  2.11 us
    convert_element_type x1, other arithmetic, on_device(): (inner_gate.astype(jnp.float32) * signal.astype(jnp.float32)).astype(jnp....  1.1 us
    reduce_sum x1, other arithmetic, on_device(): block_state = jnp.sum(to_end * driven[None, :, :], axis=2)  1.09 us
    reduce_sum x1, other arithmetic, on_device(): carry_part = jnp.sum(carry_coef[:, :, None] * falling, axis=0)  1.01 us
    convert_element_type x1, other arithmetic, on_device(): (outer_gate.astype(jnp.float32) * convolved).astype(jnp.bfloat16)  0.79 us
  transfers between devices with their start and end apart: 5, of which 4 were waited for; matrix products, arithmetic and copies ran while one was open for 27% of the time, Pallas kernels for 0%

profile of v10, /device:TPU:0, one launch (start us, length us, event | category | flops | bytes accessed | tf_op | source)
XLA Modules:
  0.0 26.1 jit_solution(13553544889564557357)
XLA Ops:
  0.7 1.1 %multiply_convert_fusion = bf16[512,256]{1,0:T(8,128)(2,1)S(1)} fusion(bf16[512,256]{1,0:T(8,128)(2,1)} %param.6, bf16[512,256]{1,0:T(8,128)(2,1)} %param.7), kind=kLoop, calls=%fused_computation.43 | loop fusion | flops 524288 | bytes 786432 | tf_op jit(solution)/shard_map/convert_element_type | solution.py:45
  1.8 0.1 copy.20
  2.0 0.3 %multiply_exponential_fusion.3 = (f32[16,512,16]{1,2,0:T(8,128)S(1)}, f32[16,512,16]{1,2,0:T(8,128)S(1)}, f32[16,512,16]{1,2,0:T(8,128)S(1)}, f32[16,512,16]{1,2,0:T(8,128)S(1)}) fusion(f32[16]{0:T(128)S(1)} %iota_multiply_fusion.1, f32[16,512]{1,0:T(8,128)S(1)} %bitcast_negate_fusion, f32[16]{0:T(128)S(1)} %get-tuple-element.76, f32[16]{0:T(128)S(1)} %get-tuple-element.77), kind=kLoop, calls=%fused_computation.45 | loop fusion | flops 524288 | bytes 2130112 | tf_op jit(solution)/shard_map/exp | solution.py:24
  2.4 1.1 %multiply_reduce_fusion.1 = f32[16,512]{1,0:T(8,128)S(1)} fusion(f32[512,16,16]{0,2,1:T(8,128)S(1)} %bitcast.41, f32[16,512,16]{1,2,0:T(8,128)S(1)} %get-tuple-element.71, f32[16,512,16]{1,2,0:T(8,128)S(1)} %get-tuple-element.68), kind=kLoop, calls=%fused_computation.1 | loop fusion | flops 6283264 | bytes 1605632 | tf_op jit(solution)/shard_map/reduce_sum | solution.py:51
  3.5 3.1 %collective-permute-start = (f32[16,512]{1,0:T(8,128)S(1)}, f32[16,512]{1,0:T(8,128)S(1)}, u32[]{:S(2)}, u32[]{:S(2)}) collective-permute-start(f32[16,512]{1,0:T(8,128)S(1)} %multiply_reduce_fusion.1), channel_id=1, source_target_pairs={{0,1},{1,0},{2,3},{3,2},{4,5},{5,4},{6,7},{7,6},{8,9},{9,8},{10,11... | collective-permute-start | bytes 98312 | tf_op jit(solution)/shard_map/ppermute | solution.py:66
  6.6 0.5 %fusion.4 = f32[16,128,256]{2,1,0:T(8,128)S(1)} fusion(f32[128,256]{1,0:T(8,128)S(1)} %get-tuple-element.23, f32[16,128]{1,0:T(8,128)S(1)} %get-tuple-element.65), kind=kOutput, calls=%fused_computation.18 | convolution fusion | flops 270073856 | bytes 2236416 | tf_op jit(solution)/shard_map/mcs,st->mct/dot_general | solution.py:15
  7.1 1.1 %multiply_reduce_fusion.5 = f32[128,256]{1,0:T(8,128)S(1)} fusion(f32[16,128,256]{2,1,0:T(8,128)S(1)} %fusion.4, f32[128,256]{1,0:T(8,128)S(1)} %get-tuple-element.23, f32[16,128]{1,0:T(8,128)S(1)} %get-tuple-element.65, f32[16,128]{1,0:T(8,128)S(1)} %get-tuple-element.61, f32[16,128]{1,0:T(8,128)S(1)} %get-tuple-element.78), kind=kOutput, calls=%fused_computation.14 | convolution fusion | flops 274235392 | bytes 2383872 | tf_op jit(solution)/shard_map/mcs,st->mct/dot_general | solution.py:16
  8.5 3.1 %collective-permute-start.1 = (f32[16,512]{1,0:T(8,128)S(1)}, f32[16,512]{1,0:T(8,128)S(1)}, u32[]{:S(2)}, u32[]{:S(2)}) collective-permute-start(f32[16,512]{1,0:T(8,128)S(1)} %get-tuple-element.26), channel_id=1, source_target_pairs={{0,2},{1,3},{2,0},{3,1},{4,6},{5,7},{6,4},{7,5},{8,10},{9,11},{10,... | collective-permute-start | bytes 98312 | tf_op jit(solution)/shard_map/ppermute | solution.py:66
  11.6 0.5 %fusion.6 = f32[16,128,256]{2,1,0:T(8,128)S(1)} fusion(f32[128,256]{1,0:T(8,128)S(1)} %get-tuple-element.28, f32[16,128]{1,0:T(8,128)S(1)} %get-tuple-element.64), kind=kOutput, calls=%fused_computation.19 | convolution fusion | flops 270073856 | bytes 2236416 | tf_op jit(solution)/shard_map/mcs,st->mct/dot_general | solution.py:15
  12.1 1.1 %multiply_reduce_fusion.4 = f32[128,256]{1,0:T(8,128)S(1)} fusion(f32[16,128,256]{2,1,0:T(8,128)S(1)} %fusion.6, f32[128,256]{1,0:T(8,128)S(1)} %get-tuple-element.28, f32[16,128]{1,0:T(8,128)S(1)} %get-tuple-element.64, f32[16,128]{1,0:T(8,128)S(1)} %get-tuple-element.62, f32[16,128]{1,0:T(8,128)S(1)} %get-tuple-element.79), kind=kOutput, calls=%fused_computation.10 | convolution fusion | flops 274235392 | bytes 2383872 | tf_op jit(solution)/shard_map/mcs,st->mct/dot_general | solution.py:16
  13.3 0.1 collective-permute-done.1
  13.6 0.5 %fusion.8 = f32[16,128,256]{2,1,0:T(8,128)S(1)} fusion(f32[128,256]{1,0:T(8,128)S(1)} %get-tuple-element.33, f32[16,128]{1,0:T(8,128)S(1)} %get-tuple-element.67), kind=kOutput, calls=%fused_computation.20 | convolution fusion | flops 270073856 | bytes 2236416 | tf_op jit(solution)/shard_map/mcs,st->mct/dot_general | solution.py:15
  14.1 1.2 %multiply_reduce_fusion.3 = f32[128,256]{1,0:T(8,128)S(1)} fusion(f32[16,128,256]{2,1,0:T(8,128)S(1)} %fusion.8, f32[128,256]{1,0:T(8,128)S(1)} %get-tuple-element.33, f32[16,128]{1,0:T(8,128)S(1)} %get-tuple-element.67, f32[16,128]{1,0:T(8,128)S(1)} %get-tuple-element.63, f32[16,128]{1,0:T(8,128)S(1)} %get-tuple-element.80), kind=kOutput, calls=%fused_computation.6 | convolution fusion | flops 274235392 | bytes 2383872 | tf_op jit(solution)/shard_map/mcs,st->mct/dot_general | solution.py:16
  15.3 0.1 multiply_add_fusion.1
  15.4 1.9 %collective-permute-start.3 = (f32[16,512]{1,0:T(8,128)S(1)}, f32[16,512]{1,0:T(8,128)S(1)}, u32[]{:S(2)}, u32[]{:S(2)}) collective-permute-start(f32[16,512]{1,0:T(8,128)S(1)} %get-tuple-element.36), channel_id=1, source_target_pairs={{0,8},{1,9},{2,10},{3,11},{4,12},{5,13},{6,14},{7,15},{8,0},{9,1},... | collective-permute-start | bytes 98312 | tf_op jit(solution)/shard_map/ppermute | solution.py:66
  17.3 0.5 %fusion.10 = f32[16,128,256]{2,1,0:T(8,128)S(1)} fusion(f32[128,256]{1,0:T(8,128)S(1)} %get-tuple-element.38, f32[16,128]{1,0:T(8,128)S(1)} %get-tuple-element.66), kind=kOutput, calls=%fused_computation.21 | convolution fusion | flops 270073856 | bytes 2236416 | tf_op jit(solution)/shard_map/mcs,st->mct/dot_general | solution.py:15
  17.9 1.1 %multiply_reduce_fusion.2 = f32[128,256]{1,0:T(8,128)S(1)} fusion(f32[16,128,256]{2,1,0:T(8,128)S(1)} %fusion.10, f32[128,256]{1,0:T(8,128)S(1)} %get-tuple-element.38, f32[16,128]{1,0:T(8,128)S(1)} %get-tuple-element.66, f32[16,128]{1,0:T(8,128)S(1)} %get-tuple-element.60, f32[16,128]{1,0:T(8,128)S(1)} %get-tuple-element.81), kind=kOutput, calls=%fused_computation.2 | convolution fusion | flops 274235392 | bytes 2383872 | tf_op jit(solution)/shard_map/mcs,st->mct/dot_general | solution.py:16
  19.1 0.3 %collective-permute-done.3 = f32[16,512]{1,0:T(8,128)S(1)} collective-permute-done((f32[16,512]{1,0:T(8,128)S(1)}, f32[16,512]{1,0:T(8,128)S(1)}, u32[]{:S(2)}, u32[]{:S(2)}) %collective-permute-start.3) | collective-permute-done | bytes 32800 | tf_op jit(solution)/shard_map/ppermute | solution.py:66
  19.4 1.9 %collective-permute-start.4 = (f32[16,512]{1,0:T(8,128)S(1)}, f32[16,512]{1,0:T(8,128)S(1)}, u32[]{:S(2)}, u32[]{:S(2)}) collective-permute-start(f32[16,512]{1,0:T(8,128)S(1)} %get-tuple-element.41), channel_id=1, source_target_pairs={{0,16},{1,17},{2,18},{3,19},{4,20},{5,21},{6,22},{7,23},{8,24},{9,... | collective-permute-start | bytes 98312 | tf_op jit(solution)/shard_map/ppermute | solution.py:66
  21.4 2.1 %collective-permute-done.4 = f32[16,512]{1,0:T(8,128)S(1)} collective-permute-done((f32[16,512]{1,0:T(8,128)S(1)}, f32[16,512]{1,0:T(8,128)S(1)}, u32[]{:S(2)}, u32[]{:S(2)}) %collective-permute-start.4) | collective-permute-done | bytes 32800 | tf_op jit(solution)/shard_map/ppermute | solution.py:66
  23.4 1.0 %multiply_reduce_fusion = f32[512,16,16]{0,2,1:T(8,128)S(1)} fusion(f32[16,512,16]{1,2,0:T(8,128)S(1)} %get-tuple-element.70, f32[16,512,16]{1,2,0:T(8,128)S(1)} %get-tuple-element.69, f32[16,512]{1,0:T(8,128)S(1)} %fusion.39), kind=kLoop, calls=%fused_computation | loop fusion | flops 6160384 | bytes 1605632 | tf_op jit(solution)/shard_map/reduce_sum | solution.py:83
  24.5 0.2 copy.21
  24.7 0.8 %fusion.29 = bf16[512,256]{1,0:T(8,128)(2,1)} fusion(f32[512,256]{1,0:T(8,128)S(1)} %copy.21, f32[128,256]{1,0:T(8,128)S(1)} %multiply_add_fusion, f32[128,256]{1,0:T(8,128)S(1)} %multiply_add_fusion.1, f32[128,256]{1,0:T(8,128)S(1)} %multiply_add_fusion.2, f32[128,256]{1,0:T(8,128)S(1)} %multiply_add_fusion.3, bf16[512,256]{1,0:T(8,128)(2,1)S(1)} %copy-done.2), kind=kLoop, calls=%fused_computation.40 | loop fusion | flops 917504 | bytes 1572864 | tf_op jit(solution)/shard_map/convert_element_type | solution.py:85
  25.5 0.6 %bitcast_multiply_fusion = f32[512,16]{0,1:T(8,128)} fusion(f32[512,16]{0,1:T(8,128)S(1)} %copy-done.1, f32[16,512]{1,0:T(8,128)S(1)} %collective-permute-done.4, f32[16,512]{1,0:T(8,128)S(1)} %get-tuple-element.41, pred[]{:T(512)S(6)} %ne.42, f32[512,16]{0,1:T(8,128)S(1)} %copy-done), kind=kLoop, calls=%fused_computation.57 | loop fusion | flops 65536 | bytes 163841 | tf_op jit(solution)/shard_map/mul | solution.py:80
  (25 shorter events, 0.6 us)
Async XLA Ops:
  0.6 1.3 %copy-start = (f32[512,16]{0,1:T(8,128)S(1)}, f32[512,16]{0,1:T(8,128)}, u32[]{:S(2)}) copy-start(f32[512,16]{0,1:T(8,128)} %param.9) | copy-start | bytes 98308
  2.0 4.6 %copy-start.3 = (f32[512]{0:T(512)S(1)}, f32[512]{0:T(512)}, u32[]{:S(2)}) copy-start(f32[512]{0:T(512)} %param.11) | copy-start | bytes 6148
  2.0 4.6 %copy-start.1 = (f32[512,16]{0,1:T(8,128)S(1)}, f32[512,16]{0,1:T(8,128)}, u32[]{:S(2)}) copy-start(f32[512,16]{0,1:T(8,128)} %param.10) | copy-start | bytes 98308
  3.5 5.0 %collective-permute-start = (f32[16,512]{1,0:T(8,128)S(1)}, f32[16,512]{1,0:T(8,128)S(1)}, u32[]{:S(2)}, u32[]{:S(2)}) collective-permute-start(f32[16,512]{1,0:T(8,128)S(1)} %multiply_reduce_fusion.1), channel_id=1, source_target_pairs={{0,1},{1,0},{2,3},{3,2},{4,5},{5,4},{6,7},{7,6},{8,9},{9,8},{10,11... | collective-permute-start | bytes 98312 | tf_op jit(solution)/shard_map/ppermute | solution.py:66
  8.5 5.0 %collective-permute-start.1 = (f32[16,512]{1,0:T(8,128)S(1)}, f32[16,512]{1,0:T(8,128)S(1)}, u32[]{:S(2)}, u32[]{:S(2)}) collective-permute-start(f32[16,512]{1,0:T(8,128)S(1)} %get-tuple-element.26), channel_id=1, source_target_pairs={{0,2},{1,3},{2,0},{3,1},{4,6},{5,7},{6,4},{7,5},{8,10},{9,11},{10,... | collective-permute-start | bytes 98312 | tf_op jit(solution)/shard_map/ppermute | solution.py:66
  13.5 1.9 %collective-permute-start.2 = (f32[16,512]{1,0:T(8,128)S(1)}, f32[16,512]{1,0:T(8,128)S(1)}, u32[]{:S(2)}, u32[]{:S(2)}) collective-permute-start(f32[16,512]{1,0:T(8,128)S(1)} %get-tuple-element.31), channel_id=1, source_target_pairs={{0,4},{1,5},{2,6},{3,7},{4,0},{5,1},{6,2},{7,3},{8,12},{9,13},{10,... | collective-permute-start | bytes 98312 | tf_op jit(solution)/shard_map/ppermute | solution.py:66
  15.4 4.0 %collective-permute-start.3 = (f32[16,512]{1,0:T(8,128)S(1)}, f32[16,512]{1,0:T(8,128)S(1)}, u32[]{:S(2)}, u32[]{:S(2)}) collective-permute-start(f32[16,512]{1,0:T(8,128)S(1)} %get-tuple-element.36), channel_id=1, source_target_pairs={{0,8},{1,9},{2,10},{3,11},{4,12},{5,13},{6,14},{7,15},{8,0},{9,1},... | collective-permute-start | bytes 98312 | tf_op jit(solution)/shard_map/ppermute | solution.py:66
  19.0 5.7 %copy-start.2 = (bf16[512,256]{1,0:T(8,128)(2,1)S(1)}, bf16[512,256]{1,0:T(8,128)(2,1)}, u32[]{:S(2)}) copy-start(bf16[512,256]{1,0:T(8,128)(2,1)} %param.8) | copy-start | bytes 786436
  19.4 4.0 %collective-permute-start.4 = (f32[16,512]{1,0:T(8,128)S(1)}, f32[16,512]{1,0:T(8,128)S(1)}, u32[]{:S(2)}, u32[]{:S(2)}) collective-permute-start(f32[16,512]{1,0:T(8,128)S(1)} %get-tuple-element.41), channel_id=1, source_target_pairs={{0,16},{1,17},{2,18},{3,19},{4,20},{5,21},{6,22},{7,23},{8,24},{9,... | collective-permute-start | bytes 98312 | tf_op jit(solution)/shard_map/ppermute | solution.py:66

commit v11 on v10

--- a/solution.py
+++ b/solution.py
@@ -71,13 +71,19 @@
         upper = (owner_idx & width) != 0
         place = (owner_idx % width).astype(jnp.float32)
         carry_in = jnp.where(upper, carry_in + jnp.exp(-span_rate * place) * other, carry_in)
+        shrink = jnp.exp(-span_rate * width)
+        if level == rounds - 1:
+            own_w = residue_t * jnp.where(upper, 1.0, shrink)
+            other_w = residue_t * jnp.where(upper, shrink, 1.0)
+            own_part, other_w = lax.optimization_barrier((own_w * group_total, other_w))
+            modal_t = own_part + other_w * other
         later = jnp.where(upper, group_total, other)
         earlier = jnp.where(upper, other, group_total)
-        group_total = later + jnp.exp(-span_rate * width) * earlier
+        group_total = later + shrink * earlier
         if level < pieces:
             group_total, carry_in, chunk_out = lax.optimization_barrier((group_total, carry_in, chunk_out))
             direct.append(chunk_out)
-    modal_state = residue * group_total.T
+    modal_state = modal_t.T
     falling = power_table(rate_t, 0.0, 1.0)
     carry_coef = residue_t * jnp.exp(-rate_t) * carry_in
     carry_part = jnp.sum(carry_coef[:, :, None] * falling, axis=0)

time: 26.3 us -> 26.2 us (level)
    mul x2 -> x1, other arithmetic: 0.65 us -> 0.03 us  [on_device(): other_w = residue_t * jnp.where(upper, shrink, 1.0)]
    transpose x0 -> x1, other arithmetic: none -> 0.62 us  [on_device(): modal_state = modal_t.T]
  transfers between devices with their start and end apart: 5 -> 5, of which waited for: 4 -> 3; matrix products, arithmetic and copies ran while one was open for 27% -> 27% of each run, Pallas kernels for 0% -> 0%
where the time goes in v11:
time: 26.2 us; the launch traced here: 26.1 us
  starting transfers between devices  10 us (38%)
  matrix products  6.76 us (26%)
  other arithmetic  5.46 us (21%)
  waiting for transfers between devices  2.53 us (10%)
  between operations  0.92 us (4%)
  local copies, waits for them, and re-layouts  0.4 us (2%)
    ppermute x5, starting transfers between devices, on_device(): other = lax.ppermute(group_total, ('seq', 'chan'), pairs)  10 us
    dot_general x4, matrix products, prefix_sum(): jnp.einsum('mcs,st->mct', lower, tri, preferred_element_type=jnp.float32)  4.65 us
    ppermute x5, waiting for transfers between devices, on_device(): other = lax.ppermute(group_total, ('seq', 'chan'), pairs)  2.53 us
    dot_general x4, matrix products, prefix_sum(): jnp.einsum('mcs,st->mct', upper, tri, preferred_element_type=jnp.float32)  2.11 us
    convert_element_type x1, other arithmetic, on_device(): (inner_gate.astype(jnp.float32) * signal.astype(jnp.float32)).astype(jnp....  1.1 us
    reduce_sum x1, other arithmetic, on_device(): block_state = jnp.sum(to_end * driven[None, :, :], axis=2)  1.09 us
    reduce_sum x1, other arithmetic, on_device(): carry_part = jnp.sum(carry_coef[:, :, None] * falling, axis=0)  1.01 us
    convert_element_type x1, other arithmetic, on_device(): (outer_gate.astype(jnp.float32) * convolved).astype(jnp.bfloat16)  0.79 us
  transfers between devices with their start and end apart: 5, of which 3 were waited for; matrix products, arithmetic and copies ran while one was open for 27% of the time, Pallas kernels for 0%

profile of v11, /device:TPU:0, one launch (start us, length us, event | category | flops | bytes accessed | tf_op | source)
XLA Modules:
  0.0 26.1 jit_solution(16450170338679088359)
XLA Ops:
  0.7 1.1 %multiply_convert_fusion = bf16[512,256]{1,0:T(8,128)(2,1)S(1)} fusion(bf16[512,256]{1,0:T(8,128)(2,1)} %param.6, bf16[512,256]{1,0:T(8,128)(2,1)} %param.7), kind=kLoop, calls=%fused_computation.43 | loop fusion | flops 524288 | bytes 786432 | tf_op jit(solution)/shard_map/convert_element_type | solution.py:45
  1.8 0.1 copy.20
  2.0 0.3 %multiply_exponential_fusion.3 = (f32[16,512,16]{1,2,0:T(8,128)S(1)}, f32[16,512,16]{1,2,0:T(8,128)S(1)}, f32[16,512,16]{1,2,0:T(8,128)S(1)}, f32[16,512,16]{1,2,0:T(8,128)S(1)}) fusion(f32[16]{0:T(128)S(1)} %iota_multiply_fusion.1, f32[16,512]{1,0:T(8,128)S(1)} %bitcast_negate_fusion, f32[16]{0:T(128)S(1)} %get-tuple-element.83, f32[16]{0:T(128)S(1)} %get-tuple-element.84), kind=kLoop, calls=%fused_computation.45 | loop fusion | flops 524288 | bytes 2130112 | tf_op jit(solution)/shard_map/exp | solution.py:24
  2.4 1.1 %multiply_reduce_fusion.1 = f32[16,512]{1,0:T(8,128)S(1)} fusion(f32[512,16,16]{0,2,1:T(8,128)S(1)} %bitcast.45, f32[16,512,16]{1,2,0:T(8,128)S(1)} %get-tuple-element.78, f32[16,512,16]{1,2,0:T(8,128)S(1)} %get-tuple-element.75), kind=kLoop, calls=%fused_computation.1 | loop fusion | flops 6283264 | bytes 1605632 | tf_op jit(solution)/shard_map/reduce_sum | solution.py:51
  3.5 3.1 %collective-permute-start = (f32[16,512]{1,0:T(8,128)S(1)}, f32[16,512]{1,0:T(8,128)S(1)}, u32[]{:S(2)}, u32[]{:S(2)}) collective-permute-start(f32[16,512]{1,0:T(8,128)S(1)} %multiply_reduce_fusion.1), channel_id=1, source_target_pairs={{0,1},{1,0},{2,3},{3,2},{4,5},{5,4},{6,7},{7,6},{8,9},{9,8},{10,11... | collective-permute-start | bytes 98312 | tf_op jit(solution)/shard_map/ppermute | solution.py:66
  6.6 0.5 %fusion.4 = f32[16,128,256]{2,1,0:T(8,128)S(1)} fusion(f32[128,256]{1,0:T(8,128)S(1)} %get-tuple-element.25, f32[16,128]{1,0:T(8,128)S(1)} %get-tuple-element.72), kind=kOutput, calls=%fused_computation.18 | convolution fusion | flops 270073856 | bytes 2236416 | tf_op jit(solution)/shard_map/mcs,st->mct/dot_general | solution.py:15
  7.1 1.2 %multiply_reduce_fusion.5 = f32[128,256]{1,0:T(8,128)S(1)} fusion(f32[16,128,256]{2,1,0:T(8,128)S(1)} %fusion.4, f32[128,256]{1,0:T(8,128)S(1)} %get-tuple-element.25, f32[16,128]{1,0:T(8,128)S(1)} %get-tuple-element.72, f32[16,128]{1,0:T(8,128)S(1)} %get-tuple-element.68, f32[16,128]{1,0:T(8,128)S(1)} %get-tuple-element.85), kind=kOutput, calls=%fused_computation.14 | convolution fusion | flops 274235392 | bytes 2383872 | tf_op jit(solution)/shard_map/mcs,st->mct/dot_general | solution.py:16
  8.5 3.1 %collective-permute-start.1 = (f32[16,512]{1,0:T(8,128)S(1)}, f32[16,512]{1,0:T(8,128)S(1)}, u32[]{:S(2)}, u32[]{:S(2)}) collective-permute-start(f32[16,512]{1,0:T(8,128)S(1)} %get-tuple-element.28), channel_id=1, source_target_pairs={{0,2},{1,3},{2,0},{3,1},{4,6},{5,7},{6,4},{7,5},{8,10},{9,11},{10,... | collective-permute-start | bytes 98312 | tf_op jit(solution)/shard_map/ppermute | solution.py:66
  11.6 0.5 %fusion.6 = f32[16,128,256]{2,1,0:T(8,128)S(1)} fusion(f32[128,256]{1,0:T(8,128)S(1)} %get-tuple-element.30, f32[16,128]{1,0:T(8,128)S(1)} %get-tuple-element.71), kind=kOutput, calls=%fused_computation.19 | convolution fusion | flops 270073856 | bytes 2236416 | tf_op jit(solution)/shard_map/mcs,st->mct/dot_general | solution.py:15
  12.1 1.1 %multiply_reduce_fusion.4 = f32[128,256]{1,0:T(8,128)S(1)} fusion(f32[16,128,256]{2,1,0:T(8,128)S(1)} %fusion.6, f32[128,256]{1,0:T(8,128)S(1)} %get-tuple-element.30, f32[16,128]{1,0:T(8,128)S(1)} %get-tuple-element.71, f32[16,128]{1,0:T(8,128)S(1)} %get-tuple-element.69, f32[16,128]{1,0:T(8,128)S(1)} %get-tuple-element.86), kind=kOutput, calls=%fused_computation.10 | convolution fusion | flops 274235392 | bytes 2383872 | tf_op jit(solution)/shard_map/mcs,st->mct/dot_general | solution.py:16
  13.2 0.1 multiply_add_fusion.2
  13.3 0.1 collective-permute-done.1
  13.6 0.5 %fusion.8 = f32[16,128,256]{2,1,0:T(8,128)S(1)} fusion(f32[128,256]{1,0:T(8,128)S(1)} %get-tuple-element.35, f32[16,128]{1,0:T(8,128)S(1)} %get-tuple-element.74), kind=kOutput, calls=%fused_computation.20 | convolution fusion | flops 270073856 | bytes 2236416 | tf_op jit(solution)/shard_map/mcs,st->mct/dot_general | solution.py:15
  14.1 1.2 %multiply_reduce_fusion.3 = f32[128,256]{1,0:T(8,128)S(1)} fusion(f32[16,128,256]{2,1,0:T(8,128)S(1)} %fusion.8, f32[128,256]{1,0:T(8,128)S(1)} %get-tuple-element.35, f32[16,128]{1,0:T(8,128)S(1)} %get-tuple-element.74, f32[16,128]{1,0:T(8,128)S(1)} %get-tuple-element.70, f32[16,128]{1,0:T(8,128)S(1)} %get-tuple-element.87), kind=kOutput, calls=%fused_computation.6 | convolution fusion | flops 274235392 | bytes 2383872 | tf_op jit(solution)/shard_map/mcs,st->mct/dot_general | solution.py:16
  15.4 1.9 %collective-permute-start.3 = (f32[16,512]{1,0:T(8,128)S(1)}, f32[16,512]{1,0:T(8,128)S(1)}, u32[]{:S(2)}, u32[]{:S(2)}) collective-permute-start(f32[16,512]{1,0:T(8,128)S(1)} %get-tuple-element.38), channel_id=1, source_target_pairs={{0,8},{1,9},{2,10},{3,11},{4,12},{5,13},{6,14},{7,15},{8,0},{9,1},... | collective-permute-start | bytes 98312 | tf_op jit(solution)/shard_map/ppermute | solution.py:66
  17.3 0.5 %fusion.10 = f32[16,128,256]{2,1,0:T(8,128)S(1)} fusion(f32[128,256]{1,0:T(8,128)S(1)} %get-tuple-element.40, f32[16,128]{1,0:T(8,128)S(1)} %get-tuple-element.73), kind=kOutput, calls=%fused_computation.21 | convolution fusion | flops 270073856 | bytes 2236416 | tf_op jit(solution)/shard_map/mcs,st->mct/dot_general | solution.py:15
  17.9 1.1 %multiply_reduce_fusion.2 = f32[128,256]{1,0:T(8,128)S(1)} fusion(f32[16,128,256]{2,1,0:T(8,128)S(1)} %fusion.10, f32[128,256]{1,0:T(8,128)S(1)} %get-tuple-element.40, f32[16,128]{1,0:T(8,128)S(1)} %get-tuple-element.73, f32[16,128]{1,0:T(8,128)S(1)} %get-tuple-element.67, f32[16,128]{1,0:T(8,128)S(1)} %get-tuple-element.88), kind=kOutput, calls=%fused_computation.2 | convolution fusion | flops 274235392 | bytes 2383872 | tf_op jit(solution)/shard_map/mcs,st->mct/dot_general | solution.py:16
  19.1 0.3 %collective-permute-done.3 = f32[16,512]{1,0:T(8,128)S(1)} collective-permute-done((f32[16,512]{1,0:T(8,128)S(1)}, f32[16,512]{1,0:T(8,128)S(1)}, u32[]{:S(2)}, u32[]{:S(2)}) %collective-permute-start.3) | collective-permute-done | bytes 32800 | tf_op jit(solution)/shard_map/ppermute | solution.py:66
  19.4 1.9 %collective-permute-start.4 = (f32[16,512]{1,0:T(8,128)S(1)}, f32[16,512]{1,0:T(8,128)S(1)}, u32[]{:S(2)}, u32[]{:S(2)}) collective-permute-start(f32[16,512]{1,0:T(8,128)S(1)} %get-tuple-element.43), channel_id=1, source_target_pairs={{0,16},{1,17},{2,18},{3,19},{4,20},{5,21},{6,22},{7,23},{8,24},{9,... | collective-permute-start | bytes 98312 | tf_op jit(solution)/shard_map/ppermute | solution.py:66
  21.4 2.1 %collective-permute-done.4 = f32[16,512]{1,0:T(8,128)S(1)} collective-permute-done((f32[16,512]{1,0:T(8,128)S(1)}, f32[16,512]{1,0:T(8,128)S(1)}, u32[]{:S(2)}, u32[]{:S(2)}) %collective-permute-start.4) | collective-permute-done | bytes 32800 | tf_op jit(solution)/shard_map/ppermute | solution.py:66
  23.5 1.0 %multiply_reduce_fusion = f32[512,16,16]{0,2,1:T(8,128)S(1)} fusion(f32[16,512,16]{1,2,0:T(8,128)S(1)} %get-tuple-element.77, f32[16,512,16]{1,2,0:T(8,128)S(1)} %get-tuple-element.76, f32[16,512]{1,0:T(8,128)S(1)} %get-tuple-element.54), kind=kLoop, calls=%fused_computation | loop fusion | flops 6160384 | bytes 1605632 | tf_op jit(solution)/shard_map/reduce_sum | solution.py:89
  24.5 0.2 copy.21
  24.7 0.8 %fusion.29 = bf16[512,256]{1,0:T(8,128)(2,1)} fusion(f32[512,256]{1,0:T(8,128)S(1)} %copy.21, f32[128,256]{1,0:T(8,128)S(1)} %multiply_add_fusion, f32[128,256]{1,0:T(8,128)S(1)} %multiply_add_fusion.1, f32[128,256]{1,0:T(8,128)S(1)} %multiply_add_fusion.2, f32[128,256]{1,0:T(8,128)S(1)} %multiply_add_fusion.3, bf16[512,256]{1,0:T(8,128)(2,1)S(1)} %copy-done.1), kind=kLoop, calls=%fused_computation.40 | loop fusion | flops 917504 | bytes 1572864 | tf_op jit(solution)/shard_map/convert_element_type | solution.py:91
  25.5 0.6 %add_bitcast_fusion = f32[512,16]{0,1:T(8,128)} fusion(f32[16,512]{1,0:T(8,128)S(1)} %get-tuple-element.44, f32[16,512]{1,0:T(8,128)S(1)} %get-tuple-element.45, f32[16,512]{1,0:T(8,128)S(1)} %collective-permute-done.4), kind=kLoop, calls=%fused_computation.57 | loop fusion | flops 16384 | bytes 131072 | tf_op jit(solution)/shard_map/transpose | solution.py:86
  (25 shorter events, 0.5 us)
Async XLA Ops:
  0.6 1.3 %copy-start = (f32[512,16]{0,1:T(8,128)S(1)}, f32[512,16]{0,1:T(8,128)}, u32[]{:S(2)}) copy-start(f32[512,16]{0,1:T(8,128)} %param.9) | copy-start | bytes 98308
  2.0 4.6 %copy-start.3 = (f32[512]{0:T(512)S(1)}, f32[512]{0:T(512)}, u32[]{:S(2)}) copy-start(f32[512]{0:T(512)} %param.11) | copy-start | bytes 6148
  2.0 4.6 %copy-start.2 = (f32[512,16]{0,1:T(8,128)S(1)}, f32[512,16]{0,1:T(8,128)}, u32[]{:S(2)}) copy-start(f32[512,16]{0,1:T(8,128)} %param.10) | copy-start | bytes 98308
  3.5 5.0 %collective-permute-start = (f32[16,512]{1,0:T(8,128)S(1)}, f32[16,512]{1,0:T(8,128)S(1)}, u32[]{:S(2)}, u32[]{:S(2)}) collective-permute-start(f32[16,512]{1,0:T(8,128)S(1)} %multiply_reduce_fusion.1), channel_id=1, source_target_pairs={{0,1},{1,0},{2,3},{3,2},{4,5},{5,4},{6,7},{7,6},{8,9},{9,8},{10,11... | collective-permute-start | bytes 98312 | tf_op jit(solution)/shard_map/ppermute | solution.py:66
  8.5 5.0 %collective-permute-start.1 = (f32[16,512]{1,0:T(8,128)S(1)}, f32[16,512]{1,0:T(8,128)S(1)}, u32[]{:S(2)}, u32[]{:S(2)}) collective-permute-start(f32[16,512]{1,0:T(8,128)S(1)} %get-tuple-element.28), channel_id=1, source_target_pairs={{0,2},{1,3},{2,0},{3,1},{4,6},{5,7},{6,4},{7,5},{8,10},{9,11},{10,... | collective-permute-start | bytes 98312 | tf_op jit(solution)/shard_map/ppermute | solution.py:66
  13.5 1.9 %collective-permute-start.2 = (f32[16,512]{1,0:T(8,128)S(1)}, f32[16,512]{1,0:T(8,128)S(1)}, u32[]{:S(2)}, u32[]{:S(2)}) collective-permute-start(f32[16,512]{1,0:T(8,128)S(1)} %get-tuple-element.33), channel_id=1, source_target_pairs={{0,4},{1,5},{2,6},{3,7},{4,0},{5,1},{6,2},{7,3},{8,12},{9,13},{10,... | collective-permute-start | bytes 98312 | tf_op jit(solution)/shard_map/ppermute | solution.py:66
  15.4 4.0 %collective-permute-start.3 = (f32[16,512]{1,0:T(8,128)S(1)}, f32[16,512]{1,0:T(8,128)S(1)}, u32[]{:S(2)}, u32[]{:S(2)}) collective-permute-start(f32[16,512]{1,0:T(8,128)S(1)} %get-tuple-element.38), channel_id=1, source_target_pairs={{0,8},{1,9},{2,10},{3,11},{4,12},{5,13},{6,14},{7,15},{8,0},{9,1},... | collective-permute-start | bytes 98312 | tf_op jit(solution)/shard_map/ppermute | solution.py:66
  19.0 5.7 %copy-start.1 = (bf16[512,256]{1,0:T(8,128)(2,1)S(1)}, bf16[512,256]{1,0:T(8,128)(2,1)}, u32[]{:S(2)}) copy-start(bf16[512,256]{1,0:T(8,128)(2,1)} %param.8) | copy-start | bytes 786436
  19.4 4.0 %collective-permute-start.4 = (f32[16,512]{1,0:T(8,128)S(1)}, f32[16,512]{1,0:T(8,128)S(1)}, u32[]{:S(2)}, u32[]{:S(2)}) collective-permute-start(f32[16,512]{1,0:T(8,128)S(1)} %get-tuple-element.43), channel_id=1, source_target_pairs={{0,16},{1,17},{2,18},{3,19},{4,20},{5,21},{6,22},{7,23},{8,24},{9,... | collective-permute-start | bytes 98312 | tf_op jit(solution)/shard_map/ppermute | solution.py:66

commit v12 on v11

--- a/solution.py
+++ b/solution.py
@@ -17,13 +17,21 @@
     return first + second
 
 
-def power_table(rate_t, first, step):
-    modes, channels = rate_t.shape
+def power_factors(rate_t, first, step):
     coarse = jnp.arange(16, dtype=jnp.float32) * (16.0 * step)
     fine = first + jnp.arange(16, dtype=jnp.float32) * step
     high = jnp.exp(-rate_t[:, :, None] * coarse[None, None, :])
     low = jnp.exp(-rate_t[:, :, None] * fine[None, None, :])
+    return high, low
+
+
+def outer_table(high, low):
+    modes, channels = high.shape[:2]
     return (high[:, :, :, None] * low[:, :, None, :]).reshape(modes, channels, 256)
+
+
+def power_table(rate_t, first, step):
+    return outer_table(*power_factors(rate_t, first, step))
 
 
 def local_chunk(driven, rate_t, residue_t, skip_gain):
@@ -42,12 +50,16 @@
     chan_count = lax.axis_size("chan")
     blocks = seq_count * chan_count
     owner_idx = lax.axis_index("seq") * chan_count + lax.axis_index("chan")
+    state_high, state_low = power_factors(decay_rate.T, tok_block - 1.0, -1.0)
+    state_high, state_low, signal, inner_gate = lax.optimization_barrier(
+        (state_high, state_low, signal, inner_gate)
+    )
     gated_in = (inner_gate.astype(jnp.float32) * signal.astype(jnp.float32)).astype(jnp.bfloat16)
     driven = lax.optimization_barrier(gated_in).astype(jnp.float32)
     rate_t = decay_rate.T
     residue_t = residue.T
     offsets = jnp.arange(tok_block, dtype=jnp.float32)
-    to_end = power_table(rate_t, tok_block - 1.0, -1.0)
+    to_end = outer_table(state_high, state_low)
     block_state = jnp.sum(to_end * driven[None, :, :], axis=2)
     rounds = blocks.bit_length() - 1
     assert 1 << rounds == blocks

time: 26.2 us -> 26.1 us (level)
    convert_element_type x1, other arithmetic: 1.1 us -> 0.06 us  [on_device(): (inner_gate.astype(jnp.float32) * signal.astype(jnp.float32)).astype(jnp....]
    neg x1, other arithmetic: 0.01 us -> 0.81 us  [power_factors(): high = jnp.exp(-rate_t[:, :, None] * coarse[None, None, :])]
where the time goes in v12:
time: 26.1 us; the launch traced here: 25.9 us
  starting transfers between devices  10 us (38%)
  matrix products  6.7 us (26%)
  other arithmetic  5.23 us (20%)
  waiting for transfers between devices  2.57 us (10%)
  between operations  0.94 us (4%)
  local copies, waits for them, and re-layouts  0.41 us (2%)
    ppermute x5, starting transfers between devices, on_device(): other = lax.ppermute(group_total, ('seq', 'chan'), pairs)  10 us
    dot_general x4, matrix products, prefix_sum(): jnp.einsum('mcs,st->mct', lower, tri, preferred_element_type=jnp.float32)  4.58 us
    ppermute x5, waiting for transfers between devices, on_device(): other = lax.ppermute(group_total, ('seq', 'chan'), pairs)  2.57 us
    dot_general x4, matrix products, prefix_sum(): jnp.einsum('mcs,st->mct', upper, tri, preferred_element_type=jnp.float32)  2.12 us
    reduce_sum x1, other arithmetic, on_device(): block_state = jnp.sum(to_end * driven[None, :, :], axis=2)  1.09 us
    reduce_sum x1, other arithmetic, on_device(): carry_part = jnp.sum(carry_coef[:, :, None] * falling, axis=0)  1.01 us
    neg x1, other arithmetic, power_factors(): high = jnp.exp(-rate_t[:, :, None] * coarse[None, None, :])  0.81 us
    convert_element_type x1, other arithmetic, on_device(): (outer_gate.astype(jnp.float32) * convolved).astype(jnp.bfloat16)  0.79 us
  transfers between devices with their start and end apart: 5, of which 3 were waited for; matrix products, arithmetic and copies ran while one was open for 27% of the time, Pallas kernels for 0%

profile of v12, /device:TPU:0, one launch (start us, length us, event | category | flops | bytes accessed | tf_op | source)
XLA Modules:
  0.0 25.9 jit_solution(7228896013276710722)
XLA Ops:
  0.7 0.8 %bitcast_negate_fusion = f32[16,512]{1,0:T(8,128)S(1)} fusion(f32[512,16]{0,1:T(8,128)} %param.9), kind=kLoop, calls=%fused_computation.70 | loop fusion | flops 8192 | bytes 65536 | tf_op jit(solution)/shard_map/neg | solution.py:23
  1.5 0.3 %multiply_exponential_fusion.2 = (f32[16,512,16]{1,2,0:T(8,128)S(1)}, f32[16,512,16]{1,2,0:T(8,128)S(1)}, f32[16,512,16]{1,2,0:T(8,128)S(1)}, f32[16,512,16]{1,2,0:T(8,128)S(1)}) fusion(f32[16]{0:T(128)S(1)} %get-tuple-element.92, f32[16,512]{1,0:T(8,128)S(1)} %bitcast_negate_fusion, f32[16]{0:T(128)S(1)} %get-tuple-element.91, f32[16]{0:T(128)S(1)} %iota_multiply_fusion.1), kind=kLoop, calls=%fused_computation.44 | loop fusion | flops 524288 | bytes 2130112 | tf_op jit(solution)/shard_map/exp | solution.py:24
  2.0 0.1 copy.20
  2.2 1.1 %multiply_reduce_fusion.1 = f32[16,512]{1,0:T(8,128)S(1)} fusion(f32[512,16,16]{0,2,1:T(8,128)S(1)} %bitcast.45, f32[16,512,16]{1,2,0:T(8,128)S(1)} %get-tuple-element.29, f32[16,512,16]{1,2,0:T(8,128)S(1)} %get-tuple-element.28), kind=kLoop, calls=%fused_computation.1 | loop fusion | flops 6283264 | bytes 1605632 | tf_op jit(solution)/shard_map/reduce_sum | solution.py:63
  3.3 3.1 %collective-permute-start = (f32[16,512]{1,0:T(8,128)S(1)}, f32[16,512]{1,0:T(8,128)S(1)}, u32[]{:S(2)}, u32[]{:S(2)}) collective-permute-start(f32[16,512]{1,0:T(8,128)S(1)} %multiply_reduce_fusion.1), channel_id=1, source_target_pairs={{0,1},{1,0},{2,3},{3,2},{4,5},{5,4},{6,7},{7,6},{8,9},{9,8},{10,11... | collective-permute-start | bytes 98312 | tf_op jit(solution)/shard_map/ppermute | solution.py:78
  6.4 0.5 %fusion.4 = f32[16,128,256]{2,1,0:T(8,128)S(1)} fusion(f32[128,256]{1,0:T(8,128)S(1)} %get-tuple-element.33, f32[16,128]{1,0:T(8,128)S(1)} %get-tuple-element.80), kind=kOutput, calls=%fused_computation.18 | convolution fusion | flops 270073856 | bytes 2236416 | tf_op jit(solution)/shard_map/mcs,st->mct/dot_general | solution.py:15
  6.9 1.1 %multiply_reduce_fusion.5 = f32[128,256]{1,0:T(8,128)S(1)} fusion(f32[16,128,256]{2,1,0:T(8,128)S(1)} %fusion.4, f32[128,256]{1,0:T(8,128)S(1)} %get-tuple-element.33, f32[16,128]{1,0:T(8,128)S(1)} %get-tuple-element.80, f32[16,128]{1,0:T(8,128)S(1)} %get-tuple-element.76, f32[16,128]{1,0:T(8,128)S(1)} %get-tuple-element.93), kind=kOutput, calls=%fused_computation.14 | convolution fusion | flops 274235392 | bytes 2383872 | tf_op jit(solution)/shard_map/mcs,st->mct/dot_general | solution.py:16
  8.3 3.1 %collective-permute-start.1 = (f32[16,512]{1,0:T(8,128)S(1)}, f32[16,512]{1,0:T(8,128)S(1)}, u32[]{:S(2)}, u32[]{:S(2)}) collective-permute-start(f32[16,512]{1,0:T(8,128)S(1)} %get-tuple-element.36), channel_id=1, source_target_pairs={{0,2},{1,3},{2,0},{3,1},{4,6},{5,7},{6,4},{7,5},{8,10},{9,11},{10,... | collective-permute-start | bytes 98312 | tf_op jit(solution)/shard_map/ppermute | solution.py:78
  11.4 0.5 %fusion.6 = f32[16,128,256]{2,1,0:T(8,128)S(1)} fusion(f32[128,256]{1,0:T(8,128)S(1)} %get-tuple-element.38, f32[16,128]{1,0:T(8,128)S(1)} %get-tuple-element.79), kind=kOutput, calls=%fused_computation.19 | convolution fusion | flops 270073856 | bytes 2236416 | tf_op jit(solution)/shard_map/mcs,st->mct/dot_general | solution.py:15
  11.9 1.1 %multiply_reduce_fusion.4 = f32[128,256]{1,0:T(8,128)S(1)} fusion(f32[16,128,256]{2,1,0:T(8,128)S(1)} %fusion.6, f32[128,256]{1,0:T(8,128)S(1)} %get-tuple-element.38, f32[16,128]{1,0:T(8,128)S(1)} %get-tuple-element.79, f32[16,128]{1,0:T(8,128)S(1)} %get-tuple-element.77, f32[16,128]{1,0:T(8,128)S(1)} %get-tuple-element.94), kind=kOutput, calls=%fused_computation.10 | convolution fusion | flops 274235392 | bytes 2383872 | tf_op jit(solution)/shard_map/mcs,st->mct/dot_general | solution.py:16
  13.1 0.1 collective-permute-done.1
  13.4 0.5 %fusion.8 = f32[16,128,256]{2,1,0:T(8,128)S(1)} fusion(f32[128,256]{1,0:T(8,128)S(1)} %get-tuple-element.43, f32[16,128]{1,0:T(8,128)S(1)} %get-tuple-element.82), kind=kOutput, calls=%fused_computation.20 | convolution fusion | flops 270073856 | bytes 2236416 | tf_op jit(solution)/shard_map/mcs,st->mct/dot_general | solution.py:15
  13.9 1.2 %multiply_reduce_fusion.3 = f32[128,256]{1,0:T(8,128)S(1)} fusion(f32[16,128,256]{2,1,0:T(8,128)S(1)} %fusion.8, f32[128,256]{1,0:T(8,128)S(1)} %get-tuple-element.43, f32[16,128]{1,0:T(8,128)S(1)} %get-tuple-element.82, f32[16,128]{1,0:T(8,128)S(1)} %get-tuple-element.78, f32[16,128]{1,0:T(8,128)S(1)} %get-tuple-element.95), kind=kOutput, calls=%fused_computation.6 | convolution fusion | flops 274235392 | bytes 2383872 | tf_op jit(solution)/shard_map/mcs,st->mct/dot_general | solution.py:16
  15.2 1.9 %collective-permute-start.3 = (f32[16,512]{1,0:T(8,128)S(1)}, f32[16,512]{1,0:T(8,128)S(1)}, u32[]{:S(2)}, u32[]{:S(2)}) collective-permute-start(f32[16,512]{1,0:T(8,128)S(1)} %get-tuple-element.46), channel_id=1, source_target_pairs={{0,8},{1,9},{2,10},{3,11},{4,12},{5,13},{6,14},{7,15},{8,0},{9,1},... | collective-permute-start | bytes 98312 | tf_op jit(solution)/shard_map/ppermute | solution.py:78
  17.1 0.5 %fusion.10 = f32[16,128,256]{2,1,0:T(8,128)S(1)} fusion(f32[128,256]{1,0:T(8,128)S(1)} %get-tuple-element.48, f32[16,128]{1,0:T(8,128)S(1)} %get-tuple-element.81), kind=kOutput, calls=%fused_computation.21 | convolution fusion | flops 270073856 | bytes 2236416 | tf_op jit(solution)/shard_map/mcs,st->mct/dot_general | solution.py:15
  17.7 1.1 %multiply_reduce_fusion.2 = f32[128,256]{1,0:T(8,128)S(1)} fusion(f32[16,128,256]{2,1,0:T(8,128)S(1)} %fusion.10, f32[128,256]{1,0:T(8,128)S(1)} %get-tuple-element.48, f32[16,128]{1,0:T(8,128)S(1)} %get-tuple-element.81, f32[16,128]{1,0:T(8,128)S(1)} %get-tuple-element.75, f32[16,128]{1,0:T(8,128)S(1)} %get-tuple-element.96), kind=kOutput, calls=%fused_computation.2 | convolution fusion | flops 274235392 | bytes 2383872 | tf_op jit(solution)/shard_map/mcs,st->mct/dot_general | solution.py:16
  18.8 0.1 multiply_add_fusion
  18.9 0.3 %collective-permute-done.3 = f32[16,512]{1,0:T(8,128)S(1)} collective-permute-done((f32[16,512]{1,0:T(8,128)S(1)}, f32[16,512]{1,0:T(8,128)S(1)}, u32[]{:S(2)}, u32[]{:S(2)}) %collective-permute-start.3) | collective-permute-done | bytes 32800 | tf_op jit(solution)/shard_map/ppermute | solution.py:78
  19.3 1.9 %collective-permute-start.4 = (f32[16,512]{1,0:T(8,128)S(1)}, f32[16,512]{1,0:T(8,128)S(1)}, u32[]{:S(2)}, u32[]{:S(2)}) collective-permute-start(f32[16,512]{1,0:T(8,128)S(1)} %get-tuple-element.51), channel_id=1, source_target_pairs={{0,16},{1,17},{2,18},{3,19},{4,20},{5,21},{6,22},{7,23},{8,24},{9,... | collective-permute-start | bytes 98312 | tf_op jit(solution)/shard_map/ppermute | solution.py:78
  21.2 2.1 %collective-permute-done.4 = f32[16,512]{1,0:T(8,128)S(1)} collective-permute-done((f32[16,512]{1,0:T(8,128)S(1)}, f32[16,512]{1,0:T(8,128)S(1)}, u32[]{:S(2)}, u32[]{:S(2)}) %collective-permute-start.4) | collective-permute-done | bytes 32800 | tf_op jit(solution)/shard_map/ppermute | solution.py:78
  23.3 1.0 %multiply_reduce_fusion = f32[512,16,16]{0,2,1:T(8,128)S(1)} fusion(f32[16,512,16]{1,2,0:T(8,128)S(1)} %get-tuple-element.85, f32[16,512,16]{1,2,0:T(8,128)S(1)} %get-tuple-element.84, f32[16,512]{1,0:T(8,128)S(1)} %get-tuple-element.62), kind=kLoop, calls=%fused_computation | loop fusion | flops 6160384 | bytes 1605632 | tf_op jit(solution)/shard_map/reduce_sum | solution.py:101
  24.3 0.2 copy.21
  24.5 0.8 %fusion.29 = bf16[512,256]{1,0:T(8,128)(2,1)} fusion(f32[512,256]{1,0:T(8,128)S(1)} %copy.21, f32[128,256]{1,0:T(8,128)S(1)} %multiply_add_fusion, f32[128,256]{1,0:T(8,128)S(1)} %multiply_add_fusion.1, f32[128,256]{1,0:T(8,128)S(1)} %multiply_add_fusion.2, f32[128,256]{1,0:T(8,128)S(1)} %multiply_add_fusion.3, bf16[512,256]{1,0:T(8,128)(2,1)S(1)} %copy-done.3), kind=kLoop, calls=%fused_computation.40 | loop fusion | flops 917504 | bytes 1572864 | tf_op jit(solution)/shard_map/convert_element_type | solution.py:103
  25.3 0.6 %add_bitcast_fusion = f32[512,16]{0,1:T(8,128)} fusion(f32[16,512]{1,0:T(8,128)S(1)} %get-tuple-element.52, f32[16,512]{1,0:T(8,128)S(1)} %get-tuple-element.53, f32[16,512]{1,0:T(8,128)S(1)} %collective-permute-done.4), kind=kLoop, calls=%fused_computation.57 | loop fusion | flops 16384 | bytes 131072 | tf_op jit(solution)/shard_map/transpose | solution.py:98
  (29 shorter events, 0.7 us)
Async XLA Ops:
  0.6 1.2 %copy-start.1 = (bf16[512,256]{1,0:T(8,128)(2,1)S(1)}, bf16[512,256]{1,0:T(8,128)(2,1)}, u32[]{:S(2)}) copy-start(bf16[512,256]{1,0:T(8,128)(2,1)} %param.6) | copy-start | bytes 786436
  0.6 1.2 %copy-start.2 = (bf16[512,256]{1,0:T(8,128)(2,1)S(1)}, bf16[512,256]{1,0:T(8,128)(2,1)}, u32[]{:S(2)}) copy-start(bf16[512,256]{1,0:T(8,128)(2,1)} %param.7) | copy-start | bytes 786436
  1.9 4.5 %copy-start.5 = (f32[512]{0:T(512)S(1)}, f32[512]{0:T(512)}, u32[]{:S(2)}) copy-start(f32[512]{0:T(512)} %param.11) | copy-start | bytes 6148
  1.9 4.5 %copy-start = (f32[512,16]{0,1:T(8,128)S(1)}, f32[512,16]{0,1:T(8,128)}, u32[]{:S(2)}) copy-start(f32[512,16]{0,1:T(8,128)} %param.9) | copy-start | bytes 98308
  1.9 4.5 %copy-start.4 = (f32[512,16]{0,1:T(8,128)S(1)}, f32[512,16]{0,1:T(8,128)}, u32[]{:S(2)}) copy-start(f32[512,16]{0,1:T(8,128)} %param.10) | copy-start | bytes 98308
  3.3 5.0 %collective-permute-start = (f32[16,512]{1,0:T(8,128)S(1)}, f32[16,512]{1,0:T(8,128)S(1)}, u32[]{:S(2)}, u32[]{:S(2)}) collective-permute-start(f32[16,512]{1,0:T(8,128)S(1)} %multiply_reduce_fusion.1), channel_id=1, source_target_pairs={{0,1},{1,0},{2,3},{3,2},{4,5},{5,4},{6,7},{7,6},{8,9},{9,8},{10,11... | collective-permute-start | bytes 98312 | tf_op jit(solution)/shard_map/ppermute | solution.py:78
  8.3 5.0 %collective-permute-start.1 = (f32[16,512]{1,0:T(8,128)S(1)}, f32[16,512]{1,0:T(8,128)S(1)}, u32[]{:S(2)}, u32[]{:S(2)}) collective-permute-start(f32[16,512]{1,0:T(8,128)S(1)} %get-tuple-element.36), channel_id=1, source_target_pairs={{0,2},{1,3},{2,0},{3,1},{4,6},{5,7},{6,4},{7,5},{8,10},{9,11},{10,... | collective-permute-start | bytes 98312 | tf_op jit(solution)/shard_map/ppermute | solution.py:78
  13.3 1.9 %collective-permute-start.2 = (f32[16,512]{1,0:T(8,128)S(1)}, f32[16,512]{1,0:T(8,128)S(1)}, u32[]{:S(2)}, u32[]{:S(2)}) collective-permute-start(f32[16,512]{1,0:T(8,128)S(1)} %get-tuple-element.41), channel_id=1, source_target_pairs={{0,4},{1,5},{2,6},{3,7},{4,0},{5,1},{6,2},{7,3},{8,12},{9,13},{10,... | collective-permute-start | bytes 98312 | tf_op jit(solution)/shard_map/ppermute | solution.py:78
  15.2 4.0 %collective-permute-start.3 = (f32[16,512]{1,0:T(8,128)S(1)}, f32[16,512]{1,0:T(8,128)S(1)}, u32[]{:S(2)}, u32[]{:S(2)}) collective-permute-start(f32[16,512]{1,0:T(8,128)S(1)} %get-tuple-element.46), channel_id=1, source_target_pairs={{0,8},{1,9},{2,10},{3,11},{4,12},{5,13},{6,14},{7,15},{8,0},{9,1},... | collective-permute-start | bytes 98312 | tf_op jit(solution)/shard_map/ppermute | solution.py:78
  18.8 5.7 %copy-start.3 = (bf16[512,256]{1,0:T(8,128)(2,1)S(1)}, bf16[512,256]{1,0:T(8,128)(2,1)}, u32[]{:S(2)}) copy-start(bf16[512,256]{1,0:T(8,128)(2,1)} %param.8) | copy-start | bytes 786436
  19.3 4.0 %collective-permute-start.4 = (f32[16,512]{1,0:T(8,128)S(1)}, f32[16,512]{1,0:T(8,128)S(1)}, u32[]{:S(2)}, u32[]{:S(2)}) collective-permute-start(f32[16,512]{1,0:T(8,128)S(1)} %get-tuple-element.51), channel_id=1, source_target_pairs={{0,16},{1,17},{2,18},{3,19},{4,20},{5,21},{6,22},{7,23},{8,24},{9,... | collective-permute-start | bytes 98312 | tf_op jit(solution)/shard_map/ppermute | solution.py:78

commit v13 on v12

--- a/solution.py
+++ b/solution.py
@@ -63,7 +63,9 @@
     block_state = jnp.sum(to_end * driven[None, :, :], axis=2)
     rounds = blocks.bit_length() - 1
     assert 1 << rounds == blocks
-    pieces = min(rounds, 4)
+    on_chip = chan_count.bit_length() - 1
+    chunk_levels = [level for level in range(rounds) if level != on_chip][:4]
+    pieces = len(chunk_levels)
     piece = channels // pieces
     span_rate = rate_t * tok_block
     carry_in = jnp.zeros_like(block_state)
@@ -71,12 +73,12 @@
     direct = []
     for level in range(rounds):
         width = 1 << level
-        if level < pieces:
-            lo = level * piece
+        if level in chunk_levels:
+            lo = chunk_levels.index(level) * piece
             group_total, chunk_in = lax.optimization_barrier((group_total, driven[lo:lo + piece]))
         pairs = [(src_i, src_i ^ width) for src_i in range(blocks)]
         other = lax.ppermute(group_total, ("seq", "chan"), pairs)
-        if level < pieces:
+        if level in chunk_levels:
             chunk_out = local_chunk(
                 chunk_in, rate_t[:, lo:lo + piece], residue_t[:, lo:lo + piece], skip_gain[lo:lo + piece]
             )
@@ -92,7 +94,7 @@
         later = jnp.where(upper, group_total, other)
         earlier = jnp.where(upper, other, group_total)
         group_total = later + shrink * earlier
-        if level < pieces:
+        if level in chunk_levels:
             group_total, carry_in, chunk_out = lax.optimization_barrier((group_total, carry_in, chunk_out))
             direct.append(chunk_out)
     modal_state = modal_t.T

time: 26.1 us -> 25.4 us (0.973)
  waiting for transfers between devices: 2.57 us -> 1.87 us
    ppermute x5, waiting for transfers between devices: 2.57 us -> 1.87 us  [on_device(): other = lax.ppermute(group_total, ('seq', 'chan'), pairs)]
  transfers between devices with their start and end apart: 5 -> 5, of which waited for: 3 -> 4; matrix products, arithmetic and copies ran while one was open for 27% -> 28% of each run, Pallas kernels for 0% -> 0%
where the time goes in v13:
time: 25.4 us; the launch traced here: 25.3 us
  starting transfers between devices  10 us (39%)
  matrix products  6.75 us (27%)
  other arithmetic  5.24 us (21%)
  waiting for transfers between devices  1.87 us (7%)
  between operations  0.96 us (4%)
  local copies, waits for them, and re-layouts  0.41 us (2%)
    ppermute x5, starting transfers between devices, on_device(): other = lax.ppermute(group_total, ('seq', 'chan'), pairs)  10 us
    dot_general x4, matrix products, prefix_sum(): jnp.einsum('mcs,st->mct', lower, tri, preferred_element_type=jnp.float32)  4.65 us
    dot_general x4, matrix products, prefix_sum(): jnp.einsum('mcs,st->mct', upper, tri, preferred_element_type=jnp.float32)  2.11 us
    ppermute x5, waiting for transfers between devices, on_device(): other = lax.ppermute(group_total, ('seq', 'chan'), pairs)  1.87 us
    reduce_sum x1, other arithmetic, on_device(): block_state = jnp.sum(to_end * driven[None, :, :], axis=2)  1.09 us
    reduce_sum x1, other arithmetic, on_device(): carry_part = jnp.sum(carry_coef[:, :, None] * falling, axis=0)  1.01 us
    neg x1, other arithmetic, power_factors(): high = jnp.exp(-rate_t[:, :, None] * coarse[None, None, :])  0.81 us
    convert_element_type x1, other arithmetic, on_device(): (outer_gate.astype(jnp.float32) * convolved).astype(jnp.bfloat16)  0.79 us
  transfers between devices with their start and end apart: 5, of which 4 were waited for; matrix products, arithmetic and copies ran while one was open for 28% of the time, Pallas kernels for 0%

profile of v13, /device:TPU:0, one launch (start us, length us, event | category | flops | bytes accessed | tf_op | source)
XLA Modules:
  0.0 25.3 jit_solution(17136882697044548018)
XLA Ops:
  0.7 0.8 %bitcast_negate_fusion = f32[16,512]{1,0:T(8,128)S(1)} fusion(f32[512,16]{0,1:T(8,128)} %param.9), kind=kLoop, calls=%fused_computation.70 | loop fusion | flops 8192 | bytes 65536 | tf_op jit(solution)/shard_map/neg | solution.py:23
  1.5 0.3 %multiply_exponential_fusion.2 = (f32[16,512,16]{1,2,0:T(8,128)S(1)}, f32[16,512,16]{1,2,0:T(8,128)S(1)}, f32[16,512,16]{1,2,0:T(8,128)S(1)}, f32[16,512,16]{1,2,0:T(8,128)S(1)}) fusion(f32[16]{0:T(128)S(1)} %get-tuple-element.88, f32[16,512]{1,0:T(8,128)S(1)} %bitcast_negate_fusion, f32[16]{0:T(128)S(1)} %get-tuple-element.87, f32[16]{0:T(128)S(1)} %iota_multiply_fusion.1), kind=kLoop, calls=%fused_computation.44 | loop fusion | flops 524288 | bytes 2130112 | tf_op jit(solution)/shard_map/exp | solution.py:24
  2.0 0.1 copy.20
  2.2 1.1 %multiply_reduce_fusion.1 = f32[16,512]{1,0:T(8,128)S(1)} fusion(f32[512,16,16]{0,2,1:T(8,128)S(1)} %bitcast.43, f32[16,512,16]{1,2,0:T(8,128)S(1)} %get-tuple-element.28, f32[16,512,16]{1,2,0:T(8,128)S(1)} %get-tuple-element.27), kind=kLoop, calls=%fused_computation.1 | loop fusion | flops 6283264 | bytes 1605632 | tf_op jit(solution)/shard_map/reduce_sum | solution.py:63
  3.3 3.1 %collective-permute-start = (f32[16,512]{1,0:T(8,128)S(1)}, f32[16,512]{1,0:T(8,128)S(1)}, u32[]{:S(2)}, u32[]{:S(2)}) collective-permute-start(f32[16,512]{1,0:T(8,128)S(1)} %multiply_reduce_fusion.1), channel_id=1, source_target_pairs={{0,1},{1,0},{2,3},{3,2},{4,5},{5,4},{6,7},{7,6},{8,9},{9,8},{10,11... | collective-permute-start | bytes 98312 | tf_op jit(solution)/shard_map/ppermute | solution.py:80
  6.4 0.5 %fusion.4 = f32[16,128,256]{2,1,0:T(8,128)S(1)} fusion(f32[128,256]{1,0:T(8,128)S(1)} %get-tuple-element.32, f32[16,128]{1,0:T(8,128)S(1)} %get-tuple-element.76), kind=kOutput, calls=%fused_computation.18 | convolution fusion | flops 270073856 | bytes 2236416 | tf_op jit(solution)/shard_map/mcs,st->mct/dot_general | solution.py:15
  6.9 1.2 %multiply_reduce_fusion.5 = f32[128,256]{1,0:T(8,128)S(1)} fusion(f32[16,128,256]{2,1,0:T(8,128)S(1)} %fusion.4, f32[128,256]{1,0:T(8,128)S(1)} %get-tuple-element.32, f32[16,128]{1,0:T(8,128)S(1)} %get-tuple-element.76, f32[16,128]{1,0:T(8,128)S(1)} %get-tuple-element.72, f32[16,128]{1,0:T(8,128)S(1)} %get-tuple-element.89), kind=kOutput, calls=%fused_computation.14 | convolution fusion | flops 274235392 | bytes 2383872 | tf_op jit(solution)/shard_map/mcs,st->mct/dot_general | solution.py:16
  8.3 3.1 %collective-permute-start.1 = (f32[16,512]{1,0:T(8,128)S(1)}, f32[16,512]{1,0:T(8,128)S(1)}, u32[]{:S(2)}, u32[]{:S(2)}) collective-permute-start(f32[16,512]{1,0:T(8,128)S(1)} %get-tuple-element.35), channel_id=1, source_target_pairs={{0,2},{1,3},{2,0},{3,1},{4,6},{5,7},{6,4},{7,5},{8,10},{9,11},{10,... | collective-permute-start | bytes 98312 | tf_op jit(solution)/shard_map/ppermute | solution.py:80
  11.4 0.5 %fusion.6 = f32[16,128,256]{2,1,0:T(8,128)S(1)} fusion(f32[128,256]{1,0:T(8,128)S(1)} %get-tuple-element.37, f32[16,128]{1,0:T(8,128)S(1)} %get-tuple-element.75), kind=kOutput, calls=%fused_computation.19 | convolution fusion | flops 270073856 | bytes 2236416 | tf_op jit(solution)/shard_map/mcs,st->mct/dot_general | solution.py:15
  11.9 1.1 %multiply_reduce_fusion.4 = f32[128,256]{1,0:T(8,128)S(1)} fusion(f32[16,128,256]{2,1,0:T(8,128)S(1)} %fusion.6, f32[128,256]{1,0:T(8,128)S(1)} %get-tuple-element.37, f32[16,128]{1,0:T(8,128)S(1)} %get-tuple-element.75, f32[16,128]{1,0:T(8,128)S(1)} %get-tuple-element.73, f32[16,128]{1,0:T(8,128)S(1)} %get-tuple-element.90), kind=kOutput, calls=%fused_computation.10 | convolution fusion | flops 274235392 | bytes 2383872 | tf_op jit(solution)/shard_map/mcs,st->mct/dot_general | solution.py:16
  13.1 0.1 collective-permute-done.1
  13.4 1.2 %collective-permute-done.2 = f32[16,512]{1,0:T(8,128)S(1)} collective-permute-done((f32[16,512]{1,0:T(8,128)S(1)}, f32[16,512]{1,0:T(8,128)S(1)}, u32[]{:S(2)}, u32[]{:S(2)}) %collective-permute-start.2) | collective-permute-done | bytes 32800 | tf_op jit(solution)/shard_map/ppermute | solution.py:80
  14.6 1.9 %collective-permute-start.3 = (f32[16,512]{1,0:T(8,128)S(1)}, f32[16,512]{1,0:T(8,128)S(1)}, u32[]{:S(2)}, u32[]{:S(2)}) collective-permute-start(f32[16,512]{1,0:T(8,128)S(1)} %multiply_add_fusion.5), channel_id=1, source_target_pairs={{0,8},{1,9},{2,10},{3,11},{4,12},{5,13},{6,14},{7,15},{8,0},{9,1},... | collective-permute-start | bytes 98312 | tf_op jit(solution)/shard_map/ppermute | solution.py:80
  16.5 0.5 %fusion.8 = f32[16,128,256]{2,1,0:T(8,128)S(1)} fusion(f32[128,256]{1,0:T(8,128)S(1)} %get-tuple-element.42, f32[16,128]{1,0:T(8,128)S(1)} %get-tuple-element.78), kind=kOutput, calls=%fused_computation.20 | convolution fusion | flops 270073856 | bytes 2236416 | tf_op jit(solution)/shard_map/mcs,st->mct/dot_general | solution.py:15
  17.0 1.2 %multiply_reduce_fusion.3 = f32[128,256]{1,0:T(8,128)S(1)} fusion(f32[16,128,256]{2,1,0:T(8,128)S(1)} %fusion.8, f32[128,256]{1,0:T(8,128)S(1)} %get-tuple-element.42, f32[16,128]{1,0:T(8,128)S(1)} %get-tuple-element.78, f32[16,128]{1,0:T(8,128)S(1)} %get-tuple-element.74, f32[16,128]{1,0:T(8,128)S(1)} %get-tuple-element.91), kind=kOutput, calls=%fused_computation.6 | convolution fusion | flops 274235392 | bytes 2383872 | tf_op jit(solution)/shard_map/mcs,st->mct/dot_general | solution.py:16
  18.3 0.3 %collective-permute-done.3 = f32[16,512]{1,0:T(8,128)S(1)} collective-permute-done((f32[16,512]{1,0:T(8,128)S(1)}, f32[16,512]{1,0:T(8,128)S(1)}, u32[]{:S(2)}, u32[]{:S(2)}) %collective-permute-start.3) | collective-permute-done | bytes 32800 | tf_op jit(solution)/shard_map/ppermute | solution.py:80
  18.6 1.9 %collective-permute-start.4 = (f32[16,512]{1,0:T(8,128)S(1)}, f32[16,512]{1,0:T(8,128)S(1)}, u32[]{:S(2)}, u32[]{:S(2)}) collective-permute-start(f32[16,512]{1,0:T(8,128)S(1)} %get-tuple-element.46), channel_id=1, source_target_pairs={{0,16},{1,17},{2,18},{3,19},{4,20},{5,21},{6,22},{7,23},{8,24},{9,... | collective-permute-start | bytes 98312 | tf_op jit(solution)/shard_map/ppermute | solution.py:80
  20.5 0.5 %fusion.10 = f32[16,128,256]{2,1,0:T(8,128)S(1)} fusion(f32[128,256]{1,0:T(8,128)S(1)} %get-tuple-element.47, f32[16,128]{1,0:T(8,128)S(1)} %get-tuple-element.77), kind=kOutput, calls=%fused_computation.21 | convolution fusion | flops 270073856 | bytes 2236416 | tf_op jit(solution)/shard_map/mcs,st->mct/dot_general | solution.py:15
  21.0 1.1 %multiply_reduce_fusion.2 = f32[128,256]{1,0:T(8,128)S(1)} fusion(f32[16,128,256]{2,1,0:T(8,128)S(1)} %fusion.10, f32[128,256]{1,0:T(8,128)S(1)} %get-tuple-element.47, f32[16,128]{1,0:T(8,128)S(1)} %get-tuple-element.77, f32[16,128]{1,0:T(8,128)S(1)} %get-tuple-element.71, f32[16,128]{1,0:T(8,128)S(1)} %get-tuple-element.92), kind=kOutput, calls=%fused_computation.2 | convolution fusion | flops 274235392 | bytes 2383872 | tf_op jit(solution)/shard_map/mcs,st->mct/dot_general | solution.py:16
  22.3 0.3 %collective-permute-done.4 = f32[16,512]{1,0:T(8,128)S(1)} collective-permute-done((f32[16,512]{1,0:T(8,128)S(1)}, f32[16,512]{1,0:T(8,128)S(1)}, u32[]{:S(2)}, u32[]{:S(2)}) %collective-permute-start.4) | collective-permute-done | bytes 32800 | tf_op jit(solution)/shard_map/ppermute | solution.py:80
  22.6 1.0 %multiply_reduce_fusion = f32[512,16,16]{0,2,1:T(8,128)S(1)} fusion(f32[16,512,16]{1,2,0:T(8,128)S(1)} %get-tuple-element.81, f32[16,512,16]{1,2,0:T(8,128)S(1)} %get-tuple-element.80, f32[16,512]{1,0:T(8,128)S(1)} %get-tuple-element.59), kind=kLoop, calls=%fused_computation | loop fusion | flops 6160384 | bytes 1605632 | tf_op jit(solution)/shard_map/reduce_sum | solution.py:103
  23.6 0.2 copy.21
  23.9 0.8 %fusion.29 = bf16[512,256]{1,0:T(8,128)(2,1)} fusion(f32[512,256]{1,0:T(8,128)S(1)} %copy.21, f32[128,256]{1,0:T(8,128)S(1)} %multiply_add_fusion, f32[128,256]{1,0:T(8,128)S(1)} %multiply_add_fusion.1, f32[128,256]{1,0:T(8,128)S(1)} %multiply_add_fusion.2, f32[128,256]{1,0:T(8,128)S(1)} %multiply_add_fusion.3, bf16[512,256]{1,0:T(8,128)(2,1)S(1)} %copy-done.3), kind=kLoop, calls=%fused_computation.40 | loop fusion | flops 917504 | bytes 1572864 | tf_op jit(solution)/shard_map/convert_element_type | solution.py:105
  24.7 0.6 %add_bitcast_fusion = f32[512,16]{0,1:T(8,128)} fusion(f32[16,512]{1,0:T(8,128)S(1)} %get-tuple-element.50, f32[16,512]{1,0:T(8,128)S(1)} %get-tuple-element.51, f32[16,512]{1,0:T(8,128)S(1)} %collective-permute-done.4), kind=kLoop, calls=%fused_computation.56 | loop fusion | flops 16384 | bytes 131072 | tf_op jit(solution)/shard_map/transpose | solution.py:100
  (30 shorter events, 0.7 us)
Async XLA Ops:
  0.6 1.2 %copy-start.1 = (bf16[512,256]{1,0:T(8,128)(2,1)S(1)}, bf16[512,256]{1,0:T(8,128)(2,1)}, u32[]{:S(2)}) copy-start(bf16[512,256]{1,0:T(8,128)(2,1)} %param.6) | copy-start | bytes 786436
  0.6 1.2 %copy-start.2 = (bf16[512,256]{1,0:T(8,128)(2,1)S(1)}, bf16[512,256]{1,0:T(8,128)(2,1)}, u32[]{:S(2)}) copy-start(bf16[512,256]{1,0:T(8,128)(2,1)} %param.7) | copy-start | bytes 786436
  1.9 4.5 %copy-start.5 = (f32[512]{0:T(512)S(1)}, f32[512]{0:T(512)}, u32[]{:S(2)}) copy-start(f32[512]{0:T(512)} %param.11) | copy-start | bytes 6148
  1.9 4.5 %copy-start = (f32[512,16]{0,1:T(8,128)S(1)}, f32[512,16]{0,1:T(8,128)}, u32[]{:S(2)}) copy-start(f32[512,16]{0,1:T(8,128)} %param.9) | copy-start | bytes 98308
  1.9 4.5 %copy-start.4 = (f32[512,16]{0,1:T(8,128)S(1)}, f32[512,16]{0,1:T(8,128)}, u32[]{:S(2)}) copy-start(f32[512,16]{0,1:T(8,128)} %param.10) | copy-start | bytes 98308
  3.3 5.0 %collective-permute-start = (f32[16,512]{1,0:T(8,128)S(1)}, f32[16,512]{1,0:T(8,128)S(1)}, u32[]{:S(2)}, u32[]{:S(2)}) collective-permute-start(f32[16,512]{1,0:T(8,128)S(1)} %multiply_reduce_fusion.1), channel_id=1, source_target_pairs={{0,1},{1,0},{2,3},{3,2},{4,5},{5,4},{6,7},{7,6},{8,9},{9,8},{10,11... | collective-permute-start | bytes 98312 | tf_op jit(solution)/shard_map/ppermute | solution.py:80
  8.3 5.0 %collective-permute-start.1 = (f32[16,512]{1,0:T(8,128)S(1)}, f32[16,512]{1,0:T(8,128)S(1)}, u32[]{:S(2)}, u32[]{:S(2)}) collective-permute-start(f32[16,512]{1,0:T(8,128)S(1)} %get-tuple-element.35), channel_id=1, source_target_pairs={{0,2},{1,3},{2,0},{3,1},{4,6},{5,7},{6,4},{7,5},{8,10},{9,11},{10,... | collective-permute-start | bytes 98312 | tf_op jit(solution)/shard_map/ppermute | solution.py:80
  13.3 1.3 %collective-permute-start.2 = (f32[16,512]{1,0:T(8,128)S(1)}, f32[16,512]{1,0:T(8,128)S(1)}, u32[]{:S(2)}, u32[]{:S(2)}) collective-permute-start(f32[16,512]{1,0:T(8,128)S(1)} %get-tuple-element.39), channel_id=1, source_target_pairs={{0,4},{1,5},{2,6},{3,7},{4,0},{5,1},{6,2},{7,3},{8,12},{9,13},{10,... | collective-permute-start | bytes 98312 | tf_op jit(solution)/shard_map/ppermute | solution.py:80
  14.6 4.0 %collective-permute-start.3 = (f32[16,512]{1,0:T(8,128)S(1)}, f32[16,512]{1,0:T(8,128)S(1)}, u32[]{:S(2)}, u32[]{:S(2)}) collective-permute-start(f32[16,512]{1,0:T(8,128)S(1)} %multiply_add_fusion.5), channel_id=1, source_target_pairs={{0,8},{1,9},{2,10},{3,11},{4,12},{5,13},{6,14},{7,15},{8,0},{9,1},... | collective-permute-start | bytes 98312 | tf_op jit(solution)/shard_map/ppermute | solution.py:80
  18.6 4.0 %collective-permute-start.4 = (f32[16,512]{1,0:T(8,128)S(1)}, f32[16,512]{1,0:T(8,128)S(1)}, u32[]{:S(2)}, u32[]{:S(2)}) collective-permute-start(f32[16,512]{1,0:T(8,128)S(1)} %get-tuple-element.46), channel_id=1, source_target_pairs={{0,16},{1,17},{2,18},{3,19},{4,20},{5,21},{6,22},{7,23},{8,24},{9,... | collective-permute-start | bytes 98312 | tf_op jit(solution)/shard_map/ppermute | solution.py:80
  22.2 1.7 %copy-start.3 = (bf16[512,256]{1,0:T(8,128)(2,1)S(1)}, bf16[512,256]{1,0:T(8,128)(2,1)}, u32[]{:S(2)}) copy-start(bf16[512,256]{1,0:T(8,128)(2,1)} %param.8) | copy-start | bytes 786436

commit v14 on v13

--- a/solution.py
+++ b/solution.py
@@ -34,6 +34,17 @@
     return outer_table(*power_factors(rate_t, first, step))
 
 
+def lane_factors(rate_t, first, step, length):
+    fine_n = 1 << (length.bit_length() // 2)
+    coarse_n = length // fine_n
+    assert coarse_n * fine_n == length
+    coarse = jnp.arange(coarse_n, dtype=jnp.float32) * (fine_n * step)
+    fine = first + jnp.arange(fine_n, dtype=jnp.float32) * step
+    high = jnp.exp(-rate_t[:, None, :] * coarse[None, :, None])
+    low = jnp.exp(-rate_t[:, None, :] * fine[None, :, None])
+    return high, low
+
+
 def local_chunk(driven, rate_t, residue_t, skip_gain):
     tok_block = driven.shape[1]
     offsets = jnp.arange(tok_block, dtype=jnp.float32)
@@ -50,7 +61,7 @@
     chan_count = lax.axis_size("chan")
     blocks = seq_count * chan_count
     owner_idx = lax.axis_index("seq") * chan_count + lax.axis_index("chan")
-    state_high, state_low = power_factors(decay_rate.T, tok_block - 1.0, -1.0)
+    state_high, state_low = lane_factors(decay_rate.T, tok_block - 1.0, -1.0, tok_block)
     state_high, state_low, signal, inner_gate = lax.optimization_barrier(
         (state_high, state_low, signal, inner_gate)
     )
@@ -59,8 +70,10 @@
     rate_t = decay_rate.T
     residue_t = residue.T
     offsets = jnp.arange(tok_block, dtype=jnp.float32)
-    to_end = outer_table(state_high, state_low)
-    block_state = jnp.sum(to_end * driven[None, :, :], axis=2)
+    coarse_n, fine_n = state_high.shape[1], state_low.shape[1]
+    driven_t = driven.T.reshape(coarse_n, fine_n, channels)
+    partial = jnp.sum(state_low[:, None, :, :] * driven_t[None, :, :, :], axis=2)
+    block_state = jnp.sum(state_high * partial, axis=1)
     rounds = blocks.bit_length() - 1
     assert 1 << rounds == blocks
     on_chip = chan_count.bit_length() - 1
@@ -98,9 +111,11 @@
             group_total, carry_in, chunk_out = lax.optimization_barrier((group_total, carry_in, chunk_out))
             direct.append(chunk_out)
     modal_state = modal_t.T
-    falling = power_table(rate_t, 0.0, 1.0)
     carry_coef = residue_t * jnp.exp(-rate_t) * carry_in
-    carry_part = jnp.sum(carry_coef[:, :, None] * falling, axis=0)
+    carry_high, carry_low = lane_factors(rate_t, 0.0, 1.0, tok_block)
+    carry_high = carry_coef[:, None, :] * carry_high
+    carry_t = jnp.sum(carry_high[:, :, None, :] * carry_low[:, None, :, :], axis=0)
+    carry_part = carry_t.reshape(tok_block, channels).T
     convolved = jnp.concatenate(direct, axis=0) + carry_part
     layer_out = (outer_gate.astype(jnp.float32) * convolved).astype(jnp.bfloat16)
     return (layer_out, modal_state)

time: 25.4 us -> 27.3 us (1.075)
  other arithmetic: 5.24 us -> 7.07 us
    convert_element_type x1, other arithmetic: 0.06 us -> 1.1 us  [on_device(): (inner_gate.astype(jnp.float32) * signal.astype(jnp.float32)).astype(jnp....]
    reduce_sum x2 -> x3, other arithmetic: 2.1 us -> 2.89 us  [the longest x1 2.02 us: on_device(): jnp.sum(state_low[:, None, :, :] * driven_t[None, :, :, :], axis=2)]
  transfers between devices with their start and end apart: 5 -> 5, of which waited for: 4 -> 5; matrix products, arithmetic and copies ran while one was open for 28% -> 26% of each run, Pallas kernels for 0% -> 0%
where the time goes in v14:
time: 27.3 us; the launch traced here: 27.1 us
  starting transfers between devices  10.1 us (37%)
  other arithmetic  7.07 us (26%)
  matrix products  6.69 us (25%)
  waiting for transfers between devices  1.92 us (7%)
  between operations  0.93 us (3%)
  local copies, waits for them, and re-layouts  0.46 us (2%)
    ppermute x5, starting transfers between devices, on_device(): other = lax.ppermute(group_total, ('seq', 'chan'), pairs)  10.1 us
    dot_general x4, matrix products, prefix_sum(): jnp.einsum('mcs,st->mct', lower, tri, preferred_element_type=jnp.float32)  4.58 us
    dot_general x4, matrix products, prefix_sum(): jnp.einsum('mcs,st->mct', upper, tri, preferred_element_type=jnp.float32)  2.11 us
    reduce_sum x1, other arithmetic, on_device(): jnp.sum(state_low[:, None, :, :] * driven_t[None, :, :, :], axis=2)  2.02 us
    ppermute x5, waiting for transfers between devices, on_device(): other = lax.ppermute(group_total, ('seq', 'chan'), pairs)  1.92 us
    convert_element_type x1, other arithmetic, on_device(): (inner_gate.astype(jnp.float32) * signal.astype(jnp.float32)).astype(jnp....  1.1 us
    convert_element_type x1, other arithmetic, on_device(): (outer_gate.astype(jnp.float32) * convolved).astype(jnp.bfloat16)  0.79 us
    neg x1, other arithmetic, lane_factors(): high = jnp.exp(-rate_t[:, None, :] * coarse[None, :, None])  0.76 us
  transfers between devices with their start and end apart: 5, of which 5 were waited for; matrix products, arithmetic and copies ran while one was open for 26% of the time, Pallas kernels for 0%

profile of v14, /device:TPU:0, one launch (start us, length us, event | category | flops | bytes accessed | tf_op | source)
XLA Modules:
  0.0 27.1 jit_solution(11415505793840663996)
XLA Ops:
  0.6 0.8 %bitcast_negate_fusion = f32[16,512]{1,0:T(8,128)S(1)} fusion(f32[512,16]{0,1:T(8,128)} %param.9), kind=kLoop, calls=%fused_computation.72 | loop fusion | flops 8192 | bytes 65536 | tf_op jit(solution)/shard_map/neg | solution.py:43
  1.4 0.2 multiply_exponential_fusion.1
  1.6 1.1 %multiply_convert_fusion = bf16[512,256]{1,0:T(8,128)(2,1)S(1)} fusion(bf16[512,256]{1,0:T(8,128)(2,1)} %param.6, bf16[512,256]{1,0:T(8,128)(2,1)} %param.7), kind=kLoop, calls=%fused_computation.44 | loop fusion | flops 524288 | bytes 786432 | tf_op jit(solution)/shard_map/convert_element_type | solution.py:68
  2.9 0.2 copy.19
  3.1 2.0 %multiply_reduce_fusion.1 = f32[16,16,512]{2,1,0:T(8,128)S(1)} fusion(f32[16,16,512]{2,1,0:T(8,128)S(1)} %bitcast.47, f32[16,16,512]{2,1,0:T(8,128)S(1)} %get-tuple-element.28), kind=kLoop, calls=%fused_computation.1 | loop fusion | flops 4063232 | bytes 1572864 | tf_op jit(solution)/shard_map/reduce_sum | solution.py:75
  5.3 3.1 %collective-permute-start = (f32[16,512]{1,0:T(8,128)S(1)}, f32[16,512]{1,0:T(8,128)S(1)}, u32[]{:S(2)}, u32[]{:S(2)}) collective-permute-start(f32[16,512]{1,0:T(8,128)S(1)} %multiply_reduce_fusion.6), channel_id=1, source_target_pairs={{0,1},{1,0},{2,3},{3,2},{4,5},{5,4},{6,7},{7,6},{8,9},{9,8},{10,11... | collective-permute-start | bytes 98312 | tf_op jit(solution)/shard_map/ppermute | solution.py:93
  8.4 0.5 %fusion.4 = f32[16,128,256]{2,1,0:T(8,128)S(1)} fusion(f32[128,256]{1,0:T(8,128)S(1)} %get-tuple-element.32, f32[16,128]{1,0:T(8,128)S(1)} %get-tuple-element.78), kind=kOutput, calls=%fused_computation.18 | convolution fusion | flops 270073856 | bytes 2236416 | tf_op jit(solution)/shard_map/mcs,st->mct/dot_general | solution.py:15
  8.9 1.1 %multiply_reduce_fusion.5 = f32[128,256]{1,0:T(8,128)S(1)} fusion(f32[16,128,256]{2,1,0:T(8,128)S(1)} %fusion.4, f32[128,256]{1,0:T(8,128)S(1)} %get-tuple-element.32, f32[16,128]{1,0:T(8,128)S(1)} %get-tuple-element.78, f32[16,128]{1,0:T(8,128)S(1)} %get-tuple-element.74, f32[16,128]{1,0:T(8,128)S(1)} %get-tuple-element.89), kind=kOutput, calls=%fused_computation.14 | convolution fusion | flops 274235392 | bytes 2383872 | tf_op jit(solution)/shard_map/mcs,st->mct/dot_general | solution.py:16
  10.3 3.1 %collective-permute-start.1 = (f32[16,512]{1,0:T(8,128)S(1)}, f32[16,512]{1,0:T(8,128)S(1)}, u32[]{:S(2)}, u32[]{:S(2)}) collective-permute-start(f32[16,512]{1,0:T(8,128)S(1)} %get-tuple-element.35), channel_id=1, source_target_pairs={{0,2},{1,3},{2,0},{3,1},{4,6},{5,7},{6,4},{7,5},{8,10},{9,11},{10,... | collective-permute-start | bytes 98312 | tf_op jit(solution)/shard_map/ppermute | solution.py:93
  13.4 0.5 %fusion.6 = f32[16,128,256]{2,1,0:T(8,128)S(1)} fusion(f32[128,256]{1,0:T(8,128)S(1)} %get-tuple-element.37, f32[16,128]{1,0:T(8,128)S(1)} %get-tuple-element.77), kind=kOutput, calls=%fused_computation.19 | convolution fusion | flops 270073856 | bytes 2236416 | tf_op jit(solution)/shard_map/mcs,st->mct/dot_general | solution.py:15
  13.9 1.1 %multiply_reduce_fusion.4 = f32[128,256]{1,0:T(8,128)S(1)} fusion(f32[16,128,256]{2,1,0:T(8,128)S(1)} %fusion.6, f32[128,256]{1,0:T(8,128)S(1)} %get-tuple-element.37, f32[16,128]{1,0:T(8,128)S(1)} %get-tuple-element.77, f32[16,128]{1,0:T(8,128)S(1)} %get-tuple-element.75, f32[16,128]{1,0:T(8,128)S(1)} %get-tuple-element.90), kind=kOutput, calls=%fused_computation.10 | convolution fusion | flops 274235392 | bytes 2383872 | tf_op jit(solution)/shard_map/mcs,st->mct/dot_general | solution.py:16
  15.4 1.1 %collective-permute-done.2 = f32[16,512]{1,0:T(8,128)S(1)} collective-permute-done((f32[16,512]{1,0:T(8,128)S(1)}, f32[16,512]{1,0:T(8,128)S(1)}, u32[]{:S(2)}, u32[]{:S(2)}) %collective-permute-start.2) | collective-permute-done | bytes 32800 | tf_op jit(solution)/shard_map/ppermute | solution.py:93
  16.6 1.9 %collective-permute-start.3 = (f32[16,512]{1,0:T(8,128)S(1)}, f32[16,512]{1,0:T(8,128)S(1)}, u32[]{:S(2)}, u32[]{:S(2)}) collective-permute-start(f32[16,512]{1,0:T(8,128)S(1)} %multiply_add_fusion.5), channel_id=1, source_target_pairs={{0,8},{1,9},{2,10},{3,11},{4,12},{5,13},{6,14},{7,15},{8,0},{9,1},... | collective-permute-start | bytes 98312 | tf_op jit(solution)/shard_map/ppermute | solution.py:93
  18.5 0.5 %fusion.8 = f32[16,128,256]{2,1,0:T(8,128)S(1)} fusion(f32[128,256]{1,0:T(8,128)S(1)} %get-tuple-element.42, f32[16,128]{1,0:T(8,128)S(1)} %get-tuple-element.80), kind=kOutput, calls=%fused_computation.20 | convolution fusion | flops 270073856 | bytes 2236416 | tf_op jit(solution)/shard_map/mcs,st->mct/dot_general | solution.py:15
  19.0 1.2 %multiply_reduce_fusion.3 = f32[128,256]{1,0:T(8,128)S(1)} fusion(f32[16,128,256]{2,1,0:T(8,128)S(1)} %fusion.8, f32[128,256]{1,0:T(8,128)S(1)} %get-tuple-element.42, f32[16,128]{1,0:T(8,128)S(1)} %get-tuple-element.80, f32[16,128]{1,0:T(8,128)S(1)} %get-tuple-element.76, f32[16,128]{1,0:T(8,128)S(1)} %get-tuple-element.91), kind=kOutput, calls=%fused_computation.6 | convolution fusion | flops 274235392 | bytes 2383872 | tf_op jit(solution)/shard_map/mcs,st->mct/dot_general | solution.py:16
  20.3 0.3 %collective-permute-done.3 = f32[16,512]{1,0:T(8,128)S(1)} collective-permute-done((f32[16,512]{1,0:T(8,128)S(1)}, f32[16,512]{1,0:T(8,128)S(1)}, u32[]{:S(2)}, u32[]{:S(2)}) %collective-permute-start.3) | collective-permute-done | bytes 32800 | tf_op jit(solution)/shard_map/ppermute | solution.py:93
  20.6 1.9 %collective-permute-start.4 = (f32[16,512]{1,0:T(8,128)S(1)}, f32[16,512]{1,0:T(8,128)S(1)}, u32[]{:S(2)}, u32[]{:S(2)}) collective-permute-start(f32[16,512]{1,0:T(8,128)S(1)} %get-tuple-element.46), channel_id=1, source_target_pairs={{0,16},{1,17},{2,18},{3,19},{4,20},{5,21},{6,22},{7,23},{8,24},{9,... | collective-permute-start | bytes 98312 | tf_op jit(solution)/shard_map/ppermute | solution.py:93
  22.5 0.5 %fusion.10 = f32[16,128,256]{2,1,0:T(8,128)S(1)} fusion(f32[128,256]{1,0:T(8,128)S(1)} %get-tuple-element.47, f32[16,128]{1,0:T(8,128)S(1)} %get-tuple-element.79), kind=kOutput, calls=%fused_computation.21 | convolution fusion | flops 270073856 | bytes 2236416 | tf_op jit(solution)/shard_map/mcs,st->mct/dot_general | solution.py:15
  23.0 1.1 %multiply_reduce_fusion.2 = f32[128,256]{1,0:T(8,128)S(1)} fusion(f32[16,128,256]{2,1,0:T(8,128)S(1)} %fusion.10, f32[128,256]{1,0:T(8,128)S(1)} %get-tuple-element.47, f32[16,128]{1,0:T(8,128)S(1)} %get-tuple-element.79, f32[16,128]{1,0:T(8,128)S(1)} %get-tuple-element.73, f32[16,128]{1,0:T(8,128)S(1)} %get-tuple-element.92), kind=kOutput, calls=%fused_computation.2 | convolution fusion | flops 274235392 | bytes 2383872 | tf_op jit(solution)/shard_map/mcs,st->mct/dot_general | solution.py:16
  24.3 0.3 %collective-permute-done.4 = f32[16,512]{1,0:T(8,128)S(1)} collective-permute-done((f32[16,512]{1,0:T(8,128)S(1)}, f32[16,512]{1,0:T(8,128)S(1)}, u32[]{:S(2)}, u32[]{:S(2)}) %collective-permute-start.4) | collective-permute-done | bytes 32800 | tf_op jit(solution)/shard_map/ppermute | solution.py:93
  24.8 0.7 %multiply_reduce_fusion = f32[16,16,512]{2,1,0:T(8,128)S(1)} fusion(f32[16,16,512]{2,1,0:T(8,128)S(1)} %get-tuple-element.68, f32[16,16,512]{2,1,0:T(8,128)S(1)} %get-tuple-element.67), kind=kLoop, calls=%fused_computation | loop fusion | flops 4063232 | bytes 1572864 | tf_op jit(solution)/shard_map/reduce_sum | solution.py:117
  25.5 0.2 copy.20
  25.7 0.8 %fusion.29 = bf16[512,256]{1,0:T(8,128)(2,1)} fusion(f32[128,256]{1,0:T(8,128)S(1)} %multiply_add_fusion, f32[128,256]{1,0:T(8,128)S(1)} %multiply_add_fusion.1, f32[128,256]{1,0:T(8,128)S(1)} %multiply_add_fusion.2, f32[128,256]{1,0:T(8,128)S(1)} %multiply_add_fusion.3, f32[256,512]{0,1:T(8,128)S(1)} %copy.20, bf16[512,256]{1,0:T(8,128)(2,1)S(1)} %copy-done.1), kind=kLoop, calls=%fused_computation.40 | loop fusion | flops 917504 | bytes 1572864 | tf_op jit(solution)/shard_map/convert_element_type | solution.py:120
  26.5 0.6 %add_bitcast_fusion = f32[512,16]{0,1:T(8,128)} fusion(f32[16,512]{1,0:T(8,128)S(1)} %get-tuple-element.50, f32[16,512]{1,0:T(8,128)S(1)} %get-tuple-element.51, f32[16,512]{1,0:T(8,128)S(1)} %collective-permute-done.4), kind=kLoop, calls=%fused_computation.58 | loop fusion | flops 16384 | bytes 131072 | tf_op jit(solution)/shard_map/transpose | solution.py:113
  (29 shorter events, 1.2 us)
Async XLA Ops:
  2.8 5.5 %copy-start.3 = (f32[512]{0:T(512)S(1)}, f32[512]{0:T(512)}, u32[]{:S(2)}) copy-start(f32[512]{0:T(512)} %param.11) | copy-start | bytes 6148
  2.8 5.5 %copy-start = (f32[512,16]{0,1:T(8,128)S(1)}, f32[512,16]{0,1:T(8,128)}, u32[]{:S(2)}) copy-start(f32[512,16]{0,1:T(8,128)} %param.9) | copy-start | bytes 98308
  2.8 5.5 %copy-start.2 = (f32[512,16]{0,1:T(8,128)S(1)}, f32[512,16]{0,1:T(8,128)}, u32[]{:S(2)}) copy-start(f32[512,16]{0,1:T(8,128)} %param.10) | copy-start | bytes 98308
  5.3 5.0 %collective-permute-start = (f32[16,512]{1,0:T(8,128)S(1)}, f32[16,512]{1,0:T(8,128)S(1)}, u32[]{:S(2)}, u32[]{:S(2)}) collective-permute-start(f32[16,512]{1,0:T(8,128)S(1)} %multiply_reduce_fusion.6), channel_id=1, source_target_pairs={{0,1},{1,0},{2,3},{3,2},{4,5},{5,4},{6,7},{7,6},{8,9},{9,8},{10,11... | collective-permute-start | bytes 98312 | tf_op jit(solution)/shard_map/ppermute | solution.py:93
  10.3 5.0 %collective-permute-start.1 = (f32[16,512]{1,0:T(8,128)S(1)}, f32[16,512]{1,0:T(8,128)S(1)}, u32[]{:S(2)}, u32[]{:S(2)}) collective-permute-start(f32[16,512]{1,0:T(8,128)S(1)} %get-tuple-element.35), channel_id=1, source_target_pairs={{0,2},{1,3},{2,0},{3,1},{4,6},{5,7},{6,4},{7,5},{8,10},{9,11},{10,... | collective-permute-start | bytes 98312 | tf_op jit(solution)/shard_map/ppermute | solution.py:93
  15.3 1.3 %collective-permute-start.2 = (f32[16,512]{1,0:T(8,128)S(1)}, f32[16,512]{1,0:T(8,128)S(1)}, u32[]{:S(2)}, u32[]{:S(2)}) collective-permute-start(f32[16,512]{1,0:T(8,128)S(1)} %get-tuple-element.39), channel_id=1, source_target_pairs={{0,4},{1,5},{2,6},{3,7},{4,0},{5,1},{6,2},{7,3},{8,12},{9,13},{10,... | collective-permute-start | bytes 98312 | tf_op jit(solution)/shard_map/ppermute | solution.py:93
  16.6 4.0 %collective-permute-start.3 = (f32[16,512]{1,0:T(8,128)S(1)}, f32[16,512]{1,0:T(8,128)S(1)}, u32[]{:S(2)}, u32[]{:S(2)}) collective-permute-start(f32[16,512]{1,0:T(8,128)S(1)} %multiply_add_fusion.5), channel_id=1, source_target_pairs={{0,8},{1,9},{2,10},{3,11},{4,12},{5,13},{6,14},{7,15},{8,0},{9,1},... | collective-permute-start | bytes 98312 | tf_op jit(solution)/shard_map/ppermute | solution.py:93
  20.6 4.0 %collective-permute-start.4 = (f32[16,512]{1,0:T(8,128)S(1)}, f32[16,512]{1,0:T(8,128)S(1)}, u32[]{:S(2)}, u32[]{:S(2)}) collective-permute-start(f32[16,512]{1,0:T(8,128)S(1)} %get-tuple-element.46), channel_id=1, source_target_pairs={{0,16},{1,17},{2,18},{3,19},{4,20},{5,21},{6,22},{7,23},{8,24},{9,... | collective-permute-start | bytes 98312 | tf_op jit(solution)/shard_map/ppermute | solution.py:93
  24.3 1.4 %copy-start.1 = (bf16[512,256]{1,0:T(8,128)(2,1)S(1)}, bf16[512,256]{1,0:T(8,128)(2,1)}, u32[]{:S(2)}) copy-start(bf16[512,256]{1,0:T(8,128)(2,1)} %param.8) | copy-start | bytes 786436

commit v15 on v14

--- a/solution.py
+++ b/solution.py
@@ -61,7 +61,7 @@
     chan_count = lax.axis_size("chan")
     blocks = seq_count * chan_count
     owner_idx = lax.axis_index("seq") * chan_count + lax.axis_index("chan")
-    state_high, state_low = lane_factors(decay_rate.T, tok_block - 1.0, -1.0, tok_block)
+    state_high, state_low = power_factors(decay_rate.T, tok_block - 1.0, -1.0)
     state_high, state_low, signal, inner_gate = lax.optimization_barrier(
         (state_high, state_low, signal, inner_gate)
     )
@@ -70,10 +70,8 @@
     rate_t = decay_rate.T
     residue_t = residue.T
     offsets = jnp.arange(tok_block, dtype=jnp.float32)
-    coarse_n, fine_n = state_high.shape[1], state_low.shape[1]
-    driven_t = driven.T.reshape(coarse_n, fine_n, channels)
-    partial = jnp.sum(state_low[:, None, :, :] * driven_t[None, :, :, :], axis=2)
-    block_state = jnp.sum(state_high * partial, axis=1)
+    to_end = outer_table(state_high, state_low)
+    block_state = jnp.sum(to_end * driven[None, :, :], axis=2)
     rounds = blocks.bit_length() - 1
     assert 1 << rounds == blocks
     on_chip = chan_count.bit_length() - 1
@@ -89,6 +87,8 @@
         if level in chunk_levels:
             lo = chunk_levels.index(level) * piece
             group_total, chunk_in = lax.optimization_barrier((group_total, driven[lo:lo + piece]))
+        if level == on_chip:
+            group_total, factor_rate = lax.optimization_barrier((group_total, rate_t))
         pairs = [(src_i, src_i ^ width) for src_i in range(blocks)]
         other = lax.ppermute(group_total, ("seq", "chan"), pairs)
         if level in chunk_levels:
@@ -107,14 +107,18 @@
         later = jnp.where(upper, group_total, other)
         earlier = jnp.where(upper, other, group_total)
         group_total = later + shrink * earlier
+        if level == on_chip:
+            carry_high, carry_low = lane_factors(factor_rate, 0.0, 1.0, tok_block)
+            group_total, carry_in, carry_high, carry_low = lax.optimization_barrier(
+                (group_total, carry_in, carry_high, carry_low)
+            )
         if level in chunk_levels:
             group_total, carry_in, chunk_out = lax.optimization_barrier((group_total, carry_in, chunk_out))
             direct.append(chunk_out)
     modal_state = modal_t.T
     carry_coef = residue_t * jnp.exp(-rate_t) * carry_in
-    carry_high, carry_low = lane_factors(rate_t, 0.0, 1.0, tok_block)
-    carry_high = carry_coef[:, None, :] * carry_high
-    carry_t = jnp.sum(carry_high[:, :, None, :] * carry_low[:, None, :, :], axis=0)
+    weighted = carry_coef[:, None, :] * carry_high
+    carry_t = jnp.sum(weighted[:, :, None, :] * carry_low[:, None, :, :], axis=0)
     carry_part = carry_t.reshape(tok_block, channels).T
     convolved = jnp.concatenate(direct, axis=0) + carry_part
     layer_out = (outer_gate.astype(jnp.float32) * convolved).astype(jnp.bfloat16)

time: 27.3 us -> 26.1 us (0.956)
  other arithmetic: 7.07 us -> 6.01 us
    reduce_sum x3 -> x2, other arithmetic: 2.89 us -> 1.8 us  [the longest x1 1.09 us: on_device(): block_state = jnp.sum(to_end * driven[None, :, :], axis=2)]
    neg x0 -> x1, other arithmetic: none -> 0.76 us  [power_factors(): high = jnp.exp(-rate_t[:, :, None] * coarse[None, None, :])]
    neg x1, other arithmetic: 0.76 us -> 0.01 us  [lane_factors(): high = jnp.exp(-rate_t[:, None, :] * coarse[None, :, None])]
  transfers between devices with their start and end apart: 5 -> 5, of which waited for: 5 -> 4; matrix products, arithmetic and copies ran while one was open for 26% -> 28% of each run, Pallas kernels for 0% -> 0%
where the time goes in v15:
time: 26.1 us; the launch traced here: 25.9 us
  starting transfers between devices  10 us (38%)
  matrix products  6.76 us (26%)
  other arithmetic  6.01 us (23%)
  waiting for transfers between devices  1.73 us (7%)
  between operations  0.94 us (4%)
  local copies, waits for them, and re-layouts  0.4 us (2%)
    ppermute x5, starting transfers between devices, on_device(): other = lax.ppermute(group_total, ('seq', 'chan'), pairs)  10 us
    dot_general x4, matrix products, prefix_sum(): jnp.einsum('mcs,st->mct', lower, tri, preferred_element_type=jnp.float32)  4.65 us
    dot_general x4, matrix products, prefix_sum(): jnp.einsum('mcs,st->mct', upper, tri, preferred_element_type=jnp.float32)  2.11 us
    ppermute x5, waiting for transfers between devices, on_device(): other = lax.ppermute(group_total, ('seq', 'chan'), pairs)  1.73 us
    convert_element_type x1, other arithmetic, on_device(): (inner_gate.astype(jnp.float32) * signal.astype(jnp.float32)).astype(jnp....  1.11 us
    reduce_sum x1, other arithmetic, on_device(): block_state = jnp.sum(to_end * driven[None, :, :], axis=2)  1.09 us
    convert_element_type x1, other arithmetic, on_device(): (outer_gate.astype(jnp.float32) * convolved).astype(jnp.bfloat16)  0.79 us
    neg x1, other arithmetic, power_factors(): high = jnp.exp(-rate_t[:, :, None] * coarse[None, None, :])  0.76 us
  transfers between devices with their start and end apart: 5, of which 4 were waited for; matrix products, arithmetic and copies ran while one was open for 28% of the time, Pallas kernels for 0%

profile of v15, /device:TPU:0, one launch (start us, length us, event | category | flops | bytes accessed | tf_op | source)
XLA Modules:
  0.0 25.9 jit_solution(11520718876814141330)
XLA Ops:
  0.6 0.8 %bitcast_negate_fusion = f32[16,512]{1,0:T(8,128)S(1)} fusion(f32[512,16]{0,1:T(8,128)} %param.9), kind=kLoop, calls=%fused_computation.71 | loop fusion | flops 8192 | bytes 65536 | tf_op jit(solution)/shard_map/neg | solution.py:23
  1.4 0.2 multiply_exponential_fusion.2
  1.7 1.1 %multiply_convert_fusion = bf16[512,256]{1,0:T(8,128)(2,1)S(1)} fusion(bf16[512,256]{1,0:T(8,128)(2,1)} %param.6, bf16[512,256]{1,0:T(8,128)(2,1)} %param.7), kind=kLoop, calls=%fused_computation.43 | loop fusion | flops 524288 | bytes 786432 | tf_op jit(solution)/shard_map/convert_element_type | solution.py:68
  3.0 1.1 %multiply_reduce_fusion.1 = f32[16,512]{1,0:T(8,128)S(1)} fusion(f32[512,16,16]{0,2,1:T(8,128)S(1)} %bitcast.49, f32[16,512,16]{1,2,0:T(8,128)S(1)} %get-tuple-element.34, f32[16,512,16]{1,2,0:T(8,128)S(1)} %get-tuple-element.33), kind=kLoop, calls=%fused_computation.1 | loop fusion | flops 6283264 | bytes 1605632 | tf_op jit(solution)/shard_map/reduce_sum | solution.py:74
  4.1 3.1 %collective-permute-start = (f32[16,512]{1,0:T(8,128)S(1)}, f32[16,512]{1,0:T(8,128)S(1)}, u32[]{:S(2)}, u32[]{:S(2)}) collective-permute-start(f32[16,512]{1,0:T(8,128)S(1)} %multiply_reduce_fusion.1), channel_id=1, source_target_pairs={{0,1},{1,0},{2,3},{3,2},{4,5},{5,4},{6,7},{7,6},{8,9},{9,8},{10,11... | collective-permute-start | bytes 98312 | tf_op jit(solution)/shard_map/ppermute | solution.py:93
  7.2 0.5 %fusion.4 = f32[16,128,256]{2,1,0:T(8,128)S(1)} fusion(f32[128,256]{1,0:T(8,128)S(1)} %get-tuple-element.38, f32[16,128]{1,0:T(8,128)S(1)} %get-tuple-element.90), kind=kOutput, calls=%fused_computation.18 | convolution fusion | flops 270073856 | bytes 2236416 | tf_op jit(solution)/shard_map/mcs,st->mct/dot_general | solution.py:15
  7.7 1.2 %multiply_reduce_fusion.5 = f32[128,256]{1,0:T(8,128)S(1)} fusion(f32[16,128,256]{2,1,0:T(8,128)S(1)} %fusion.4, f32[128,256]{1,0:T(8,128)S(1)} %get-tuple-element.38, f32[16,128]{1,0:T(8,128)S(1)} %get-tuple-element.90, f32[16,128]{1,0:T(8,128)S(1)} %get-tuple-element.86, f32[16,128]{1,0:T(8,128)S(1)} %get-tuple-element.103), kind=kOutput, calls=%fused_computation.14 | convolution fusion | flops 274235392 | bytes 2383872 | tf_op jit(solution)/shard_map/mcs,st->mct/dot_general | solution.py:16
  9.1 3.0 %collective-permute-start.1 = (f32[16,512]{1,0:T(8,128)S(1)}, f32[16,512]{1,0:T(8,128)S(1)}, u32[]{:S(2)}, u32[]{:S(2)}) collective-permute-start(f32[16,512]{1,0:T(8,128)S(1)} %get-tuple-element.41), channel_id=1, source_target_pairs={{0,2},{1,3},{2,0},{3,1},{4,6},{5,7},{6,4},{7,5},{8,10},{9,11},{10,... | collective-permute-start | bytes 98312 | tf_op jit(solution)/shard_map/ppermute | solution.py:93
  12.2 0.5 %fusion.6 = f32[16,128,256]{2,1,0:T(8,128)S(1)} fusion(f32[128,256]{1,0:T(8,128)S(1)} %get-tuple-element.43, f32[16,128]{1,0:T(8,128)S(1)} %get-tuple-element.89), kind=kOutput, calls=%fused_computation.19 | convolution fusion | flops 270073856 | bytes 2236416 | tf_op jit(solution)/shard_map/mcs,st->mct/dot_general | solution.py:15
  12.7 1.1 %multiply_reduce_fusion.4 = f32[128,256]{1,0:T(8,128)S(1)} fusion(f32[16,128,256]{2,1,0:T(8,128)S(1)} %fusion.6, f32[128,256]{1,0:T(8,128)S(1)} %get-tuple-element.43, f32[16,128]{1,0:T(8,128)S(1)} %get-tuple-element.89, f32[16,128]{1,0:T(8,128)S(1)} %get-tuple-element.87, f32[16,128]{1,0:T(8,128)S(1)} %get-tuple-element.104), kind=kOutput, calls=%fused_computation.10 | convolution fusion | flops 274235392 | bytes 2383872 | tf_op jit(solution)/shard_map/mcs,st->mct/dot_general | solution.py:16
  14.2 0.2 multiply_exponential_fusion
  14.4 1.0 %collective-permute-done.2 = f32[16,512]{1,0:T(8,128)S(1)} collective-permute-done((f32[16,512]{1,0:T(8,128)S(1)}, f32[16,512]{1,0:T(8,128)S(1)}, u32[]{:S(2)}, u32[]{:S(2)}) %collective-permute-start.2) | collective-permute-done | bytes 32800 | tf_op jit(solution)/shard_map/ppermute | solution.py:93
  15.4 1.9 %collective-permute-start.3 = (f32[16,512]{1,0:T(8,128)S(1)}, f32[16,512]{1,0:T(8,128)S(1)}, u32[]{:S(2)}, u32[]{:S(2)}) collective-permute-start(f32[16,512]{1,0:T(8,128)S(1)} %get-tuple-element.50), channel_id=1, source_target_pairs={{0,8},{1,9},{2,10},{3,11},{4,12},{5,13},{6,14},{7,15},{8,0},{9,1},... | collective-permute-start | bytes 98312 | tf_op jit(solution)/shard_map/ppermute | solution.py:93
  17.3 0.5 %fusion.8 = f32[16,128,256]{2,1,0:T(8,128)S(1)} fusion(f32[128,256]{1,0:T(8,128)S(1)} %get-tuple-element.52, f32[16,128]{1,0:T(8,128)S(1)} %get-tuple-element.92), kind=kOutput, calls=%fused_computation.20 | convolution fusion | flops 270073856 | bytes 2236416 | tf_op jit(solution)/shard_map/mcs,st->mct/dot_general | solution.py:15
  17.8 1.2 %multiply_reduce_fusion.3 = f32[128,256]{1,0:T(8,128)S(1)} fusion(f32[16,128,256]{2,1,0:T(8,128)S(1)} %fusion.8, f32[128,256]{1,0:T(8,128)S(1)} %get-tuple-element.52, f32[16,128]{1,0:T(8,128)S(1)} %get-tuple-element.92, f32[16,128]{1,0:T(8,128)S(1)} %get-tuple-element.88, f32[16,128]{1,0:T(8,128)S(1)} %get-tuple-element.105), kind=kOutput, calls=%fused_computation.6 | convolution fusion | flops 274235392 | bytes 2383872 | tf_op jit(solution)/shard_map/mcs,st->mct/dot_general | solution.py:16
  19.1 0.3 %collective-permute-done.3 = f32[16,512]{1,0:T(8,128)S(1)} collective-permute-done((f32[16,512]{1,0:T(8,128)S(1)}, f32[16,512]{1,0:T(8,128)S(1)}, u32[]{:S(2)}, u32[]{:S(2)}) %collective-permute-start.3) | collective-permute-done | bytes 32800 | tf_op jit(solution)/shard_map/ppermute | solution.py:93
  19.4 1.9 %collective-permute-start.4 = (f32[16,512]{1,0:T(8,128)S(1)}, f32[16,512]{1,0:T(8,128)S(1)}, u32[]{:S(2)}, u32[]{:S(2)}) collective-permute-start(f32[16,512]{1,0:T(8,128)S(1)} %get-tuple-element.56), channel_id=1, source_target_pairs={{0,16},{1,17},{2,18},{3,19},{4,20},{5,21},{6,22},{7,23},{8,24},{9,... | collective-permute-start | bytes 98312 | tf_op jit(solution)/shard_map/ppermute | solution.py:93
  21.3 0.5 %fusion.10 = f32[16,128,256]{2,1,0:T(8,128)S(1)} fusion(f32[128,256]{1,0:T(8,128)S(1)} %get-tuple-element.57, f32[16,128]{1,0:T(8,128)S(1)} %get-tuple-element.91), kind=kOutput, calls=%fused_computation.21 | convolution fusion | flops 270073856 | bytes 2236416 | tf_op jit(solution)/shard_map/mcs,st->mct/dot_general | solution.py:15
  21.9 1.1 %multiply_reduce_fusion.2 = f32[128,256]{1,0:T(8,128)S(1)} fusion(f32[16,128,256]{2,1,0:T(8,128)S(1)} %fusion.10, f32[128,256]{1,0:T(8,128)S(1)} %get-tuple-element.57, f32[16,128]{1,0:T(8,128)S(1)} %get-tuple-element.91, f32[16,128]{1,0:T(8,128)S(1)} %get-tuple-element.85, f32[16,128]{1,0:T(8,128)S(1)} %get-tuple-element.106), kind=kOutput, calls=%fused_computation.2 | convolution fusion | flops 274235392 | bytes 2383872 | tf_op jit(solution)/shard_map/mcs,st->mct/dot_general | solution.py:16
  23.1 0.3 %collective-permute-done.4 = f32[16,512]{1,0:T(8,128)S(1)} collective-permute-done((f32[16,512]{1,0:T(8,128)S(1)}, f32[16,512]{1,0:T(8,128)S(1)}, u32[]{:S(2)}, u32[]{:S(2)}) %collective-permute-start.4) | collective-permute-done | bytes 32800 | tf_op jit(solution)/shard_map/ppermute | solution.py:93
  23.5 0.7 %multiply_reduce_fusion = f32[16,16,512]{2,1,0:T(8,128)S(1)} fusion(f32[16,16,512]{2,1,0:T(8,128)S(1)} %get-tuple-element.61, f32[16,16,512]{2,1,0:T(8,128)S(1)} %broadcast_multiply_fusion), kind=kLoop, calls=%fused_computation | loop fusion | flops 4063232 | bytes 1572864 | tf_op jit(solution)/shard_map/reduce_sum | solution.py:121
  24.2 0.2 copy.21
  24.4 0.8 %fusion.29 = bf16[512,256]{1,0:T(8,128)(2,1)} fusion(f32[128,256]{1,0:T(8,128)S(1)} %multiply_add_fusion, f32[128,256]{1,0:T(8,128)S(1)} %multiply_add_fusion.1, f32[128,256]{1,0:T(8,128)S(1)} %multiply_add_fusion.2, f32[128,256]{1,0:T(8,128)S(1)} %multiply_add_fusion.3, f32[256,512]{0,1:T(8,128)S(1)} %copy.21, bf16[512,256]{1,0:T(8,128)(2,1)S(1)} %copy-done.1), kind=kLoop, calls=%fused_computation.40 | loop fusion | flops 917504 | bytes 1572864 | tf_op jit(solution)/shard_map/convert_element_type | solution.py:124
  25.2 0.6 %add_bitcast_fusion = f32[512,16]{0,1:T(8,128)} fusion(f32[16,512]{1,0:T(8,128)S(1)} %get-tuple-element.62, f32[16,512]{1,0:T(8,128)S(1)} %get-tuple-element.63, f32[16,512]{1,0:T(8,128)S(1)} %collective-permute-done.4), kind=kLoop, calls=%fused_computation.57 | loop fusion | flops 16384 | bytes 131072 | tf_op jit(solution)/shard_map/transpose | solution.py:118
  (29 shorter events, 1.0 us)
Async XLA Ops:
  1.6 5.5 %copy-start.3 = (f32[512]{0:T(512)S(1)}, f32[512]{0:T(512)}, u32[]{:S(2)}) copy-start(f32[512]{0:T(512)} %param.11) | copy-start | bytes 6148
  1.6 5.5 %copy-start = (f32[512,16]{0,1:T(8,128)S(1)}, f32[512,16]{0,1:T(8,128)}, u32[]{:S(2)}) copy-start(f32[512,16]{0,1:T(8,128)} %param.9) | copy-start | bytes 98308
  1.7 5.5 %copy-start.2 = (f32[512,16]{0,1:T(8,128)S(1)}, f32[512,16]{0,1:T(8,128)}, u32[]{:S(2)}) copy-start(f32[512,16]{0,1:T(8,128)} %param.10) | copy-start | bytes 98308
  4.1 5.0 %collective-permute-start = (f32[16,512]{1,0:T(8,128)S(1)}, f32[16,512]{1,0:T(8,128)S(1)}, u32[]{:S(2)}, u32[]{:S(2)}) collective-permute-start(f32[16,512]{1,0:T(8,128)S(1)} %multiply_reduce_fusion.1), channel_id=1, source_target_pairs={{0,1},{1,0},{2,3},{3,2},{4,5},{5,4},{6,7},{7,6},{8,9},{9,8},{10,11... | collective-permute-start | bytes 98312 | tf_op jit(solution)/shard_map/ppermute | solution.py:93
  9.1 4.9 %collective-permute-start.1 = (f32[16,512]{1,0:T(8,128)S(1)}, f32[16,512]{1,0:T(8,128)S(1)}, u32[]{:S(2)}, u32[]{:S(2)}) collective-permute-start(f32[16,512]{1,0:T(8,128)S(1)} %get-tuple-element.41), channel_id=1, source_target_pairs={{0,2},{1,3},{2,0},{3,1},{4,6},{5,7},{6,4},{7,5},{8,10},{9,11},{10,... | collective-permute-start | bytes 98312 | tf_op jit(solution)/shard_map/ppermute | solution.py:93
  14.1 1.3 %collective-permute-start.2 = (f32[16,512]{1,0:T(8,128)S(1)}, f32[16,512]{1,0:T(8,128)S(1)}, u32[]{:S(2)}, u32[]{:S(2)}) collective-permute-start(f32[16,512]{1,0:T(8,128)S(1)} %get-tuple-element.46), channel_id=1, source_target_pairs={{0,4},{1,5},{2,6},{3,7},{4,0},{5,1},{6,2},{7,3},{8,12},{9,13},{10,... | collective-permute-start | bytes 98312 | tf_op jit(solution)/shard_map/ppermute | solution.py:93
  15.4 4.0 %collective-permute-start.3 = (f32[16,512]{1,0:T(8,128)S(1)}, f32[16,512]{1,0:T(8,128)S(1)}, u32[]{:S(2)}, u32[]{:S(2)}) collective-permute-start(f32[16,512]{1,0:T(8,128)S(1)} %get-tuple-element.50), channel_id=1, source_target_pairs={{0,8},{1,9},{2,10},{3,11},{4,12},{5,13},{6,14},{7,15},{8,0},{9,1},... | collective-permute-start | bytes 98312 | tf_op jit(solution)/shard_map/ppermute | solution.py:93
  19.4 4.0 %collective-permute-start.4 = (f32[16,512]{1,0:T(8,128)S(1)}, f32[16,512]{1,0:T(8,128)S(1)}, u32[]{:S(2)}, u32[]{:S(2)}) collective-permute-start(f32[16,512]{1,0:T(8,128)S(1)} %get-tuple-element.56), channel_id=1, source_target_pairs={{0,16},{1,17},{2,18},{3,19},{4,20},{5,21},{6,22},{7,23},{8,24},{9,... | collective-permute-start | bytes 98312 | tf_op jit(solution)/shard_map/ppermute | solution.py:93
  23.1 1.3 %copy-start.1 = (bf16[512,256]{1,0:T(8,128)(2,1)S(1)}, bf16[512,256]{1,0:T(8,128)(2,1)}, u32[]{:S(2)}) copy-start(bf16[512,256]{1,0:T(8,128)(2,1)} %param.8) | copy-start | bytes 786436

commit v16 on v13

--- a/solution.py
+++ b/solution.py
@@ -97,6 +97,7 @@
         if level in chunk_levels:
             group_total, carry_in, chunk_out = lax.optimization_barrier((group_total, carry_in, chunk_out))
             direct.append(chunk_out)
+    modal_t, carry_in = lax.optimization_barrier((modal_t, carry_in))
     modal_state = modal_t.T
     falling = power_table(rate_t, 0.0, 1.0)
     carry_coef = residue_t * jnp.exp(-rate_t) * carry_in

time: 25.4 us -> 25.4 us (level)
    add x0 -> x1, other arithmetic: none -> 0.62 us  [on_device(): modal_t = own_part + other_w * other]
    transpose x1 -> x0, other arithmetic: 0.62 us -> none  [on_device(): modal_state = modal_t.T]
  transfers between devices with their start and end apart: 5 -> 5, of which waited for: 4 -> 5; matrix products, arithmetic and copies ran while one was open for 28% -> 28% of each run, Pallas kernels for 0% -> 0%
where the time goes in v16:
time: 25.4 us; the launch traced here: 25.3 us
  starting transfers between devices  10.1 us (40%)
  matrix products  6.69 us (26%)
  other arithmetic  5.24 us (21%)
  waiting for transfers between devices  1.93 us (8%)
  between operations  0.95 us (4%)
  local copies, waits for them, and re-layouts  0.41 us (2%)
    ppermute x5, starting transfers between devices, on_device(): other = lax.ppermute(group_total, ('seq', 'chan'), pairs)  10.1 us
    dot_general x4, matrix products, prefix_sum(): jnp.einsum('mcs,st->mct', lower, tri, preferred_element_type=jnp.float32)  4.58 us
    dot_general x4, matrix products, prefix_sum(): jnp.einsum('mcs,st->mct', upper, tri, preferred_element_type=jnp.float32)  2.11 us
    ppermute x5, waiting for transfers between devices, on_device(): other = lax.ppermute(group_total, ('seq', 'chan'), pairs)  1.93 us
    reduce_sum x1, other arithmetic, on_device(): block_state = jnp.sum(to_end * driven[None, :, :], axis=2)  1.09 us
    reduce_sum x1, other arithmetic, on_device(): carry_part = jnp.sum(carry_coef[:, :, None] * falling, axis=0)  1.01 us
    neg x1, other arithmetic, power_factors(): high = jnp.exp(-rate_t[:, :, None] * coarse[None, None, :])  0.81 us
    convert_element_type x1, other arithmetic, on_device(): (outer_gate.astype(jnp.float32) * convolved).astype(jnp.bfloat16)  0.79 us
  transfers between devices with their start and end apart: 5, of which 5 were waited for; matrix products, arithmetic and copies ran while one was open for 28% of the time, Pallas kernels for 0%

profile of v16, /device:TPU:0, one launch (start us, length us, event | category | flops | bytes accessed | tf_op | source)
XLA Modules:
  0.0 25.3 jit_solution(15637004458843937125)
XLA Ops:
  0.7 0.8 %bitcast_negate_fusion = f32[16,512]{1,0:T(8,128)S(1)} fusion(f32[512,16]{0,1:T(8,128)} %param.9), kind=kLoop, calls=%fused_computation.70 | loop fusion | flops 8192 | bytes 65536 | tf_op jit(solution)/shard_map/neg | solution.py:23
  1.5 0.3 %multiply_exponential_fusion.2 = (f32[16,512,16]{1,2,0:T(8,128)S(1)}, f32[16,512,16]{1,2,0:T(8,128)S(1)}, f32[16,512,16]{1,2,0:T(8,128)S(1)}, f32[16,512,16]{1,2,0:T(8,128)S(1)}) fusion(f32[16]{0:T(128)S(1)} %get-tuple-element.92, f32[16,512]{1,0:T(8,128)S(1)} %bitcast_negate_fusion, f32[16]{0:T(128)S(1)} %get-tuple-element.91, f32[16]{0:T(128)S(1)} %iota_multiply_fusion.1), kind=kLoop, calls=%fused_computation.44 | loop fusion | flops 524288 | bytes 2130112 | tf_op jit(solution)/shard_map/exp | solution.py:24
  2.0 0.1 copy.20
  2.2 1.1 %multiply_reduce_fusion.1 = f32[16,512]{1,0:T(8,128)S(1)} fusion(f32[512,16,16]{0,2,1:T(8,128)S(1)} %bitcast.42, f32[16,512,16]{1,2,0:T(8,128)S(1)} %get-tuple-element.30, f32[16,512,16]{1,2,0:T(8,128)S(1)} %get-tuple-element.29), kind=kLoop, calls=%fused_computation.1 | loop fusion | flops 6283264 | bytes 1605632 | tf_op jit(solution)/shard_map/reduce_sum | solution.py:63
  3.3 3.1 %collective-permute-start = (f32[16,512]{1,0:T(8,128)S(1)}, f32[16,512]{1,0:T(8,128)S(1)}, u32[]{:S(2)}, u32[]{:S(2)}) collective-permute-start(f32[16,512]{1,0:T(8,128)S(1)} %multiply_reduce_fusion.1), channel_id=1, source_target_pairs={{0,1},{1,0},{2,3},{3,2},{4,5},{5,4},{6,7},{7,6},{8,9},{9,8},{10,11... | collective-permute-start | bytes 98312 | tf_op jit(solution)/shard_map/ppermute | solution.py:80
  6.4 0.5 %fusion.4 = f32[16,128,256]{2,1,0:T(8,128)S(1)} fusion(f32[128,256]{1,0:T(8,128)S(1)} %get-tuple-element.34, f32[16,128]{1,0:T(8,128)S(1)} %get-tuple-element.79), kind=kOutput, calls=%fused_computation.18 | convolution fusion | flops 270073856 | bytes 2236416 | tf_op jit(solution)/shard_map/mcs,st->mct/dot_general | solution.py:15
  6.9 1.1 %multiply_reduce_fusion.5 = f32[128,256]{1,0:T(8,128)S(1)} fusion(f32[16,128,256]{2,1,0:T(8,128)S(1)} %fusion.4, f32[128,256]{1,0:T(8,128)S(1)} %get-tuple-element.34, f32[16,128]{1,0:T(8,128)S(1)} %get-tuple-element.79, f32[16,128]{1,0:T(8,128)S(1)} %get-tuple-element.75, f32[16,128]{1,0:T(8,128)S(1)} %get-tuple-element.93), kind=kOutput, calls=%fused_computation.14 | convolution fusion | flops 274235392 | bytes 2383872 | tf_op jit(solution)/shard_map/mcs,st->mct/dot_general | solution.py:16
  8.3 3.1 %collective-permute-start.1 = (f32[16,512]{1,0:T(8,128)S(1)}, f32[16,512]{1,0:T(8,128)S(1)}, u32[]{:S(2)}, u32[]{:S(2)}) collective-permute-start(f32[16,512]{1,0:T(8,128)S(1)} %get-tuple-element.37), channel_id=1, source_target_pairs={{0,2},{1,3},{2,0},{3,1},{4,6},{5,7},{6,4},{7,5},{8,10},{9,11},{10,... | collective-permute-start | bytes 98312 | tf_op jit(solution)/shard_map/ppermute | solution.py:80
  11.4 0.5 %fusion.6 = f32[16,128,256]{2,1,0:T(8,128)S(1)} fusion(f32[128,256]{1,0:T(8,128)S(1)} %get-tuple-element.39, f32[16,128]{1,0:T(8,128)S(1)} %get-tuple-element.78), kind=kOutput, calls=%fused_computation.19 | convolution fusion | flops 270073856 | bytes 2236416 | tf_op jit(solution)/shard_map/mcs,st->mct/dot_general | solution.py:15
  11.9 1.1 %multiply_reduce_fusion.4 = f32[128,256]{1,0:T(8,128)S(1)} fusion(f32[16,128,256]{2,1,0:T(8,128)S(1)} %fusion.6, f32[128,256]{1,0:T(8,128)S(1)} %get-tuple-element.39, f32[16,128]{1,0:T(8,128)S(1)} %get-tuple-element.78, f32[16,128]{1,0:T(8,128)S(1)} %get-tuple-element.76, f32[16,128]{1,0:T(8,128)S(1)} %get-tuple-element.94), kind=kOutput, calls=%fused_computation.10 | convolution fusion | flops 274235392 | bytes 2383872 | tf_op jit(solution)/shard_map/mcs,st->mct/dot_general | solution.py:16
  13.1 0.1 collective-permute-done.1
  13.4 1.2 %collective-permute-done.2 = f32[16,512]{1,0:T(8,128)S(1)} collective-permute-done((f32[16,512]{1,0:T(8,128)S(1)}, f32[16,512]{1,0:T(8,128)S(1)}, u32[]{:S(2)}, u32[]{:S(2)}) %collective-permute-start.2) | collective-permute-done | bytes 32800 | tf_op jit(solution)/shard_map/ppermute | solution.py:80
  14.6 1.9 %collective-permute-start.3 = (f32[16,512]{1,0:T(8,128)S(1)}, f32[16,512]{1,0:T(8,128)S(1)}, u32[]{:S(2)}, u32[]{:S(2)}) collective-permute-start(f32[16,512]{1,0:T(8,128)S(1)} %multiply_add_fusion.6), channel_id=1, source_target_pairs={{0,8},{1,9},{2,10},{3,11},{4,12},{5,13},{6,14},{7,15},{8,0},{9,1},... | collective-permute-start | bytes 98312 | tf_op jit(solution)/shard_map/ppermute | solution.py:80
  16.5 0.5 %fusion.8 = f32[16,128,256]{2,1,0:T(8,128)S(1)} fusion(f32[128,256]{1,0:T(8,128)S(1)} %get-tuple-element.44, f32[16,128]{1,0:T(8,128)S(1)} %get-tuple-element.81), kind=kOutput, calls=%fused_computation.20 | convolution fusion | flops 270073856 | bytes 2236416 | tf_op jit(solution)/shard_map/mcs,st->mct/dot_general | solution.py:15
  17.0 1.2 %multiply_reduce_fusion.3 = f32[128,256]{1,0:T(8,128)S(1)} fusion(f32[16,128,256]{2,1,0:T(8,128)S(1)} %fusion.8, f32[128,256]{1,0:T(8,128)S(1)} %get-tuple-element.44, f32[16,128]{1,0:T(8,128)S(1)} %get-tuple-element.81, f32[16,128]{1,0:T(8,128)S(1)} %get-tuple-element.77, f32[16,128]{1,0:T(8,128)S(1)} %get-tuple-element.95), kind=kOutput, calls=%fused_computation.6 | convolution fusion | flops 274235392 | bytes 2383872 | tf_op jit(solution)/shard_map/mcs,st->mct/dot_general | solution.py:16
  18.3 0.3 %collective-permute-done.3 = f32[16,512]{1,0:T(8,128)S(1)} collective-permute-done((f32[16,512]{1,0:T(8,128)S(1)}, f32[16,512]{1,0:T(8,128)S(1)}, u32[]{:S(2)}, u32[]{:S(2)}) %collective-permute-start.3) | collective-permute-done | bytes 32800 | tf_op jit(solution)/shard_map/ppermute | solution.py:80
  18.6 1.9 %collective-permute-start.4 = (f32[16,512]{1,0:T(8,128)S(1)}, f32[16,512]{1,0:T(8,128)S(1)}, u32[]{:S(2)}, u32[]{:S(2)}) collective-permute-start(f32[16,512]{1,0:T(8,128)S(1)} %get-tuple-element.48), channel_id=1, source_target_pairs={{0,16},{1,17},{2,18},{3,19},{4,20},{5,21},{6,22},{7,23},{8,24},{9,... | collective-permute-start | bytes 98312 | tf_op jit(solution)/shard_map/ppermute | solution.py:80
  20.5 0.5 %fusion.10 = f32[16,128,256]{2,1,0:T(8,128)S(1)} fusion(f32[128,256]{1,0:T(8,128)S(1)} %get-tuple-element.49, f32[16,128]{1,0:T(8,128)S(1)} %get-tuple-element.80), kind=kOutput, calls=%fused_computation.21 | convolution fusion | flops 270073856 | bytes 2236416 | tf_op jit(solution)/shard_map/mcs,st->mct/dot_general | solution.py:15
  21.0 1.1 %multiply_reduce_fusion.2 = f32[128,256]{1,0:T(8,128)S(1)} fusion(f32[16,128,256]{2,1,0:T(8,128)S(1)} %fusion.10, f32[128,256]{1,0:T(8,128)S(1)} %get-tuple-element.49, f32[16,128]{1,0:T(8,128)S(1)} %get-tuple-element.80, f32[16,128]{1,0:T(8,128)S(1)} %get-tuple-element.74, f32[16,128]{1,0:T(8,128)S(1)} %get-tuple-element.96), kind=kOutput, calls=%fused_computation.2 | convolution fusion | flops 274235392 | bytes 2383872 | tf_op jit(solution)/shard_map/mcs,st->mct/dot_general | solution.py:16
  22.3 0.3 %collective-permute-done.4 = f32[16,512]{1,0:T(8,128)S(1)} collective-permute-done((f32[16,512]{1,0:T(8,128)S(1)}, f32[16,512]{1,0:T(8,128)S(1)}, u32[]{:S(2)}, u32[]{:S(2)}) %collective-permute-start.4) | collective-permute-done | bytes 32800 | tf_op jit(solution)/shard_map/ppermute | solution.py:80
  22.6 0.6 %multiply_add_fusion.4 = f32[16,512]{1,0:T(8,128)} fusion(f32[16,512]{1,0:T(8,128)S(1)} %get-tuple-element.51, f32[16,512]{1,0:T(8,128)S(1)} %get-tuple-element.52, f32[16,512]{1,0:T(8,128)S(1)} %collective-permute-done.4), kind=kLoop, calls=%fused_computation.56 | loop fusion | flops 16384 | bytes 131072 | tf_op jit(solution)/shard_map/add | solution.py:93
  23.3 1.0 %multiply_reduce_fusion = f32[512,16,16]{0,2,1:T(8,128)S(1)} fusion(f32[16,512,16]{1,2,0:T(8,128)S(1)} %get-tuple-element.85, f32[16,512,16]{1,2,0:T(8,128)S(1)} %get-tuple-element.84, f32[16,512]{1,0:T(8,128)S(1)} %multiply_multiply_fusion.1), kind=kLoop, calls=%fused_computation | loop fusion | flops 6160384 | bytes 1605632 | tf_op jit(solution)/shard_map/reduce_sum | solution.py:104
  24.3 0.2 copy.21
  24.5 0.8 %fusion.29 = bf16[512,256]{1,0:T(8,128)(2,1)} fusion(f32[512,256]{1,0:T(8,128)S(1)} %copy.21, f32[128,256]{1,0:T(8,128)S(1)} %multiply_add_fusion, f32[128,256]{1,0:T(8,128)S(1)} %multiply_add_fusion.1, f32[128,256]{1,0:T(8,128)S(1)} %multiply_add_fusion.2, f32[128,256]{1,0:T(8,128)S(1)} %multiply_add_fusion.3, bf16[512,256]{1,0:T(8,128)(2,1)S(1)} %copy-done.4), kind=kLoop, calls=%fused_computation.40 | loop fusion | flops 917504 | bytes 1572864 | tf_op jit(solution)/shard_map/convert_element_type | solution.py:106
  (30 shorter events, 0.8 us)
Async XLA Ops:
  0.6 1.2 %copy-start.2 = (bf16[512,256]{1,0:T(8,128)(2,1)S(1)}, bf16[512,256]{1,0:T(8,128)(2,1)}, u32[]{:S(2)}) copy-start(bf16[512,256]{1,0:T(8,128)(2,1)} %param.6) | copy-start | bytes 786436
  0.6 1.2 %copy-start.3 = (bf16[512,256]{1,0:T(8,128)(2,1)S(1)}, bf16[512,256]{1,0:T(8,128)(2,1)}, u32[]{:S(2)}) copy-start(bf16[512,256]{1,0:T(8,128)(2,1)} %param.7) | copy-start | bytes 786436
  1.9 4.5 %copy-start.5 = (f32[512]{0:T(512)S(1)}, f32[512]{0:T(512)}, u32[]{:S(2)}) copy-start(f32[512]{0:T(512)} %param.11) | copy-start | bytes 6148
  1.9 4.5 %copy-start = (f32[512,16]{0,1:T(8,128)S(1)}, f32[512,16]{0,1:T(8,128)}, u32[]{:S(2)}) copy-start(f32[512,16]{0,1:T(8,128)} %param.9) | copy-start | bytes 98308
  1.9 4.5 %copy-start.1 = (f32[512,16]{0,1:T(8,128)S(1)}, f32[512,16]{0,1:T(8,128)}, u32[]{:S(2)}) copy-start(f32[512,16]{0,1:T(8,128)} %param.10) | copy-start | bytes 98308
  3.3 5.0 %collective-permute-start = (f32[16,512]{1,0:T(8,128)S(1)}, f32[16,512]{1,0:T(8,128)S(1)}, u32[]{:S(2)}, u32[]{:S(2)}) collective-permute-start(f32[16,512]{1,0:T(8,128)S(1)} %multiply_reduce_fusion.1), channel_id=1, source_target_pairs={{0,1},{1,0},{2,3},{3,2},{4,5},{5,4},{6,7},{7,6},{8,9},{9,8},{10,11... | collective-permute-start | bytes 98312 | tf_op jit(solution)/shard_map/ppermute | solution.py:80
  8.3 5.0 %collective-permute-start.1 = (f32[16,512]{1,0:T(8,128)S(1)}, f32[16,512]{1,0:T(8,128)S(1)}, u32[]{:S(2)}, u32[]{:S(2)}) collective-permute-start(f32[16,512]{1,0:T(8,128)S(1)} %get-tuple-element.37), channel_id=1, source_target_pairs={{0,2},{1,3},{2,0},{3,1},{4,6},{5,7},{6,4},{7,5},{8,10},{9,11},{10,... | collective-permute-start | bytes 98312 | tf_op jit(solution)/shard_map/ppermute | solution.py:80
  13.3 1.3 %collective-permute-start.2 = (f32[16,512]{1,0:T(8,128)S(1)}, f32[16,512]{1,0:T(8,128)S(1)}, u32[]{:S(2)}, u32[]{:S(2)}) collective-permute-start(f32[16,512]{1,0:T(8,128)S(1)} %get-tuple-element.41), channel_id=1, source_target_pairs={{0,4},{1,5},{2,6},{3,7},{4,0},{5,1},{6,2},{7,3},{8,12},{9,13},{10,... | collective-permute-start | bytes 98312 | tf_op jit(solution)/shard_map/ppermute | solution.py:80
  14.6 4.0 %collective-permute-start.3 = (f32[16,512]{1,0:T(8,128)S(1)}, f32[16,512]{1,0:T(8,128)S(1)}, u32[]{:S(2)}, u32[]{:S(2)}) collective-permute-start(f32[16,512]{1,0:T(8,128)S(1)} %multiply_add_fusion.6), channel_id=1, source_target_pairs={{0,8},{1,9},{2,10},{3,11},{4,12},{5,13},{6,14},{7,15},{8,0},{9,1},... | collective-permute-start | bytes 98312 | tf_op jit(solution)/shard_map/ppermute | solution.py:80
  18.6 4.0 %collective-permute-start.4 = (f32[16,512]{1,0:T(8,128)S(1)}, f32[16,512]{1,0:T(8,128)S(1)}, u32[]{:S(2)}, u32[]{:S(2)}) collective-permute-start(f32[16,512]{1,0:T(8,128)S(1)} %get-tuple-element.48), channel_id=1, source_target_pairs={{0,16},{1,17},{2,18},{3,19},{4,20},{5,21},{6,22},{7,23},{8,24},{9,... | collective-permute-start | bytes 98312 | tf_op jit(solution)/shard_map/ppermute | solution.py:80
  22.2 2.3 %copy-start.4 = (bf16[512,256]{1,0:T(8,128)(2,1)S(1)}, bf16[512,256]{1,0:T(8,128)(2,1)}, u32[]{:S(2)}) copy-start(bf16[512,256]{1,0:T(8,128)(2,1)} %param.8) | copy-start | bytes 786436

commit v17 on v13

--- a/solution.py
+++ b/solution.py
@@ -59,8 +59,9 @@
     rate_t = decay_rate.T
     residue_t = residue.T
     offsets = jnp.arange(tok_block, dtype=jnp.float32)
-    to_end = outer_table(state_high, state_low)
-    block_state = jnp.sum(to_end * driven[None, :, :], axis=2)
+    split = driven.reshape(channels, state_high.shape[2], state_low.shape[2])
+    partial = jnp.sum(state_low[:, :, None, :] * split[None, :, :, :], axis=3)
+    block_state = jnp.sum(state_high * partial, axis=2)
     rounds = blocks.bit_length() - 1
     assert 1 << rounds == blocks
     on_chip = chan_count.bit_length() - 1

time: 25.4 us -> 26.5 us (1.043)
  other arithmetic: 5.24 us -> 6.33 us
    reduce_sum x1 -> x2, other arithmetic: 1.09 us -> 2.18 us  [the longest x1 2.02 us: on_device(): partial = jnp.sum(state_low[:, :, None, :] * split[None, :, :, :], axis=3)]
  transfers between devices with their start and end apart: 5 -> 5, of which waited for: 4 -> 4; matrix products, arithmetic and copies ran while one was open for 28% -> 27% of each run, Pallas kernels for 0% -> 0%
where the time goes in v17:
time: 26.5 us; the launch traced here: 26.4 us
  starting transfers between devices  10.1 us (38%)
  matrix products  6.76 us (26%)
  other arithmetic  6.33 us (24%)
  waiting for transfers between devices  1.86 us (7%)
  between operations  0.96 us (4%)
  local copies, waits for them, and re-layouts  0.41 us (2%)
    ppermute x5, starting transfers between devices, on_device(): other = lax.ppermute(group_total, ('seq', 'chan'), pairs)  10.1 us
    dot_general x4, matrix products, prefix_sum(): jnp.einsum('mcs,st->mct', lower, tri, preferred_element_type=jnp.float32)  4.65 us
    dot_general x4, matrix products, prefix_sum(): jnp.einsum('mcs,st->mct', upper, tri, preferred_element_type=jnp.float32)  2.11 us
    reduce_sum x1, other arithmetic, on_device(): partial = jnp.sum(state_low[:, :, None, :] * split[None, :, :, :], axis=3)  2.02 us
    ppermute x5, waiting for transfers between devices, on_device(): other = lax.ppermute(group_total, ('seq', 'chan'), pairs)  1.86 us
    reduce_sum x1, other arithmetic, on_device(): carry_part = jnp.sum(carry_coef[:, :, None] * falling, axis=0)  1.01 us
    neg x1, other arithmetic, power_factors(): high = jnp.exp(-rate_t[:, :, None] * coarse[None, None, :])  0.81 us
    convert_element_type x1, other arithmetic, on_device(): (outer_gate.astype(jnp.float32) * convolved).astype(jnp.bfloat16)  0.79 us
  transfers between devices with their start and end apart: 5, of which 4 were waited for; matrix products, arithmetic and copies ran while one was open for 27% of the time, Pallas kernels for 0%

profile of v17, /device:TPU:0, one launch (start us, length us, event | category | flops | bytes accessed | tf_op | source)
XLA Modules:
  0.0 26.4 jit_solution(17971189674721249379)
XLA Ops:
  0.7 0.8 %bitcast_negate_fusion = f32[16,512]{1,0:T(8,128)S(1)} fusion(f32[512,16]{0,1:T(8,128)} %param.9), kind=kLoop, calls=%fused_computation.71 | loop fusion | flops 8192 | bytes 65536 | tf_op jit(solution)/shard_map/neg | solution.py:23
  1.5 0.3 %multiply_exponential_fusion.2 = (f32[16,512,16]{1,2,0:T(8,128)S(1)}, f32[16,512,16]{1,2,0:T(8,128)S(1)}, f32[16,512,16]{1,2,0:T(8,128)S(1)}, f32[16,512,16]{1,2,0:T(8,128)S(1)}) fusion(f32[16]{0:T(128)S(1)} %get-tuple-element.88, f32[16,512]{1,0:T(8,128)S(1)} %bitcast_negate_fusion, f32[16]{0:T(128)S(1)} %get-tuple-element.87, f32[16]{0:T(128)S(1)} %iota_multiply_fusion.1), kind=kLoop, calls=%fused_computation.45 | loop fusion | flops 524288 | bytes 2130112 | tf_op jit(solution)/shard_map/exp | solution.py:24
  2.0 0.1 copy.20
  2.2 2.0 %multiply_reduce_fusion.1 = f32[16,512,16]{1,2,0:T(8,128)S(1)} fusion(f32[512,16,16]{0,2,1:T(8,128)S(1)} %bitcast.43, f32[16,512,16]{1,2,0:T(8,128)S(1)} %get-tuple-element.28), kind=kLoop, calls=%fused_computation.1 | loop fusion | flops 4063232 | bytes 1572864 | tf_op jit(solution)/shard_map/reduce_sum | solution.py:63
  4.2 0.2 multiply_reduce_fusion.6
  4.4 3.1 %collective-permute-start = (f32[16,512]{1,0:T(8,128)S(1)}, f32[16,512]{1,0:T(8,128)S(1)}, u32[]{:S(2)}, u32[]{:S(2)}) collective-permute-start(f32[16,512]{1,0:T(8,128)S(1)} %multiply_reduce_fusion.6), channel_id=1, source_target_pairs={{0,1},{1,0},{2,3},{3,2},{4,5},{5,4},{6,7},{7,6},{8,9},{9,8},{10,11... | collective-permute-start | bytes 98312 | tf_op jit(solution)/shard_map/ppermute | solution.py:81
  7.5 0.5 %fusion.4 = f32[16,128,256]{2,1,0:T(8,128)S(1)} fusion(f32[128,256]{1,0:T(8,128)S(1)} %get-tuple-element.32, f32[16,128]{1,0:T(8,128)S(1)} %get-tuple-element.76), kind=kOutput, calls=%fused_computation.18 | convolution fusion | flops 270073856 | bytes 2236416 | tf_op jit(solution)/shard_map/mcs,st->mct/dot_general | solution.py:15
  8.0 1.2 %multiply_reduce_fusion.5 = f32[128,256]{1,0:T(8,128)S(1)} fusion(f32[16,128,256]{2,1,0:T(8,128)S(1)} %fusion.4, f32[128,256]{1,0:T(8,128)S(1)} %get-tuple-element.32, f32[16,128]{1,0:T(8,128)S(1)} %get-tuple-element.76, f32[16,128]{1,0:T(8,128)S(1)} %get-tuple-element.72, f32[16,128]{1,0:T(8,128)S(1)} %get-tuple-element.89), kind=kOutput, calls=%fused_computation.14 | convolution fusion | flops 274235392 | bytes 2383872 | tf_op jit(solution)/shard_map/mcs,st->mct/dot_general | solution.py:16
  9.4 3.1 %collective-permute-start.1 = (f32[16,512]{1,0:T(8,128)S(1)}, f32[16,512]{1,0:T(8,128)S(1)}, u32[]{:S(2)}, u32[]{:S(2)}) collective-permute-start(f32[16,512]{1,0:T(8,128)S(1)} %get-tuple-element.35), channel_id=1, source_target_pairs={{0,2},{1,3},{2,0},{3,1},{4,6},{5,7},{6,4},{7,5},{8,10},{9,11},{10,... | collective-permute-start | bytes 98312 | tf_op jit(solution)/shard_map/ppermute | solution.py:81
  12.5 0.5 %fusion.6 = f32[16,128,256]{2,1,0:T(8,128)S(1)} fusion(f32[128,256]{1,0:T(8,128)S(1)} %get-tuple-element.37, f32[16,128]{1,0:T(8,128)S(1)} %get-tuple-element.75), kind=kOutput, calls=%fused_computation.19 | convolution fusion | flops 270073856 | bytes 2236416 | tf_op jit(solution)/shard_map/mcs,st->mct/dot_general | solution.py:15
  13.0 1.1 %multiply_reduce_fusion.4 = f32[128,256]{1,0:T(8,128)S(1)} fusion(f32[16,128,256]{2,1,0:T(8,128)S(1)} %fusion.6, f32[128,256]{1,0:T(8,128)S(1)} %get-tuple-element.37, f32[16,128]{1,0:T(8,128)S(1)} %get-tuple-element.75, f32[16,128]{1,0:T(8,128)S(1)} %get-tuple-element.73, f32[16,128]{1,0:T(8,128)S(1)} %get-tuple-element.90), kind=kOutput, calls=%fused_computation.10 | convolution fusion | flops 274235392 | bytes 2383872 | tf_op jit(solution)/shard_map/mcs,st->mct/dot_general | solution.py:16
  14.5 1.2 %collective-permute-done.2 = f32[16,512]{1,0:T(8,128)S(1)} collective-permute-done((f32[16,512]{1,0:T(8,128)S(1)}, f32[16,512]{1,0:T(8,128)S(1)}, u32[]{:S(2)}, u32[]{:S(2)}) %collective-permute-start.2) | collective-permute-done | bytes 32800 | tf_op jit(solution)/shard_map/ppermute | solution.py:81
  15.7 1.9 %collective-permute-start.3 = (f32[16,512]{1,0:T(8,128)S(1)}, f32[16,512]{1,0:T(8,128)S(1)}, u32[]{:S(2)}, u32[]{:S(2)}) collective-permute-start(f32[16,512]{1,0:T(8,128)S(1)} %multiply_add_fusion.5), channel_id=1, source_target_pairs={{0,8},{1,9},{2,10},{3,11},{4,12},{5,13},{6,14},{7,15},{8,0},{9,1},... | collective-permute-start | bytes 98312 | tf_op jit(solution)/shard_map/ppermute | solution.py:81
  17.6 0.5 %fusion.8 = f32[16,128,256]{2,1,0:T(8,128)S(1)} fusion(f32[128,256]{1,0:T(8,128)S(1)} %get-tuple-element.42, f32[16,128]{1,0:T(8,128)S(1)} %get-tuple-element.78), kind=kOutput, calls=%fused_computation.20 | convolution fusion | flops 270073856 | bytes 2236416 | tf_op jit(solution)/shard_map/mcs,st->mct/dot_general | solution.py:15
  18.1 1.2 %multiply_reduce_fusion.3 = f32[128,256]{1,0:T(8,128)S(1)} fusion(f32[16,128,256]{2,1,0:T(8,128)S(1)} %fusion.8, f32[128,256]{1,0:T(8,128)S(1)} %get-tuple-element.42, f32[16,128]{1,0:T(8,128)S(1)} %get-tuple-element.78, f32[16,128]{1,0:T(8,128)S(1)} %get-tuple-element.74, f32[16,128]{1,0:T(8,128)S(1)} %get-tuple-element.91), kind=kOutput, calls=%fused_computation.6 | convolution fusion | flops 274235392 | bytes 2383872 | tf_op jit(solution)/shard_map/mcs,st->mct/dot_general | solution.py:16
  19.4 0.3 %collective-permute-done.3 = f32[16,512]{1,0:T(8,128)S(1)} collective-permute-done((f32[16,512]{1,0:T(8,128)S(1)}, f32[16,512]{1,0:T(8,128)S(1)}, u32[]{:S(2)}, u32[]{:S(2)}) %collective-permute-start.3) | collective-permute-done | bytes 32800 | tf_op jit(solution)/shard_map/ppermute | solution.py:81
  19.7 1.9 %collective-permute-start.4 = (f32[16,512]{1,0:T(8,128)S(1)}, f32[16,512]{1,0:T(8,128)S(1)}, u32[]{:S(2)}, u32[]{:S(2)}) collective-permute-start(f32[16,512]{1,0:T(8,128)S(1)} %get-tuple-element.46), channel_id=1, source_target_pairs={{0,16},{1,17},{2,18},{3,19},{4,20},{5,21},{6,22},{7,23},{8,24},{9,... | collective-permute-start | bytes 98312 | tf_op jit(solution)/shard_map/ppermute | solution.py:81
  21.6 0.5 %fusion.10 = f32[16,128,256]{2,1,0:T(8,128)S(1)} fusion(f32[128,256]{1,0:T(8,128)S(1)} %get-tuple-element.47, f32[16,128]{1,0:T(8,128)S(1)} %get-tuple-element.77), kind=kOutput, calls=%fused_computation.21 | convolution fusion | flops 270073856 | bytes 2236416 | tf_op jit(solution)/shard_map/mcs,st->mct/dot_general | solution.py:15
  22.1 1.1 %multiply_reduce_fusion.2 = f32[128,256]{1,0:T(8,128)S(1)} fusion(f32[16,128,256]{2,1,0:T(8,128)S(1)} %fusion.10, f32[128,256]{1,0:T(8,128)S(1)} %get-tuple-element.47, f32[16,128]{1,0:T(8,128)S(1)} %get-tuple-element.77, f32[16,128]{1,0:T(8,128)S(1)} %get-tuple-element.71, f32[16,128]{1,0:T(8,128)S(1)} %get-tuple-element.92), kind=kOutput, calls=%fused_computation.2 | convolution fusion | flops 274235392 | bytes 2383872 | tf_op jit(solution)/shard_map/mcs,st->mct/dot_general | solution.py:16
  23.4 0.3 %collective-permute-done.4 = f32[16,512]{1,0:T(8,128)S(1)} collective-permute-done((f32[16,512]{1,0:T(8,128)S(1)}, f32[16,512]{1,0:T(8,128)S(1)}, u32[]{:S(2)}, u32[]{:S(2)}) %collective-permute-start.4) | collective-permute-done | bytes 32800 | tf_op jit(solution)/shard_map/ppermute | solution.py:81
  23.7 1.0 %multiply_reduce_fusion = f32[512,16,16]{0,2,1:T(8,128)S(1)} fusion(f32[16,512,16]{1,2,0:T(8,128)S(1)} %get-tuple-element.81, f32[16,512,16]{1,2,0:T(8,128)S(1)} %get-tuple-element.80, f32[16,512]{1,0:T(8,128)S(1)} %get-tuple-element.59), kind=kLoop, calls=%fused_computation | loop fusion | flops 6160384 | bytes 1605632 | tf_op jit(solution)/shard_map/reduce_sum | solution.py:104
  24.7 0.2 copy.21
  25.0 0.8 %fusion.29 = bf16[512,256]{1,0:T(8,128)(2,1)} fusion(f32[512,256]{1,0:T(8,128)S(1)} %copy.21, f32[128,256]{1,0:T(8,128)S(1)} %multiply_add_fusion, f32[128,256]{1,0:T(8,128)S(1)} %multiply_add_fusion.1, f32[128,256]{1,0:T(8,128)S(1)} %multiply_add_fusion.2, f32[128,256]{1,0:T(8,128)S(1)} %multiply_add_fusion.3, bf16[512,256]{1,0:T(8,128)(2,1)S(1)} %copy-done.3), kind=kLoop, calls=%fused_computation.40 | loop fusion | flops 917504 | bytes 1572864 | tf_op jit(solution)/shard_map/convert_element_type | solution.py:106
  25.7 0.6 %add_bitcast_fusion = f32[512,16]{0,1:T(8,128)} fusion(f32[16,512]{1,0:T(8,128)S(1)} %get-tuple-element.50, f32[16,512]{1,0:T(8,128)S(1)} %get-tuple-element.51, f32[16,512]{1,0:T(8,128)S(1)} %collective-permute-done.4), kind=kLoop, calls=%fused_computation.57 | loop fusion | flops 16384 | bytes 131072 | tf_op jit(solution)/shard_map/transpose | solution.py:101
  (31 shorter events, 0.8 us)
Async XLA Ops:
  0.6 1.2 %copy-start.1 = (bf16[512,256]{1,0:T(8,128)(2,1)S(1)}, bf16[512,256]{1,0:T(8,128)(2,1)}, u32[]{:S(2)}) copy-start(bf16[512,256]{1,0:T(8,128)(2,1)} %param.6) | copy-start | bytes 786436
  0.6 1.2 %copy-start.2 = (bf16[512,256]{1,0:T(8,128)(2,1)S(1)}, bf16[512,256]{1,0:T(8,128)(2,1)}, u32[]{:S(2)}) copy-start(bf16[512,256]{1,0:T(8,128)(2,1)} %param.7) | copy-start | bytes 786436
  1.9 5.5 %copy-start.5 = (f32[512]{0:T(512)S(1)}, f32[512]{0:T(512)}, u32[]{:S(2)}) copy-start(f32[512]{0:T(512)} %param.11) | copy-start | bytes 6148
  1.9 5.5 %copy-start = (f32[512,16]{0,1:T(8,128)S(1)}, f32[512,16]{0,1:T(8,128)}, u32[]{:S(2)}) copy-start(f32[512,16]{0,1:T(8,128)} %param.9) | copy-start | bytes 98308
  2.0 5.5 %copy-start.4 = (f32[512,16]{0,1:T(8,128)S(1)}, f32[512,16]{0,1:T(8,128)}, u32[]{:S(2)}) copy-start(f32[512,16]{0,1:T(8,128)} %param.10) | copy-start | bytes 98308
  4.4 5.0 %collective-permute-start = (f32[16,512]{1,0:T(8,128)S(1)}, f32[16,512]{1,0:T(8,128)S(1)}, u32[]{:S(2)}, u32[]{:S(2)}) collective-permute-start(f32[16,512]{1,0:T(8,128)S(1)} %multiply_reduce_fusion.6), channel_id=1, source_target_pairs={{0,1},{1,0},{2,3},{3,2},{4,5},{5,4},{6,7},{7,6},{8,9},{9,8},{10,11... | collective-permute-start | bytes 98312 | tf_op jit(solution)/shard_map/ppermute | solution.py:81
  9.4 5.0 %collective-permute-start.1 = (f32[16,512]{1,0:T(8,128)S(1)}, f32[16,512]{1,0:T(8,128)S(1)}, u32[]{:S(2)}, u32[]{:S(2)}) collective-permute-start(f32[16,512]{1,0:T(8,128)S(1)} %get-tuple-element.35), channel_id=1, source_target_pairs={{0,2},{1,3},{2,0},{3,1},{4,6},{5,7},{6,4},{7,5},{8,10},{9,11},{10,... | collective-permute-start | bytes 98312 | tf_op jit(solution)/shard_map/ppermute | solution.py:81
  14.4 1.3 %collective-permute-start.2 = (f32[16,512]{1,0:T(8,128)S(1)}, f32[16,512]{1,0:T(8,128)S(1)}, u32[]{:S(2)}, u32[]{:S(2)}) collective-permute-start(f32[16,512]{1,0:T(8,128)S(1)} %get-tuple-element.39), channel_id=1, source_target_pairs={{0,4},{1,5},{2,6},{3,7},{4,0},{5,1},{6,2},{7,3},{8,12},{9,13},{10,... | collective-permute-start | bytes 98312 | tf_op jit(solution)/shard_map/ppermute | solution.py:81
  15.7 4.0 %collective-permute-start.3 = (f32[16,512]{1,0:T(8,128)S(1)}, f32[16,512]{1,0:T(8,128)S(1)}, u32[]{:S(2)}, u32[]{:S(2)}) collective-permute-start(f32[16,512]{1,0:T(8,128)S(1)} %multiply_add_fusion.5), channel_id=1, source_target_pairs={{0,8},{1,9},{2,10},{3,11},{4,12},{5,13},{6,14},{7,15},{8,0},{9,1},... | collective-permute-start | bytes 98312 | tf_op jit(solution)/shard_map/ppermute | solution.py:81
  19.7 4.0 %collective-permute-start.4 = (f32[16,512]{1,0:T(8,128)S(1)}, f32[16,512]{1,0:T(8,128)S(1)}, u32[]{:S(2)}, u32[]{:S(2)}) collective-permute-start(f32[16,512]{1,0:T(8,128)S(1)} %get-tuple-element.46), channel_id=1, source_target_pairs={{0,16},{1,17},{2,18},{3,19},{4,20},{5,21},{6,22},{7,23},{8,24},{9,... | collective-permute-start | bytes 98312 | tf_op jit(solution)/shard_map/ppermute | solution.py:81
  23.3 1.7 %copy-start.3 = (bf16[512,256]{1,0:T(8,128)(2,1)S(1)}, bf16[512,256]{1,0:T(8,128)(2,1)}, u32[]{:S(2)}) copy-start(bf16[512,256]{1,0:T(8,128)(2,1)} %param.8) | copy-start | bytes 786436
